TPU v7x, 32 devices: a whole 2x2x4 slice. The times are simulated.
32 devices in a mesh: dp: 16 (over z, y, core), ctx: 2 (over x).
Axes of the slice: x: 2, y: 2, z: 4, core: 2. Of those that a mesh axis runs over, the one named last changes fastest.
Arguments:
- tokens: bfloat16 [16, 2, 384, 8192], P('dp', 'ctx'), may hold values from -6 to 6
- lengths: int32 [16, 2], P('dp'), may hold values from 96 to 384, as said below
- norm_gain: float32 [8192], replicated, may hold values from 0.5 to 1.5
- w_in: bfloat16 [8192, 1536], P('dp'), may hold values from -0.0625 to 0.0625
- short_filter: float32 [3, 1536], replicated, may hold values from -3.5 to 3.5
- decay_rate: float32 [16, 512], replicated, may hold values from 5e-05 to 0.03
- residue: float32 [16, 512], replicated, may hold values from -0.12 to 0.12
- skip_gain: float32 [512], replicated, may hold values from -6 to 6
- w_out: bfloat16 [512, 8192], P(None, 'dp'), may hold values from -0.25 to 0.25
- steer_table: float32 [50, 2, 8192], replicated, may hold values from -3 to 3
- steer_layer: int32 [16], P('dp'), may hold values from 0 to 49
- steer_slab: int32 [16], P('dp'), may hold values from 0 to 7
Outputs:
- result: bfloat16 [16, 2, 384, 8192], P('dp', 'ctx')
Inputs may be any that keep to these rules, and one draw needn't show every extreme that they name: `lengths`: each group holds 96 to 384 live tokens; in every sequence one group holds exactly 384.
All inputs are finite; a program needn't handle non-finite values.
Results may differ from a plain program's by a relative error of at most 0.004.
The roundings to bfloat16 on the way count: a program that leaves them out, or rounds other values in their place, can miss the bound.
Values may be sent and summed in bfloat16 or wider, within the bound.
No kernel may reach another device: no remote copies, remote signals or barrier semaphores. Data moves between devices by JAX's collectives and lax.ppermute only.
A program may use at most 192 MiB of HBM per device.

v0:
```python
import jax
import jax.numpy as jnp
from jax import lax
from jax.sharding import PartitionSpec as P

STEER_W = 1024


highest = lax.Precision.HIGHEST


def from_behind(value, axis, steps):
    count = lax.axis_size(axis)
    first, last = (max(0, -steps), min(count, count - steps))
    return lax.ppermute(value, axis, [(source, source + steps) for source in range(first, last)])


def carried_in(part, axis, combine, identity):
    place = lax.axis_index(axis)
    gathered = jax.tree.map(lambda a: lax.all_gather(a, axis), part)
    state = jax.tree.map(lambda a, e: jnp.zeros_like(a) + jnp.asarray(e, a.dtype), part, identity)

    def one(hop, state):
        return combine(
            state, jax.tree.map(lambda a: lax.dynamic_index_in_dim(a, hop, 0, False), gathered)
        )

    return lax.fori_loop(0, place, one, state)


def normalize(rows_in, gain):
    values = rows_in.astype(jnp.float32)
    scale = lax.rsqrt(jnp.mean(values * values, axis=1, keepdims=True) + 1e-06)
    return (values * scale * gain[None, :]).astype(jnp.bfloat16)


def per_device(
    tokens,
    lengths,
    norm_gain,
    w_in,
    short_filter,
    decay_rate,
    residue,
    skip_gain,
    w_out,
    steer_table,
    steer_layer,
    steer_slab,
):
    cap = tokens.shape[2]
    width = tokens.shape[3]
    slab = residue.shape[1]
    rows_in = tokens.reshape(cap, width)
    normed = normalize(rows_in, norm_gain)
    position = lax.axis_index("ctx")
    group_lens = lengths.reshape(-1)
    own_len = lax.dynamic_index_in_dim(group_lens, position, 0, keepdims=False)
    columns = normed
    proj_sum = jnp.dot(
        columns, lax.all_gather(w_in, "dp", axis=0, tiled=True), preferred_element_type=jnp.float32
    )
    proj = proj_sum.astype(jnp.bfloat16)
    own_tail = lax.dynamic_slice_in_dim(proj, own_len - 2, 2, 0)
    tail = from_behind(own_tail, "ctx", 1)
    extended = jnp.concatenate([tail, proj], axis=0).astype(jnp.float32)
    feat = (
        short_filter[0] * extended[2:]
        + short_filter[1] * extended[1:-1]
        + short_filter[2] * extended[:-2]
    )
    live = jnp.arange(cap) < own_len
    gate = feat[:, :slab]
    drive = jnp.where(live[:, None], feat[:, slab : 2 * slab] * feat[:, 2 * slab :], 0.0)
    block = min(32, cap)
    lags = jnp.arange(block)
    lags_float = lags.astype(jnp.float32)
    taps = jnp.sum(residue[None] * jnp.exp(-decay_rate[None] * lags_float[:, None, None]), axis=1)
    selector = (lags[:, None, None] - lags[None, :, None] == lags[None, None, :]).astype(
        jnp.float32
    )
    toeplitz = jnp.einsum("tsk,kc->tsc", selector, taps, precision=highest)
    lead = residue[None] * jnp.exp(-decay_rate[None] * (lags_float + 1.0)[:, None, None])
    close = jnp.exp(-decay_rate[None] * (block - 1 - lags_float)[:, None, None])
    jump = jnp.exp(-decay_rate * block)
    blocks = drive.reshape(cap // block, block, slab)

    def sweep(state, piece):
        inside = jnp.einsum("tsc,sc->tc", toeplitz, piece, precision=highest)
        earlier = jnp.einsum("tmc,mc->tc", lead, state, precision=highest)
        state = jump * state + jnp.einsum("smc,sc->mc", close, piece, precision=highest)
        return (state, inside + earlier)

    zero_state = jnp.zeros((residue.shape[0], slab), jnp.float32)
    final_state, local_parts = lax.scan(sweep, zero_state, blocks)
    filtered_local = local_parts.reshape(cap, slab)
    ending = final_state * jnp.exp(decay_rate * (cap - own_len).astype(jnp.float32))

    def combine(earlier, later):
        return (earlier[0] * jnp.exp(-decay_rate * later[1]) + later[0], earlier[1] + later[1])

    incoming, _ = carried_in(
        (ending, own_len.astype(jnp.float32)), "ctx", combine, (zero_state, jnp.float32(0.0))
    )
    after = jnp.arange(cap).astype(jnp.float32) + 1.0
    reach = residue[None] * jnp.exp(-decay_rate[None] * after[:, None, None])
    crossing = jnp.einsum("tmc,mc->tc", reach, incoming, precision=highest)
    filtered = filtered_local + crossing + skip_gain[None, :] * drive
    gated = jnp.where(live[:, None], gate * filtered, 0.0).astype(jnp.bfloat16)
    mixed = jnp.dot(
        gated, lax.all_gather(w_out, "dp", axis=1, tiled=True), preferred_element_type=jnp.float32
    )
    rows2 = lax.dynamic_index_in_dim(steer_table, steer_layer[0], 0, keepdims=False)
    shift_vec = rows2[0] - rows2[1]
    columns = jnp.arange(width) // STEER_W
    steer = jnp.where(columns == steer_slab[0], 2.0 * shift_vec, 0.0)
    summed = rows_in.astype(jnp.float32) + mixed + steer[None, :]
    summed = jnp.where(live[:, None], summed, 0.0)
    return summed.astype(jnp.bfloat16).reshape(tokens.shape)


def solution(mesh):
    placed = (
        P("dp", "ctx", None, None),
        P("dp", None),
        P(),
        P("dp", None),
        P(),
        P(),
        P(),
        P(),
        P(None, "dp"),
        P(),
        P("dp"),
        P("dp"),
    )
    return jax.shard_map(
        per_device,
        mesh=mesh,
        in_specs=placed,
        out_specs=P("dp", "ctx", None, None),
        check_vma=False,
    )
```

profile of v0, /device:TPU:0, one launch (start us, length us, event | category | flops | bytes accessed | tf_op | source)
XLA Modules:
  0.0 239.4 jit_solution(5505199059988020900)
XLA Ops:
  6.6 0.7 all-gather.4.cloned.1.call-update
  7.3 0.7 all-gather.6.cloned.1.call-update
  8.1 4.1 %fusion.4 = f32[384]{0:T(512)S(1)} fusion(bf16[1,1,384,8192]{3,2,1,0:T(8,128)(2,1)} %param.16), kind=kLoop, calls=%fused_computation.13 | loop fusion | flops 9436800 | bytes 6292992 | tf_op jit(solution)/shard_map/reduce_sum | solution.py:33
  16.2 0.7 dynamic-slice.1
  17.2 1.0 fusion.25
  18.2 1.0 fusion.31
  19.2 0.8 dynamic-update-slice
  20.0 120.3 %all-gather.4.cloned.1.call-done = bf16[8192,1536]{1,0:T(8,128)(2,1)} async-done(((bf16[512,1536]{1,0:T(8,128)(2,1)}), bf16[8192,1536]{1,0:T(8,128)(2,1)}) %all-gather.4.cloned.1.call-update) | async-done | bytes 25165840 | tf_op jit(solution)/shard_map/all_gather | solution.py:61
  140.3 16.7 %fusion.16 = bf16[384,1536]{1,0:T(8,128)(2,1)S(1)} fusion(bf16[8192,1536]{1,0:T(8,128)(2,1)} %all-gather.4.cloned.1.call-done, bf16[1,1,384,8192]{3,2,1,0:T(8,128)(2,1)} %param.16, f32[8192]{0:T(1024)S(1)} %copy-done.7, f32[384]{0:T(512)S(1)} %add_rsqrt_fusion), kind=kOutput, calls=%fused_computation.25 | convolution fusion | flops 9676849152 | bytes 32671232 | tf_op jit(solution)/shard_map/dot_general | solution.py:60
  157.0 3.4 %collective-permute-start = (bf16[2,1536]{1,0:T(2,128)(2,1)S(1)}, bf16[2,1536]{1,0:T(2,128)(2,1)S(1)}, u32[]{:S(2)}, u32[]{:S(2)}) collective-permute-start(bf16[2,1536]{1,0:T(2,128)(2,1)S(1)} %constant_dynamic-slice_fusion), channel_id=1, source_target_pairs={{0,1},{2,3},{4,5},{6,7},{8,9},{10,11},{12,13},{14,15},{16,17},{18,... | collective-permute-start | bytes 18440 | tf_op jit(solution)/shard_map/ppermute | solution.py:15
  160.4 0.7 iota_compare_fusion.2
  161.1 4.9 %all-reduce = f32[2]{0:T(128)S(1)} all-reduce(f32[2]{0:T(128)S(1)} %dynamic-update-slice), channel_id=1, replica_groups=mesh['dp'=16,'ctx'=2] {'ctx'}, use_global_device_ids=true, to_apply=%add | all-reduce | flops 2 | bytes 16
  167.0 0.7 fusion.19
  167.7 1.4 copy-done.1
  169.3 20.0 %while.30 = (s32[]{:T(128)}, f32[16,512]{1,0:T(8,128)S(1)}, f32[12,32,512]{2,1,0:T(8,128)}, f32[16,512]{1,0:T(8,128)S(1)}, f32[12,32,512]{2,1,0:T(8,128)S(1)}, /...) while((s32[]{:T(128)}, f32[16,512]{1,0:T(8,128)S(1)}, ...), condition=%wide.region_3.4_spmd.clone.clone.clone, body=%wide.region_2.3_spmd.clone.clone.clone.sunk | while | flops 2883587 | bytes 3015055 | solution.py:95
  170.3 0.6 bitcast_dynamic-update-slice_fusion.2
  178.7 0.6 bitcast_dynamic-update-slice_fusion.2
  180.3 0.6 bitcast_dynamic-update-slice_fusion.2
  183.7 0.6 bitcast_dynamic-update-slice_fusion.2
  189.3 4.7 %all-gather = f32[32,512]{1,0:T(8,128)S(1)} all-gather(f32[16,512]{1,0:T(8,128)S(1)} %exponential_multiply_fusion), channel_id=2, replica_groups=mesh['dp'=16,'ctx'=2] {'ctx'}, dimensions={0}, use_global_device_ids=true | all-gather | bytes 98304 | tf_op jit(solution)/shard_map/all_gather | solution.py:20
  194.1 4.0 %multiply_reduce_fusion.3 = f32[512,384]{0,1:T(8,128)S(1)} fusion(f32[512,16]{0,1:T(8,128)S(1)} %bitcast.81, f32[384]{0:T(512)S(1)} %convert_add_fusion.1, f32[16,512]{1,0:T(8,128)S(1)} %get-tuple-element.452, f32[16,512]{1,0:T(8,128)S(1)} %get-tuple-element.459), kind=kLoop, calls=%fused_computation.19 | loop fusion | flops 12386304 | bytes 886272 | tf_op jit(solution)/shard_map/tmc,mc->tc/dot_general | solution.py:107
  198.2 1.0 fusion.23
  199.2 21.4 %all-gather.6.cloned.1.call-done = bf16[512,8192]{1,0:T(8,128)(2,1)} async-done(((bf16[512,512]{1,0:T(8,128)(2,1)}), bf16[512,8192]{1,0:T(8,128)(2,1)}) %all-gather.6.cloned.1.call-update) | async-done | bytes 8388624 | tf_op jit(solution)/shard_map/all_gather | solution.py:111
  220.6 12.0 %fusion.10 = bf16[1,1,384,8192]{3,2,1,0:T(8,128)(2,1)} fusion(bf16[384,512]{1,0:T(8,128)(2,1)} %fusion.23, bf16[512,8192]{1,0:T(8,128)(2,1)} %all-gather.6.cloned.1.call-done, bf16[1,1,384,8192]{3,2,1,0:T(8,128)(2,1)} %param.16, f32[8192]{0:T(1024)S(1)} %fusion.33, pred[384]{0:T(512)(128)(4,1)S(1)} %iota_compare_fusion.2), kind=kOutput, calls=%fused_computation.20 | convolution fusion | flops 3236954112 | bytes 21397888 | tf_op jit(solution)/shard_map/dot_general | solution.py:110
  (111 shorter events, 18.9 us)
Async XLA Ops:
  6.5 5.7 %copy-start = (s32[1,2]{1,0:T(1,128)S(1)}, s32[1,2]{1,0:T(1,128)}, u32[]{:S(2)}) copy-start(s32[1,2]{1,0:T(1,128)} %param.17) | copy-start | bytes 28
  6.5 9.6 %copy-start.10 = (u32[32]{0:T(128)S(1)}, u32[32]{0:T(128)}, u32[]{:S(2)}) copy-start(u32[32]{0:T(128)} %constant.96) | copy-start | bytes 388
  6.5 8.2 %copy-start.5 = (f32[3,1536]{1,0:T(4,128)S(1)}, f32[3,1536]{1,0:T(4,128)}, u32[]{:S(2)}) copy-start(f32[3,1536]{1,0:T(4,128)} %param.20) | copy-start | bytes 55300
  6.5 8.3 %copy-start.4 = (f32[16,512]{1,0:T(8,128)S(1)}, f32[16,512]{1,0:T(8,128)}, u32[]{:S(2)}) copy-start(f32[16,512]{1,0:T(8,128)} %param.21) | copy-start | bytes 98308
  6.5 10.3 %copy-start.8 = (f32[16,512]{1,0:T(8,128)S(1)}, f32[16,512]{1,0:T(8,128)}, u32[]{:S(2)}) copy-start(f32[16,512]{1,0:T(8,128)} %param.22) | copy-start | bytes 98308
  6.6 133.8 %copy-start.7 = (f32[8192]{0:T(1024)S(1)}, f32[8192]{0:T(1024)}, u32[]{:S(2)}) copy-start(f32[8192]{0:T(1024)} %param.18) | copy-start | bytes 98308
  6.6 133.8 %all-gather.4.cloned.1.call-start = ((), (), s32[]{:S(2)}) async-start(), calls=%async_computation | async-start | bytes 26738688 | tf_op jit(solution)/shard_map/all_gather | solution.py:61
  7.3 213.3 %all-gather.6.cloned.1.call-start = ((), (), s32[]{:S(2)}) async-start(), calls=%async_computation.1 | async-start | bytes 8912896 | tf_op jit(solution)/shard_map/all_gather | solution.py:111
  157.0 9.6 %collective-permute-start = (bf16[2,1536]{1,0:T(2,128)(2,1)S(1)}, bf16[2,1536]{1,0:T(2,128)(2,1)S(1)}, u32[]{:S(2)}, u32[]{:S(2)}) collective-permute-start(bf16[2,1536]{1,0:T(2,128)(2,1)S(1)} %constant_dynamic-slice_fusion), channel_id=1, source_target_pairs={{0,1},{2,3},{4,5},{6,7},{8,9},{10,11},{12,13},{14,15},{16,17},{18,... | collective-permute-start | bytes 18440 | tf_op jit(solution)/shard_map/ppermute | solution.py:15
  167.0 2.3 copy-start.9
  167.7 1.4 copy-start.1
  189.3 8.8 %copy-start.2 = (f32[384,1536]{1,0:T(8,128)S(1)}, f32[384,1536]{1,0:T(8,128)}, u32[]{:S(2)}) copy-start(f32[384,1536]{1,0:T(8,128)} %copy-done.1) | copy-start | bytes 7077892
  189.3 8.8 %copy-start.3 = (f32[12,32,512]{2,1,0:T(8,128)S(1)}, f32[12,32,512]{2,1,0:T(8,128)}, u32[]{:S(2)}) copy-start(f32[12,32,512]{2,1,0:T(8,128)} %get-tuple-element.141) | copy-start | bytes 2359300
  189.3 8.9 %copy-start.6 = (f32[512]{0:T(512)S(1)}, f32[512]{0:T(512)}, u32[]{:S(2)}) copy-start(f32[512]{0:T(512)} %param.23) | copy-start | bytes 6148
Sparse Core Ops, SparseCore 0:
  9.0 131.2 all-gather.3
  142.5 78.1 all-gather.5
where the time goes:
time: 240 us; the launch traced here: 239 us
  waiting for transfers between devices  143 us (60%)
  other arithmetic  32 us (13%)
  matrix products  29.7 us (12%)
  between operations  17.6 us (7%)
  blocking collectives  9.67 us (4%)
  local copies, waits for them, and re-layouts  3.64 us (2%)
  starting transfers between devices  3.45 us (1%)
    all_gather x1, waiting for transfers between devices, per_device(): lax.all_gather(w_in, 'dp', axis=0, tiled=True)  120 us
    all_gather x1, waiting for transfers between devices, per_device(): lax.all_gather(w_out, 'dp', axis=1, tiled=True)  21.4 us
    dot_general x1, matrix products, per_device(): jnp.dot(columns, lax.all_gather(w_in, 'dp', axis=0, tiled=True), preferre...  16.7 us
    dot_general x1, matrix products, per_device(): jnp.dot(gated, lax.all_gather(w_out, 'dp', axis=1, tiled=True), preferred...  12 us
    dynamic_update_slice x12, other arithmetic, per_device(): final_state, local_parts = lax.scan(sweep, zero_state, blocks)  7.63 us
    unnamed x1, blocking collectives  4.94 us
  transfers between devices with their start and end apart: 3, of which 2 were waited for; matrix products, arithmetic and copies ran while one was open for 22% of the time, Pallas kernels for 0%

commit v1 on v0

v1 whole, which is shorter than its diff:
```python
import jax
import jax.numpy as jnp
from jax import lax
from jax.sharding import PartitionSpec as P

STEER_W = 1024
CHUNKS = 4
BLOCK = 32


def from_behind(value, axis, steps):
    count = lax.axis_size(axis)
    first, last = (max(0, -steps), min(count, count - steps))
    return lax.ppermute(value, axis, [(source, source + steps) for source in range(first, last)])


def normalize(rows_in, gain):
    values = rows_in.astype(jnp.float32)
    scale = lax.rsqrt(jnp.mean(values * values, axis=1, keepdims=True) + 1e-06)
    return (values * scale * gain[None, :]).astype(jnp.bfloat16)


def filter_tables(decay_rate, residue, block):
    lags = jnp.arange(block)
    lags_float = lags.astype(jnp.float32)
    taps = jnp.sum(residue[None] * jnp.exp(-decay_rate[None] * lags_float[:, None, None]), axis=1)
    diff = lags[:, None] - lags[None, :]
    toeplitz = jnp.where((diff >= 0)[:, :, None], taps[jnp.clip(diff, 0, block - 1)], 0.0)
    lead = residue[None] * jnp.exp(-decay_rate[None] * (lags_float + 1.0)[:, None, None])
    close = jnp.exp(-decay_rate[None] * (block - 1 - lags_float)[:, None, None])
    return toeplitz, lead, close


def local_filter(drive, decay_rate, toeplitz, lead, close, block):
    cap, width = drive.shape
    count = cap // block
    pieces = drive.reshape(count, block, width)
    inside = jnp.sum(toeplitz[None] * pieces[:, None, :, :], axis=2)
    ends = jnp.sum(close[None] * pieces[:, :, None, :], axis=1)
    steps = jnp.arange(count)
    gap = (steps[:, None] - steps[None, :]).astype(jnp.float32)
    powers = jnp.where(
        (gap >= 0)[:, :, None, None],
        jnp.exp(-decay_rate[None, None] * (block * jnp.maximum(gap, 0.0))[:, :, None, None]),
        0.0,
    )
    states = jnp.sum(powers * ends[None], axis=1)
    before = jnp.concatenate([jnp.zeros_like(states[:1]), states[:-1]], axis=0)
    earlier = jnp.sum(lead[None] * before[:, None, :, :], axis=2)
    return (inside + earlier).reshape(cap, width), states[-1]


def per_device(
    tokens,
    lengths,
    norm_gain,
    w_in,
    short_filter,
    decay_rate,
    residue,
    skip_gain,
    w_out,
    steer_table,
    steer_layer,
    steer_slab,
):
    cap = tokens.shape[2]
    width = tokens.shape[3]
    slab = residue.shape[1]
    groups = lax.axis_size("ctx")
    rows_in = tokens.reshape(cap, width)
    normed = normalize(rows_in, norm_gain)
    position = lax.axis_index("ctx")
    group_lens = lengths.reshape(-1)
    own_len = lax.dynamic_index_in_dim(group_lens, position, 0, keepdims=False)
    live = jnp.arange(cap) < own_len
    own_tail = lax.dynamic_slice_in_dim(normed, own_len - 2, 2, 0)
    tail_normed = from_behind(own_tail, "ctx", 1)

    block = BLOCK if cap % BLOCK == 0 else cap
    toeplitz, lead, close = filter_tables(decay_rate, residue, block)

    lens_f = group_lens.astype(jnp.float32)
    cumlen = jnp.cumsum(lens_f)
    after = jnp.arange(cap).astype(jnp.float32) + 1.0
    rescale = jnp.exp(decay_rate * (cap - own_len).astype(jnp.float32))

    n = slab // CHUNKS
    mixed = None
    for j in range(CHUNKS):
        cols = slice(j * n, (j + 1) * n)
        piece = jnp.concatenate(
            [
                w_in[:, j * n : (j + 1) * n],
                w_in[:, slab + j * n : slab + (j + 1) * n],
                w_in[:, 2 * slab + j * n : 2 * slab + (j + 1) * n],
                w_out[j * n : (j + 1) * n, :].T,
            ],
            axis=1,
        )
        gathered = lax.all_gather(piece, "dp", axis=0, tiled=True)
        w_in_j = gathered[:, : 3 * n]
        w_out_t = gathered[:, 3 * n :]
        proj = jnp.dot(normed, w_in_j, preferred_element_type=jnp.float32).astype(jnp.bfloat16)
        tail = jnp.dot(tail_normed, w_in_j, preferred_element_type=jnp.float32).astype(jnp.bfloat16)
        extended = jnp.concatenate([tail, proj], axis=0).astype(jnp.float32)
        sf = jnp.concatenate(
            [
                short_filter[:, j * n : (j + 1) * n],
                short_filter[:, slab + j * n : slab + (j + 1) * n],
                short_filter[:, 2 * slab + j * n : 2 * slab + (j + 1) * n],
            ],
            axis=1,
        )
        feat = sf[0] * extended[2:] + sf[1] * extended[1:-1] + sf[2] * extended[:-2]
        gate = feat[:, :n]
        drive = jnp.where(live[:, None], feat[:, n : 2 * n] * feat[:, 2 * n :], 0.0)
        rate = decay_rate[:, cols]
        local, final_state = local_filter(
            drive, rate, toeplitz[:, :, cols], lead[:, :, cols], close[:, :, cols], block
        )
        ending = final_state * rescale[:, cols]
        incoming = jnp.zeros_like(ending)
        for k in range(1, groups):
            got = from_behind(ending, "ctx", k)
            source = position - k
            between = (
                lax.dynamic_index_in_dim(cumlen, jnp.maximum(position - 1, 0), 0, keepdims=False)
                - lax.dynamic_index_in_dim(cumlen, jnp.maximum(source, 0), 0, keepdims=False)
            )
            weight = jnp.where(source >= 0, jnp.exp(-rate * between), 0.0)
            incoming = incoming + weight * got
        reach = residue[None, :, cols] * jnp.exp(-rate[None] * after[:, None, None])
        crossing = jnp.sum(reach * incoming[None], axis=1)
        filtered = local + crossing + skip_gain[None, cols] * drive
        gated = jnp.where(live[:, None], gate * filtered, 0.0).astype(jnp.bfloat16)
        part = lax.dot_general(
            gated, w_out_t, (((1,), (1,)), ((), ())), preferred_element_type=jnp.float32
        )
        mixed = part if mixed is None else mixed + part
    rows2 = lax.dynamic_index_in_dim(steer_table, steer_layer[0], 0, keepdims=False)
    shift_vec = rows2[0] - rows2[1]
    columns = jnp.arange(width) // STEER_W
    steer = jnp.where(columns == steer_slab[0], 2.0 * shift_vec, 0.0)
    summed = rows_in.astype(jnp.float32) + mixed + steer[None, :]
    summed = jnp.where(live[:, None], summed, 0.0)
    return summed.astype(jnp.bfloat16).reshape(tokens.shape)


def solution(mesh):
    placed = (
        P("dp", "ctx", None, None),
        P("dp", None),
        P(),
        P("dp", None),
        P(),
        P(),
        P(),
        P(),
        P(None, "dp"),
        P(),
        P("dp"),
        P("dp"),
    )
    return jax.shard_map(
        per_device,
        mesh=mesh,
        in_specs=placed,
        out_specs=P("dp", "ctx", None, None),
        check_vma=False,
    )
```

time: 240 us -> 416 us (1.73); the launches traced: 239 us -> 411 us
  waiting for transfers between devices: 143 us -> 237 us
  matrix products: 29.7 us -> 90.1 us
  local copies, waits for them, and re-layouts: 3.64 us -> 15.9 us
  blocking collectives: 9.67 us -> 0 us
  starting transfers between devices: 3.45 us -> 12.1 us
  other arithmetic: 32 us -> 37.7 us
    all_gather x2 -> x4, waiting for transfers between devices: 142 us -> 237 us  [per_device(): gathered = lax.all_gather(piece, 'dp', axis=0, tiled=True)]
    dot_general x3 -> x12, matrix products: 29.7 us -> 90.1 us  [the longest x4 41.2 us: per_device(): lax.dot_general(gated, w_out_t, (((1,), (1,)), ((), ())), preferred_eleme...]
    dot_general x37 -> x0, other arithmetic: 15.9 us -> none  [the longest x12 4.63 us: sweep(): earlier = jnp.einsum('tmc,mc->tc', lead, state, precision=highest)]
    reduce_sum x1 -> x14, other arithmetic: 0.35 us -> 15.4 us  [the longest x4 5.48 us: local_filter(): inside = jnp.sum(toeplitz[None] * pieces[:, None, :, :], axis=2)]
    ppermute x1 -> x5, starting transfers between devices: 3.38 us -> 11.9 us  [from_behind(): lax.ppermute(value, axis, [(source, source + steps) for source in range(f...]
    dynamic_update_slice x12 -> x0, other arithmetic: 7.63 us -> none  [per_device(): final_state, local_parts = lax.scan(sweep, zero_state, blocks)]
    slice x1 -> x10, local copies, waits for them, and re-layouts: 0.05 us -> 5.57 us  [the longest x1 1.6 us: per_device(): w_in[:, j * n:(j + 1) * n]]
    convert_element_type x1 -> x3, other arithmetic: 0.01 us -> 5.06 us  [the longest x1 5.05 us: normalize(): return (values * scale * gain[None, :]).astype(jnp.bfloat16)]
  transfers between devices with their start and end apart: 3 -> 9, of which waited for: 2 -> 4; matrix products, arithmetic and copies ran while one was open for 22% -> 19% of each run, Pallas kernels for 0% -> 0%
where the time goes in v1:
time: 416 us; the launch traced here: 411 us
  waiting for transfers between devices  237 us (57%)
  matrix products  90.1 us (22%)
  other arithmetic  37.7 us (9%)
  between operations  17.8 us (4%)
  local copies, waits for them, and re-layouts  15.9 us (4%)
  starting transfers between devices  12.1 us (3%)
    all_gather x4, waiting for transfers between devices, per_device(): gathered = lax.all_gather(piece, 'dp', axis=0, tiled=True)  237 us
    dot_general x4, matrix products, per_device(): lax.dot_general(gated, w_out_t, (((1,), (1,)), ((), ())), preferred_eleme...  41.2 us
    dot_general x4, matrix products, per_device(): jnp.dot(normed, w_in_j, preferred_element_type=jnp.float32)  33.7 us
    dot_general x4, matrix products, per_device(): jnp.dot(tail_normed, w_in_j, preferred_element_type=jnp.float32)  15.2 us
    ppermute x5, starting transfers between devices, from_behind(): lax.ppermute(value, axis, [(source, source + steps) for source in range(f...  11.9 us
  transfers between devices with their start and end apart: 9, of which 4 were waited for; matrix products, arithmetic and copies ran while one was open for 19% of the time, Pallas kernels for 0%

profile of v1, /device:TPU:0, one launch (start us, length us, event | category | flops | bytes accessed | tf_op | source)
XLA Modules:
  0.0 410.5 jit_solution(14627375695638624543)
XLA Ops:
  16.2 4.1 fusion
  20.4 5.1 %fusion.2 = bf16[384,8192]{1,0:T(8,128)(2,1)S(1)} fusion(bf16[1,1,384,8192]{3,2,1,0:T(8,128)(2,1)} %param.12, f32[8192]{0:T(1024)S(1)} %copy-done.17, f32[384]{0:T(512)S(1)} %add_rsqrt_fusion), kind=kLoop, calls=%fused_computation.6 | loop fusion | flops 12582912 | bytes 12617216 | tf_op jit(solution)/shard_map/convert_element_type | solution.py:20
  25.4 2.7 copy-done.1
  28.8 4.7 %collective-permute-start = (bf16[2,8192]{1,0:T(2,128)(2,1)}, bf16[2,8192]{1,0:T(2,128)(2,1)S(1)}, u32[]{:S(2)}, u32[]{:S(2)}) collective-permute-start(bf16[2,8192]{1,0:T(2,128)(2,1)} %constant_dynamic-slice_fusion.1), channel_id=1, source_target_pairs={{0,1},{2,3},{4,5},{6,7},{8,9},{10,11},{12,13},{14,15},{16,17},{18,... | collective-permute-start | bytes 98312 | tf_op jit(solution)/shard_map/ppermute | solution.py:14
  36.1 1.7 exponential_multiply_fusion
  37.8 3.7 gather_fusion
  50.7 40.7 %all-gather.11.cloned.1.call-done = bf16[8192,512]{0,1:T(8,128)(2,1)} async-done(((bf16[512,512]{0,1:T(8,128)(2,1)}), bf16[8192,512]{0,1:T(8,128)(2,1)}) %all-gather.11.cloned.1.call-update) | async-done | bytes 8388624 | tf_op jit(solution)/shard_map/all_gather | solution.py:101
  91.4 4.5 %fusion.51 = bf16[2,384]{1,0:T(2,128)(2,1)S(1)} fusion(bf16[2,8192]{1,0:T(2,128)(2,1)S(1)} %collective-permute-done, bf16[8192,512]{0,1:T(8,128)(2,1)} %all-gather.11.cloned.1.call-done), kind=kOutput, calls=%fused_computation.61 | convolution fusion | flops 12583680 | bytes 6325760 | tf_op jit(solution)/shard_map/dot_general | solution.py:105
  96.0 8.4 %fusion.39 = bf16[384,384]{1,0:T(8,128)(2,1)S(1)} fusion(bf16[384,8192]{1,0:T(8,128)(2,1)} %copy-done.1, bf16[8192,512]{0,1:T(8,128)(2,1)} %all-gather.11.cloned.1.call-done), kind=kOutput, calls=%fused_computation.53 | convolution fusion | flops 2416066560 | bytes 12877824 | tf_op jit(solution)/shard_map/dot_general | solution.py:104
  104.4 65.4 %all-gather.5.cloned.1.call-done = bf16[8192,512]{0,1:T(8,128)(2,1)} async-done(((bf16[512,512]{0,1:T(8,128)(2,1)}), bf16[8192,512]{0,1:T(8,128)(2,1)}) %all-gather.5.cloned.1.call-update) | async-done | bytes 8388624 | tf_op jit(solution)/shard_map/all_gather | solution.py:101
  169.9 4.5 %fusion.42 = bf16[2,384]{1,0:T(2,128)(2,1)S(1)} fusion(bf16[2,8192]{1,0:T(2,128)(2,1)S(1)} %collective-permute-done, bf16[8192,512]{0,1:T(8,128)(2,1)} %all-gather.5.cloned.1.call-done), kind=kOutput, calls=%fused_computation.58 | convolution fusion | flops 12583680 | bytes 6325760 | tf_op jit(solution)/shard_map/dot_general | solution.py:105
  174.4 8.4 %fusion.30 = bf16[384,384]{1,0:T(8,128)(2,1)S(1)} fusion(bf16[384,8192]{1,0:T(8,128)(2,1)} %copy-done.1, bf16[8192,512]{0,1:T(8,128)(2,1)} %all-gather.5.cloned.1.call-done), kind=kOutput, calls=%fused_computation.50 | convolution fusion | flops 2416066560 | bytes 12877824 | tf_op jit(solution)/shard_map/dot_general | solution.py:104
  182.9 65.5 %all-gather.9.cloned.1.call-done = bf16[8192,512]{0,1:T(8,128)(2,1)} async-done(((bf16[512,512]{0,1:T(8,128)(2,1)}), bf16[8192,512]{0,1:T(8,128)(2,1)}) %all-gather.9.cloned.1.call-update) | async-done | bytes 8388624 | tf_op jit(solution)/shard_map/all_gather | solution.py:101
  248.3 4.5 %fusion.48 = bf16[2,384]{1,0:T(2,128)(2,1)S(1)} fusion(bf16[2,8192]{1,0:T(2,128)(2,1)S(1)} %collective-permute-done, bf16[8192,512]{0,1:T(8,128)(2,1)} %all-gather.9.cloned.1.call-done), kind=kOutput, calls=%fused_computation.60 | convolution fusion | flops 12583680 | bytes 6325760 | tf_op jit(solution)/shard_map/dot_general | solution.py:105
  252.9 8.4 %fusion.36 = bf16[384,384]{1,0:T(8,128)(2,1)S(1)} fusion(bf16[384,8192]{1,0:T(8,128)(2,1)} %copy-done.1, bf16[8192,512]{0,1:T(8,128)(2,1)} %all-gather.9.cloned.1.call-done), kind=kOutput, calls=%fused_computation.52 | convolution fusion | flops 2416066560 | bytes 12877824 | tf_op jit(solution)/shard_map/dot_general | solution.py:104
  261.4 65.3 %all-gather.7.cloned.1.call-done = bf16[8192,512]{0,1:T(8,128)(2,1)} async-done(((bf16[512,512]{0,1:T(8,128)(2,1)}), bf16[8192,512]{0,1:T(8,128)(2,1)}) %all-gather.7.cloned.1.call-update) | async-done | bytes 8388624 | tf_op jit(solution)/shard_map/all_gather | solution.py:101
  326.7 8.4 %fusion.33 = bf16[384,384]{1,0:T(8,128)(2,1)S(1)} fusion(bf16[384,8192]{1,0:T(8,128)(2,1)} %copy-done.1, bf16[8192,512]{0,1:T(8,128)(2,1)} %all-gather.7.cloned.1.call-done), kind=kOutput, calls=%fused_computation.51 | convolution fusion | flops 2416066560 | bytes 12877824 | tf_op jit(solution)/shard_map/dot_general | solution.py:104
  335.1 1.7 fusion.45
  340.3 3.4 collective-permute-start.1
  357.7 4.3 %multiply_reduce_fusion.10 = (f32[384,128]{1,0:T(8,128)S(1)}, f32[384,128]{1,0:T(8,128)S(1)}, f32[384,128]{1,0:T(8,128)S(1)}, f32[384,128]{1,0:T(8,128)S(1)}) fusion(f32[16,128]{1,0:T(8,128)S(1)} %get-tuple-element.61, f32[16,128]{1,0:T(8,128)S(1)} %copy-done.19, f32[16,128]{1,0:T(8,128)S(1)} %copy-done.23, f32[384]{0:T(512)S(1)} %copy-done.33, ...), kind=kLoop, calls=%fused_computation.37 | loop fusion | flops 12386304 | bytes 886272 | tf_op jit(solution)/shard_map/reduce_sum | solution.py:134
  362.3 7.9 %fusion.24 = f32[384,8192]{1,0:T(8,128)} fusion(bf16[384,128]{1,0:T(8,128)(2,1)S(1)} %get-tuple-element.92, bf16[8192,512]{0,1:T(8,128)(2,1)} %all-gather.9.cloned.1.call-done), kind=kOutput, calls=%fused_computation.44 | convolution fusion | flops 805306368 | bytes 14778368 | tf_op jit(solution)/shard_map/dot_general | solution.py:137
  370.3 7.8 %fusion.28 = f32[384,8192]{1,0:T(8,128)} fusion(bf16[384,128]{1,0:T(8,128)(2,1)S(1)} %get-tuple-element.91, bf16[8192,512]{0,1:T(8,128)(2,1)} %all-gather.5.cloned.1.call-done), kind=kOutput, calls=%fused_computation.48 | convolution fusion | flops 805306368 | bytes 14778368 | tf_op jit(solution)/shard_map/dot_general | solution.py:137
  378.1 6.4 %fusion.26 = f32[384,8192]{1,0:T(8,128)} fusion(bf16[384,128]{1,0:T(8,128)(2,1)S(1)} %get-tuple-element.90, bf16[8192,512]{0,1:T(8,128)(2,1)S(1)} %copy-done), kind=kOutput, calls=%fused_computation.46 | convolution fusion | flops 805306368 | bytes 14778368 | tf_op jit(solution)/shard_map/dot_general | solution.py:137
  384.5 19.0 %fusion.6 = bf16[1,1,384,8192]{3,2,1,0:T(8,128)(2,1)} fusion(bf16[384,128]{1,0:T(8,128)(2,1)S(1)} %fusion.64, f32[384,8192]{1,0:T(8,128)} %fusion.24, f32[384,8192]{1,0:T(8,128)} %fusion.28, f32[384,8192]{1,0:T(8,128)} %fusion.26, bf16[1,1,384,8192]{3,2,1,0:T(8,128)(2,1)} %param.12, f32[8192]{0:T(1024)S(1)} %copy-done.16, pred[384]{0:T(512)(128)(4,1)S(1)} %copy-done.27, ...), kind=kOutput, calls=%fused_computation.10 | convolution fusion | flops 830472192 | bytes 52560256 | tf_op jit(solution)/shard_map/dot_general | solution.py:137
  (173 shorter events, 36.2 us)
Async XLA Ops:
  6.5 84.9 %all-gather.11.cloned.1.call-start = ((), (), s32[]{:S(2)}) async-start(), calls=%async_computation.3 | async-start | bytes 8912896 | tf_op jit(solution)/shard_map/all_gather | solution.py:101
  10.5 159.4 %all-gather.5.cloned.1.call-start = ((), (), s32[]{:S(2)}) async-start(), calls=%async_computation | async-start | bytes 8912896 | tf_op jit(solution)/shard_map/all_gather | solution.py:101
  11.8 236.6 %all-gather.9.cloned.1.call-start = ((), (), s32[]{:S(2)}) async-start(), calls=%async_computation.2 | async-start | bytes 8912896 | tf_op jit(solution)/shard_map/all_gather | solution.py:101
  13.1 313.6 %all-gather.7.cloned.1.call-start = ((), (), s32[]{:S(2)}) async-start(), calls=%async_computation.1 | async-start | bytes 8912896 | tf_op jit(solution)/shard_map/all_gather | solution.py:101
  20.3 15.2 %copy-start.13 = (f32[16,512]{1,0:T(8,128)S(1)}, f32[16,512]{1,0:T(8,128)}, u32[]{:S(2)}) copy-start(f32[16,512]{1,0:T(8,128)} %param.17) | copy-start | bytes 98308
  20.3 15.8 %copy-start.14 = (f32[16,512]{1,0:T(8,128)S(1)}, f32[16,512]{1,0:T(8,128)}, u32[]{:S(2)}) copy-start(f32[16,512]{1,0:T(8,128)} %param.18) | copy-start | bytes 98308
  28.8 22.0 %collective-permute-start = (bf16[2,8192]{1,0:T(2,128)(2,1)}, bf16[2,8192]{1,0:T(2,128)(2,1)S(1)}, u32[]{:S(2)}, u32[]{:S(2)}) collective-permute-start(bf16[2,8192]{1,0:T(2,128)(2,1)} %constant_dynamic-slice_fusion.1), channel_id=1, source_target_pairs={{0,1},{2,3},{4,5},{6,7},{8,9},{10,11},{12,13},{14,15},{16,17},{18,... | collective-permute-start | bytes 98312 | tf_op jit(solution)/shard_map/ppermute | solution.py:14
  49.8 288.0 %copy-start.26 = (pred[384]{0:T(512)(128)(4,1)}, pred[384]{0:T(512)(128)(4,1)S(1)}, u32[]{:S(2)}) copy-start(pred[384]{0:T(512)(128)(4,1)S(1)} %iota_compare_fusion) | copy-start | bytes 1156
  337.3 11.7 %copy-start.5 = (f32[32,32,128]{2,1,0:T(8,128)S(1)}, f32[32,32,128]{2,1,0:T(8,128)}, u32[]{:S(2)}) copy-start(f32[32,32,128]{2,1,0:T(8,128)} %get-tuple-element.25) | copy-start | bytes 1572868
  337.3 13.1 %copy-start.4 = (f32[32,32,128]{2,1,0:T(8,128)S(1)}, f32[32,32,128]{2,1,0:T(8,128)}, u32[]{:S(2)}) copy-start(f32[32,32,128]{2,1,0:T(8,128)} %get-tuple-element.28) | copy-start | bytes 1572868
  337.7 14.1 %copy-start.3 = (f32[32,32,128]{2,1,0:T(8,128)S(1)}, f32[32,32,128]{2,1,0:T(8,128)}, u32[]{:S(2)}) copy-start(f32[32,32,128]{2,1,0:T(8,128)} %get-tuple-element.27) | copy-start | bytes 1572868
  337.7 15.6 %copy-start.8 = (f32[32,16,128]{2,1,0:T(8,128)S(1)}, f32[32,16,128]{2,1,0:T(8,128)}, u32[]{:S(2)}) copy-start(f32[32,16,128]{2,1,0:T(8,128)} %get-tuple-element.42) | copy-start | bytes 786436
  337.7 16.4 %copy-start.7 = (f32[32,16,128]{2,1,0:T(8,128)S(1)}, f32[32,16,128]{2,1,0:T(8,128)}, u32[]{:S(2)}) copy-start(f32[32,16,128]{2,1,0:T(8,128)} %get-tuple-element.41) | copy-start | bytes 786436
  338.6 19.0 %copy-start.22 = (f32[16,128]{1,0:T(8,128)S(1)}, f32[16,128]{1,0:T(8,128)}, u32[]{:S(2)}) copy-start(f32[16,128]{1,0:T(8,128)} %get-tuple-element.56) | copy-start | bytes 24580
  338.6 19.0 %copy-start.23 = (f32[16,128]{1,0:T(8,128)S(1)}, f32[16,128]{1,0:T(8,128)}, u32[]{:S(2)}) copy-start(f32[16,128]{1,0:T(8,128)} %get-tuple-element.57) | copy-start | bytes 24580
  338.6 19.0 %copy-start.24 = (f32[16,128]{1,0:T(8,128)S(1)}, f32[16,128]{1,0:T(8,128)}, u32[]{:S(2)}) copy-start(f32[16,128]{1,0:T(8,128)} %get-tuple-element.58) | copy-start | bytes 24580
  338.6 19.0 %copy-start.25 = (f32[16,128]{1,0:T(8,128)S(1)}, f32[16,128]{1,0:T(8,128)}, u32[]{:S(2)}) copy-start(f32[16,128]{1,0:T(8,128)} %get-tuple-element.59) | copy-start | bytes 24580
  338.6 19.0 %copy-start.33 = (f32[384]{0:T(512)S(1)}, f32[384]{0:T(512)}, u32[]{:S(2)}) copy-start(f32[384]{0:T(512)} %convert_add_fusion.1) | copy-start | bytes 4612
  340.3 16.5 %collective-permute-start.1 = (f32[16,128]{1,0:T(8,128)S(1)}, f32[16,128]{1,0:T(8,128)S(1)}, u32[]{:S(2)}, u32[]{:S(2)}) collective-permute-start(f32[16,128]{1,0:T(8,128)S(1)} %get-tuple-element.64), channel_id=1, source_target_pairs={{0,1},{2,3},{4,5},{6,7},{8,9},{10,11},{12,13},{14,15},{16,17},{18,... | collective-permute-start | bytes 24584 | tf_op jit(solution)/shard_map/ppermute | solution.py:14
  343.7 13.1 %collective-permute-start.2 = (f32[16,128]{1,0:T(8,128)S(1)}, f32[16,128]{1,0:T(8,128)S(1)}, u32[]{:S(2)}, u32[]{:S(2)}) collective-permute-start(f32[16,128]{1,0:T(8,128)S(1)} %get-tuple-element.67), channel_id=1, source_target_pairs={{0,1},{2,3},{4,5},{6,7},{8,9},{10,11},{12,13},{14,15},{16,17},{18,... | collective-permute-start | bytes 24584 | tf_op jit(solution)/shard_map/ppermute | solution.py:14
  345.0 11.9 %collective-permute-start.3 = (f32[16,128]{1,0:T(8,128)S(1)}, f32[16,128]{1,0:T(8,128)S(1)}, u32[]{:S(2)}, u32[]{:S(2)}) collective-permute-start(f32[16,128]{1,0:T(8,128)S(1)} %get-tuple-element.66), channel_id=1, source_target_pairs={{0,1},{2,3},{4,5},{6,7},{8,9},{10,11},{12,13},{14,15},{16,17},{18,... | collective-permute-start | bytes 24584 | tf_op jit(solution)/shard_map/ppermute | solution.py:14
  346.3 10.6 %collective-permute-start.4 = (f32[16,128]{1,0:T(8,128)S(1)}, f32[16,128]{1,0:T(8,128)S(1)}, u32[]{:S(2)}, u32[]{:S(2)}) collective-permute-start(f32[16,128]{1,0:T(8,128)S(1)} %get-tuple-element.65), channel_id=1, source_target_pairs={{0,1},{2,3},{4,5},{6,7},{8,9},{10,11},{12,13},{14,15},{16,17},{18,... | collective-permute-start | bytes 24584 | tf_op jit(solution)/shard_map/ppermute | solution.py:14
  350.4 11.5 %copy-start.27 = (pred[384]{0:T(512)(128)(4,1)S(1)}, pred[384]{0:T(512)(128)(4,1)}, u32[]{:S(2)}) copy-start(pred[384]{0:T(512)(128)(4,1)} %copy-done.26) | copy-start | bytes 1156
  350.5 11.5 %copy-start.31 = (f32[128]{0:T(128)S(1)}, f32[128]{0:T(128)}, u32[]{:S(2)}) copy-start(f32[128]{0:T(128)} %get-tuple-element.88) | copy-start | bytes 1540
  (21 other events, 107.0 us)
Sparse Core Ops, SparseCore 0:
  10.6 80.7 all-gather.10
  93.6 76.2 all-gather.4
  172.0 76.2 all-gather.8
  250.4 76.2 all-gather.6

commit v2 on v1

--- a/solution.py
+++ b/solution.py
@@ -4,7 +4,6 @@
 from jax.sharding import PartitionSpec as P
 
 STEER_W = 1024
-CHUNKS = 4
 BLOCK = 32
 
 
@@ -85,59 +84,38 @@
     after = jnp.arange(cap).astype(jnp.float32) + 1.0
     rescale = jnp.exp(decay_rate * (cap - own_len).astype(jnp.float32))
 
-    n = slab // CHUNKS
-    mixed = None
-    for j in range(CHUNKS):
-        cols = slice(j * n, (j + 1) * n)
-        piece = jnp.concatenate(
-            [
-                w_in[:, j * n : (j + 1) * n],
-                w_in[:, slab + j * n : slab + (j + 1) * n],
-                w_in[:, 2 * slab + j * n : 2 * slab + (j + 1) * n],
-                w_out[j * n : (j + 1) * n, :].T,
-            ],
-            axis=1,
-        )
-        gathered = lax.all_gather(piece, "dp", axis=0, tiled=True)
-        w_in_j = gathered[:, : 3 * n]
-        w_out_t = gathered[:, 3 * n :]
-        proj = jnp.dot(normed, w_in_j, preferred_element_type=jnp.float32).astype(jnp.bfloat16)
-        tail = jnp.dot(tail_normed, w_in_j, preferred_element_type=jnp.float32).astype(jnp.bfloat16)
-        extended = jnp.concatenate([tail, proj], axis=0).astype(jnp.float32)
-        sf = jnp.concatenate(
-            [
-                short_filter[:, j * n : (j + 1) * n],
-                short_filter[:, slab + j * n : slab + (j + 1) * n],
-                short_filter[:, 2 * slab + j * n : 2 * slab + (j + 1) * n],
-            ],
-            axis=1,
-        )
-        feat = sf[0] * extended[2:] + sf[1] * extended[1:-1] + sf[2] * extended[:-2]
-        gate = feat[:, :n]
-        drive = jnp.where(live[:, None], feat[:, n : 2 * n] * feat[:, 2 * n :], 0.0)
-        rate = decay_rate[:, cols]
-        local, final_state = local_filter(
-            drive, rate, toeplitz[:, :, cols], lead[:, :, cols], close[:, :, cols], block
-        )
-        ending = final_state * rescale[:, cols]
-        incoming = jnp.zeros_like(ending)
-        for k in range(1, groups):
-            got = from_behind(ending, "ctx", k)
-            source = position - k
-            between = (
-                lax.dynamic_index_in_dim(cumlen, jnp.maximum(position - 1, 0), 0, keepdims=False)
-                - lax.dynamic_index_in_dim(cumlen, jnp.maximum(source, 0), 0, keepdims=False)
-            )
-            weight = jnp.where(source >= 0, jnp.exp(-rate * between), 0.0)
-            incoming = incoming + weight * got
-        reach = residue[None, :, cols] * jnp.exp(-rate[None] * after[:, None, None])
-        crossing = jnp.sum(reach * incoming[None], axis=1)
-        filtered = local + crossing + skip_gain[None, cols] * drive
-        gated = jnp.where(live[:, None], gate * filtered, 0.0).astype(jnp.bfloat16)
-        part = lax.dot_general(
-            gated, w_out_t, (((1,), (1,)), ((), ())), preferred_element_type=jnp.float32
-        )
-        mixed = part if mixed is None else mixed + part
+    piece = jnp.concatenate([w_in, w_out.T], axis=1)
+    gathered = lax.all_gather(piece, "dp", axis=0, tiled=True)
+    w_in_all = gathered[:, : 3 * slab]
+    w_out_t = gathered[:, 3 * slab :]
+    proj = jnp.dot(normed, w_in_all, preferred_element_type=jnp.float32).astype(jnp.bfloat16)
+    tail = jnp.dot(tail_normed, w_in_all, preferred_element_type=jnp.float32).astype(jnp.bfloat16)
+    extended = jnp.concatenate([tail, proj], axis=0).astype(jnp.float32)
+    feat = (
+        short_filter[0] * extended[2:]
+        + short_filter[1] * extended[1:-1]
+        + short_filter[2] * extended[:-2]
+    )
+    gate = feat[:, :slab]
+    drive = jnp.where(live[:, None], feat[:, slab : 2 * slab] * feat[:, 2 * slab :], 0.0)
+    local, final_state = local_filter(drive, decay_rate, toeplitz, lead, close, block)
+    ending = final_state * rescale
+    incoming = jnp.zeros_like(ending)
+    for k in range(1, groups):
+        got = from_behind(ending, "ctx", k)
+        source = position - k
+        between = lax.dynamic_index_in_dim(
+            cumlen, jnp.maximum(position - 1, 0), 0, keepdims=False
+        ) - lax.dynamic_index_in_dim(cumlen, jnp.maximum(source, 0), 0, keepdims=False)
+        weight = jnp.where(source >= 0, jnp.exp(-decay_rate * between), 0.0)
+        incoming = incoming + weight * got
+    reach = residue[None] * jnp.exp(-decay_rate[None] * after[:, None, None])
+    crossing = jnp.sum(reach * incoming[None], axis=1)
+    filtered = local + crossing + skip_gain[None, :] * drive
+    gated = jnp.where(live[:, None], gate * filtered, 0.0).astype(jnp.bfloat16)
+    mixed = lax.dot_general(
+        gated, w_out_t, (((1,), (1,)), ((), ())), preferred_element_type=jnp.float32
+    )
     rows2 = lax.dynamic_index_in_dim(steer_table, steer_layer[0], 0, keepdims=False)
     shift_vec = rows2[0] - rows2[1]
     columns = jnp.arange(width) // STEER_W

time: 416 us -> 250 us (0.60); the launches traced: 411 us -> 249 us
  waiting for transfers between devices: 237 us -> 138 us
  matrix products: 90.1 us -> 38.3 us
  local copies, waits for them, and re-layouts: 15.9 us -> 10.1 us
    all_gather x4 -> x1, waiting for transfers between devices: 237 us -> 138 us  [per_device(): gathered = lax.all_gather(piece, 'dp', axis=0, tiled=True)]
    dot_general x4 -> x1, matrix products: 41.2 us -> 11.9 us  [per_device(): lax.dot_general(gated, w_out_t, (((1,), (1,)), ((), ())), preferred_eleme...]
    dot_general x8 -> x2, matrix products: 48.9 us -> 26.4 us  [the longest x1 16.5 us: per_device(): jnp.dot(normed, w_in_all, preferred_element_type=jnp.float32)]
    slice x6 -> x1, local copies, waits for them, and re-layouts: 5.54 us -> 0.05 us  [per_device(): short_filter[0] * extended[2:] + short_filter[1] * extended[1:-1]]
    ppermute x5 -> x2, starting transfers between devices: 11.9 us -> 9.03 us  [from_behind(): lax.ppermute(value, axis, [(source, source + steps) for source in range(f...]
  transfers between devices with their start and end apart: 9 -> 3, of which waited for: 4 -> 1; matrix products, arithmetic and copies ran while one was open for 19% -> 16% of each run, Pallas kernels for 0% -> 0%
where the time goes in v2:
time: 250 us; the launch traced here: 249 us
  waiting for transfers between devices  138 us (55%)
  matrix products  38.3 us (15%)
  other arithmetic  36 us (14%)
  between operations  17.1 us (7%)
  local copies, waits for them, and re-layouts  10.1 us (4%)
  starting transfers between devices  9.03 us (4%)
    all_gather x1, waiting for transfers between devices, per_device(): gathered = lax.all_gather(piece, 'dp', axis=0, tiled=True)  138 us
    dot_general x1, matrix products, per_device(): jnp.dot(normed, w_in_all, preferred_element_type=jnp.float32)  16.5 us
    dot_general x1, matrix products, per_device(): lax.dot_general(gated, w_out_t, (((1,), (1,)), ((), ())), preferred_eleme...  11.9 us
    dot_general x1, matrix products, per_device(): jnp.dot(tail_normed, w_in_all, preferred_element_type=jnp.float32)  9.9 us
    ppermute x2, starting transfers between devices, from_behind(): lax.ppermute(value, axis, [(source, source + steps) for source in range(f...  9.03 us
    reduce_sum x1, other arithmetic, local_filter(): inside = jnp.sum(toeplitz[None] * pieces[:, None, :, :], axis=2)  5.5 us
  transfers between devices with their start and end apart: 3, of which 1 were waited for; matrix products, arithmetic and copies ran while one was open for 16% of the time, Pallas kernels for 0%

profile of v2, /device:TPU:0, one launch (start us, length us, event | category | flops | bytes accessed | tf_op | source)
XLA Modules:
  0.0 249.1 jit_solution(281652849096402255)
XLA Ops:
  6.5 1.3 copy.15
  7.8 3.0 %pad_maximum_fusion = bf16[512,2048]{1,0:T(8,128)(2,1)} fusion(bf16[512,512]{1,0:T(8,128)(2,1)S(1)} %copy.15, bf16[512,1536]{1,0:T(8,128)(2,1)} %param.15), kind=kLoop, calls=%fused_computation.28 | loop fusion | flops 4194304 | bytes 4194304 | tf_op jit(solution)/shard_map/concatenate | solution.py:87
  10.9 0.7 constant_dynamic-slice_fusion.2
  12.9 4.1 %fusion.4 = f32[384]{0:T(512)S(1)} fusion(bf16[1,1,384,8192]{3,2,1,0:T(8,128)(2,1)} %param.12), kind=kLoop, calls=%fused_computation.9 | loop fusion | flops 9436800 | bytes 6292992 | tf_op jit(solution)/shard_map/reduce_sum | solution.py:18
  17.1 4.7 %fusion.6 = bf16[384,8192]{1,0:T(8,128)(2,1)S(1)} fusion(bf16[1,1,384,8192]{3,2,1,0:T(8,128)(2,1)} %param.12, f32[8192]{0:T(1024)S(1)} %copy-done.3, f32[384]{0:T(512)S(1)} %add_rsqrt_fusion), kind=kLoop, calls=%fused_computation.11 | loop fusion | flops 12582912 | bytes 12617216 | tf_op jit(solution)/shard_map/convert_element_type | solution.py:19
  21.8 2.7 %copy-done = bf16[384,8192]{1,0:T(8,128)(2,1)} copy-done((bf16[384,8192]{1,0:T(8,128)(2,1)}, bf16[384,8192]{1,0:T(8,128)(2,1)S(1)}, u32[]{:S(2)}) %copy-start) | copy-done | bytes 6291480
  24.6 5.7 %collective-permute-start = (bf16[2,8192]{1,0:T(2,128)(2,1)S(1)}, bf16[2,8192]{1,0:T(2,128)(2,1)S(1)}, u32[]{:S(2)}, u32[]{:S(2)}) collective-permute-start(bf16[2,8192]{1,0:T(2,128)(2,1)S(1)} %constant_dynamic-slice_fusion.1), channel_id=1, source_target_pairs={{0,1},{2,3},{4,5},{6,7},{8,9},{10,11},{12,13},{14,15},{16,17},{18,... | collective-permute-start | bytes 98312 | tf_op jit(solution)/shard_map/ppermute | solution.py:13
  32.4 1.6 exponential_multiply_fusion
  34.0 4.8 %gather_fusion = f32[1024,512]{1,0:T(8,128)} fusion(f32[32,512]{1,0:T(8,128)S(1)} %get-tuple-element.9, s32[1024]{0:T(1024)S(1)} %broadcast_clamp_fusion), kind=kCustom, calls=%fused_computation | custom fusion | bytes 4198400 | tf_op jit(solution)/shard_map/gather | solution.py:27
  39.7 0.7 iota_compare_fusion
  40.5 1.0 fusion.27
  41.5 1.9 broadcast_select_fusion
  43.3 138.5 %all-gather.2.cloned.1.call-done = bf16[8192,2048]{1,0:T(8,128)(2,1)} async-done(((bf16[512,2048]{1,0:T(8,128)(2,1)}), bf16[8192,2048]{1,0:T(8,128)(2,1)}) %all-gather.2.cloned.1.call-update) | async-done | bytes 33554448 | tf_op jit(solution)/shard_map/all_gather | solution.py:88
  181.8 16.5 %fusion.12 = bf16[384,1536]{1,0:T(8,128)(2,1)S(1)} fusion(bf16[384,8192]{1,0:T(8,128)(2,1)} %copy-done, bf16[8192,2048]{1,0:T(8,128)(2,1)} %all-gather.2.cloned.1.call-done), kind=kOutput, calls=%fused_computation.21 | convolution fusion | flops 9664266240 | bytes 32636928 | tf_op jit(solution)/shard_map/dot_general | solution.py:91
  198.3 9.9 %fusion.17 = bf16[2,1536]{1,0:T(2,128)(2,1)S(1)} fusion(bf16[2,8192]{1,0:T(2,128)(2,1)S(1)} %collective-permute-done, bf16[8192,2048]{1,0:T(8,128)(2,1)} %all-gather.2.cloned.1.call-done), kind=kOutput, calls=%fused_computation.27 | convolution fusion | flops 50334720 | bytes 25204736 | tf_op jit(solution)/shard_map/dot_general | solution.py:92
  208.5 0.7 fusion.15
  209.7 1.1 multiply_reduce_fusion.3
  210.8 1.6 multiply_reduce_fusion.4
  212.5 5.5 %multiply_reduce_fusion = f32[12,32,512]{2,1,0:T(8,128)S(1)} fusion(f32[12,32,512]{2,1,0:T(8,128)S(1)} %bitcast.38, f32[32,32,512]{2,1,0:T(8,128)S(1)} %broadcast_select_fusion), kind=kLoop, calls=%fused_computation.1 | loop fusion | flops 12386304 | bytes 3670016 | tf_op jit(solution)/shard_map/reduce_sum | solution.py:37
  218.0 3.4 %collective-permute-start.1 = (f32[16,512]{1,0:T(8,128)S(1)}, f32[16,512]{1,0:T(8,128)S(1)}, u32[]{:S(2)}, u32[]{:S(2)}) collective-permute-start(f32[16,512]{1,0:T(8,128)S(1)} %fusion.28), channel_id=1, source_target_pairs={{0,1},{2,3},{4,5},{6,7},{8,9},{10,11},{12,13},{14,15},{16,17},{18,... | collective-permute-start | bytes 98312 | tf_op jit(solution)/shard_map/ppermute | solution.py:13
  221.4 3.4 %multiply_reduce_fusion.2 = f32[12,32,512]{2,1,0:T(8,128)S(1)} fusion(f32[12,16,512]{2,1,0:T(8,128)S(1)} %concatenate.11, f32[32,16,512]{2,1,0:T(8,128)S(1)} %get-tuple-element.8), kind=kLoop, calls=%fused_computation.16 | loop fusion | flops 6094848 | bytes 2228224 | tf_op jit(solution)/shard_map/reduce_sum | solution.py:48
  225.0 0.6 select_multiply_fusion
  225.7 4.3 %multiply_reduce_fusion.1 = f32[384,512]{1,0:T(8,128)S(1)} fusion(f32[16,512]{1,0:T(8,128)S(1)} %select_multiply_fusion, f32[384]{0:T(512)S(1)} %convert_add_fusion.1, f32[16,512]{1,0:T(8,128)S(1)} %neg.4, f32[16,512]{1,0:T(8,128)S(1)} %copy-done.4), kind=kLoop, calls=%fused_computation.15 | loop fusion | flops 12386304 | bytes 886272 | tf_op jit(solution)/shard_map/reduce_sum | solution.py:113
  230.3 11.9 %fusion.10 = bf16[1,1,384,8192]{3,2,1,0:T(8,128)(2,1)} fusion(bf16[384,512]{1,0:T(8,128)(2,1)S(1)} %fusion.22, bf16[8192,2048]{1,0:T(8,128)(2,1)} %all-gather.2.cloned.1.call-done, bf16[1,1,384,8192]{3,2,1,0:T(8,128)(2,1)} %param.12, f32[8192]{0:T(1024)S(1)} %fusion.30, pred[384]{0:T(512)(128)(4,1)S(1)} %iota_compare_fusion), kind=kOutput, calls=%fused_computation.18 | convolution fusion | flops 3236954112 | bytes 21397888 | tf_op jit(solution)/shard_map/dot_general | solution.py:116
  (43 shorter events, 2.5 us)
Async XLA Ops:
  6.5 4.4 %copy-start.7 = (s32[1,2]{1,0:T(1,128)S(1)}, s32[1,2]{1,0:T(1,128)}, u32[]{:S(2)}) copy-start(s32[1,2]{1,0:T(1,128)} %param.13) | copy-start | bytes 28
  6.5 175.3 %all-gather.2.cloned.1.call-start = ((), (), s32[]{:S(2)}) async-start(), calls=%async_computation | async-start | bytes 35651584 | tf_op jit(solution)/shard_map/all_gather | solution.py:88
  7.8 9.3 %copy-start.3 = (f32[8192]{0:T(1024)S(1)}, f32[8192]{0:T(1024)}, u32[]{:S(2)}) copy-start(f32[8192]{0:T(1024)} %param.14) | copy-start | bytes 98308
  17.1 13.2 %copy-start.2 = (f32[16,512]{1,0:T(8,128)S(1)}, f32[16,512]{1,0:T(8,128)}, u32[]{:S(2)}) copy-start(f32[16,512]{1,0:T(8,128)} %param.17) | copy-start | bytes 98308
  17.1 15.3 %copy-start.4 = (f32[16,512]{1,0:T(8,128)S(1)}, f32[16,512]{1,0:T(8,128)}, u32[]{:S(2)}) copy-start(f32[16,512]{1,0:T(8,128)} %param.18) | copy-start | bytes 98308
  21.8 2.7 %copy-start = (bf16[384,8192]{1,0:T(8,128)(2,1)}, bf16[384,8192]{1,0:T(8,128)(2,1)S(1)}, u32[]{:S(2)}) copy-start(bf16[384,8192]{1,0:T(8,128)(2,1)S(1)} %fusion.6) | copy-start | bytes 18874372
  24.6 173.7 %collective-permute-start = (bf16[2,8192]{1,0:T(2,128)(2,1)S(1)}, bf16[2,8192]{1,0:T(2,128)(2,1)S(1)}, u32[]{:S(2)}, u32[]{:S(2)}) collective-permute-start(bf16[2,8192]{1,0:T(2,128)(2,1)S(1)} %constant_dynamic-slice_fusion.1), channel_id=1, source_target_pairs={{0,1},{2,3},{4,5},{6,7},{8,9},{10,11},{12,13},{14,15},{16,17},{18,... | collective-permute-start | bytes 98312 | tf_op jit(solution)/shard_map/ppermute | solution.py:13
  34.0 6.4 %copy-start.5 = (f32[3,1536]{1,0:T(4,128)S(1)}, f32[3,1536]{1,0:T(4,128)}, u32[]{:S(2)}) copy-start(f32[3,1536]{1,0:T(4,128)} %param.16) | copy-start | bytes 55300
  208.5 1.2 copy-start.1
  218.0 12.0 %copy-start.6 = (f32[512]{0:T(512)S(1)}, f32[512]{0:T(512)}, u32[]{:S(2)}) copy-start(f32[512]{0:T(512)} %param.19) | copy-start | bytes 6148
  218.0 7.0 %collective-permute-start.1 = (f32[16,512]{1,0:T(8,128)S(1)}, f32[16,512]{1,0:T(8,128)S(1)}, u32[]{:S(2)}, u32[]{:S(2)}) collective-permute-start(f32[16,512]{1,0:T(8,128)S(1)} %fusion.28), channel_id=1, source_target_pairs={{0,1},{2,3},{4,5},{6,7},{8,9},{10,11},{12,13},{14,15},{16,17},{18,... | collective-permute-start | bytes 98312 | tf_op jit(solution)/shard_map/ppermute | solution.py:13
Sparse Core Ops, SparseCore 0:
  11.0 170.7 all-gather.1

commit v3 on v2

--- a/solution.py
+++ b/solution.py
@@ -30,11 +30,10 @@
     return toeplitz, lead, close
 
 
-def local_filter(drive, decay_rate, toeplitz, lead, close, block):
+def block_states(drive, decay_rate, close, block):
     cap, width = drive.shape
     count = cap // block
     pieces = drive.reshape(count, block, width)
-    inside = jnp.sum(toeplitz[None] * pieces[:, None, :, :], axis=2)
     ends = jnp.sum(close[None] * pieces[:, :, None, :], axis=1)
     steps = jnp.arange(count)
     gap = (steps[:, None] - steps[None, :]).astype(jnp.float32)
@@ -43,10 +42,19 @@
         jnp.exp(-decay_rate[None, None] * (block * jnp.maximum(gap, 0.0))[:, :, None, None]),
         0.0,
     )
-    states = jnp.sum(powers * ends[None], axis=1)
-    before = jnp.concatenate([jnp.zeros_like(states[:1]), states[:-1]], axis=0)
+    return jnp.sum(powers * ends[None], axis=1)
+
+
+def block_outputs(drive, states, incoming, decay_rate, toeplitz, lead, block):
+    cap, width = drive.shape
+    count = cap // block
+    pieces = drive.reshape(count, block, width)
+    inside = jnp.sum(toeplitz[None] * pieces[:, None, :, :], axis=2)
+    starts = (jnp.arange(count) * block).astype(jnp.float32)
+    carried = incoming[None] * jnp.exp(-decay_rate[None] * starts[:, None, None])
+    before = jnp.concatenate([jnp.zeros_like(states[:1]), states[:-1]], axis=0) + carried
     earlier = jnp.sum(lead[None] * before[:, None, :, :], axis=2)
-    return (inside + earlier).reshape(cap, width), states[-1]
+    return (inside + earlier).reshape(cap, width)
 
 
 def per_device(
@@ -81,16 +89,15 @@
 
     lens_f = group_lens.astype(jnp.float32)
     cumlen = jnp.cumsum(lens_f)
-    after = jnp.arange(cap).astype(jnp.float32) + 1.0
     rescale = jnp.exp(decay_rate * (cap - own_len).astype(jnp.float32))
 
     piece = jnp.concatenate([w_in, w_out.T], axis=1)
     gathered = lax.all_gather(piece, "dp", axis=0, tiled=True)
     w_in_all = gathered[:, : 3 * slab]
     w_out_t = gathered[:, 3 * slab :]
-    proj = jnp.dot(normed, w_in_all, preferred_element_type=jnp.float32).astype(jnp.bfloat16)
-    tail = jnp.dot(tail_normed, w_in_all, preferred_element_type=jnp.float32).astype(jnp.bfloat16)
-    extended = jnp.concatenate([tail, proj], axis=0).astype(jnp.float32)
+    rows_ext = jnp.concatenate([tail_normed, normed], axis=0)
+    extended = jnp.dot(rows_ext, w_in_all, preferred_element_type=jnp.float32)
+    extended = extended.astype(jnp.bfloat16).astype(jnp.float32)
     feat = (
         short_filter[0] * extended[2:]
         + short_filter[1] * extended[1:-1]
@@ -98,8 +105,8 @@
     )
     gate = feat[:, :slab]
     drive = jnp.where(live[:, None], feat[:, slab : 2 * slab] * feat[:, 2 * slab :], 0.0)
-    local, final_state = local_filter(drive, decay_rate, toeplitz, lead, close, block)
-    ending = final_state * rescale
+    states = block_states(drive, decay_rate, close, block)
+    ending = states[-1] * rescale
     incoming = jnp.zeros_like(ending)
     for k in range(1, groups):
         got = from_behind(ending, "ctx", k)
@@ -109,9 +116,8 @@
         ) - lax.dynamic_index_in_dim(cumlen, jnp.maximum(source, 0), 0, keepdims=False)
         weight = jnp.where(source >= 0, jnp.exp(-decay_rate * between), 0.0)
         incoming = incoming + weight * got
-    reach = residue[None] * jnp.exp(-decay_rate[None] * after[:, None, None])
-    crossing = jnp.sum(reach * incoming[None], axis=1)
-    filtered = local + crossing + skip_gain[None, :] * drive
+    local = block_outputs(drive, states, incoming, decay_rate, toeplitz, lead, block)
+    filtered = local + skip_gain[None, :] * drive
     gated = jnp.where(live[:, None], gate * filtered, 0.0).astype(jnp.bfloat16)
     mixed = lax.dot_general(
         gated, w_out_t, (((1,), (1,)), ((), ())), preferred_element_type=jnp.float32

time: 250 us -> 236 us (0.944)
  matrix products: 38.3 us -> 28.6 us
    dot_general x2 -> x1, matrix products: 26.4 us -> 16.7 us  [per_device(): extended = jnp.dot(rows_ext, w_in_all, preferred_element_type=jnp.float32)]
    reduce_sum x5 -> x4, other arithmetic: 15.9 us -> 11.4 us  [the longest x1 5.54 us: block_outputs(): inside = jnp.sum(toeplitz[None] * pieces[:, None, :, :], axis=2)]
  transfers between devices with their start and end apart: 3 -> 3, of which waited for: 1 -> 1; matrix products, arithmetic and copies ran while one was open for 16% -> 12% of each run, Pallas kernels for 0% -> 0%
where the time goes in v3:
time: 236 us
  waiting for transfers between devices  137 us (58%)
  other arithmetic  34.3 us (15%)
  matrix products  28.6 us (12%)
  between operations  17.2 us (7%)
  local copies, waits for them, and re-layouts  9.57 us (4%)
  starting transfers between devices  9.25 us (4%)
    all_gather x1, waiting for transfers between devices, per_device(): gathered = lax.all_gather(piece, 'dp', axis=0, tiled=True)  137 us
    dot_general x1, matrix products, per_device(): extended = jnp.dot(rows_ext, w_in_all, preferred_element_type=jnp.float32)  16.7 us
    dot_general x1, matrix products, per_device(): lax.dot_general(gated, w_out_t, (((1,), (1,)), ((), ())), preferred_eleme...  11.9 us
    ppermute x2, starting transfers between devices, from_behind(): lax.ppermute(value, axis, [(source, source + steps) for source in range(f...  9.25 us
    reduce_sum x1, other arithmetic, block_outputs(): inside = jnp.sum(toeplitz[None] * pieces[:, None, :, :], axis=2)  5.54 us
    convert_element_type x1, other arithmetic, normalize(): return (values * scale * gain[None, :]).astype(jnp.bfloat16)  4.73 us
  transfers between devices with their start and end apart: 3, of which 1 were waited for; matrix products, arithmetic and copies ran while one was open for 12% of the time, Pallas kernels for 0%

profile of v3, /device:TPU:0, one launch (start us, length us, event | category | flops | bytes accessed | tf_op | source)
XLA Modules:
  0.0 235.5 jit_solution(7256951210691565861)
XLA Ops:
  6.5 1.3 copy.15
  7.8 3.0 %pad_maximum_fusion = bf16[512,2048]{1,0:T(8,128)(2,1)} fusion(bf16[512,512]{1,0:T(8,128)(2,1)S(1)} %copy.15, bf16[512,1536]{1,0:T(8,128)(2,1)} %param.15), kind=kLoop, calls=%fused_computation.28 | loop fusion | flops 4194304 | bytes 4194304 | tf_op jit(solution)/shard_map/concatenate | solution.py:94
  10.9 0.7 constant_dynamic-slice_fusion.2
  12.9 4.1 %fusion.2 = f32[384]{0:T(512)S(1)} fusion(bf16[1,1,384,8192]{3,2,1,0:T(8,128)(2,1)} %param.12), kind=kLoop, calls=%fused_computation.7 | loop fusion | flops 9436800 | bytes 6292992 | tf_op jit(solution)/shard_map/reduce_sum | solution.py:18
  17.1 4.7 %fusion.4 = bf16[384,8192]{1,0:T(8,128)(2,1)S(1)} fusion(bf16[1,1,384,8192]{3,2,1,0:T(8,128)(2,1)} %param.12, f32[8192]{0:T(1024)S(1)} %copy-done.4, f32[384]{0:T(512)S(1)} %add_rsqrt_fusion), kind=kLoop, calls=%fused_computation.9 | loop fusion | flops 12582912 | bytes 12617216 | tf_op jit(solution)/shard_map/convert_element_type | solution.py:19
  21.8 2.7 %copy-done.1 = bf16[384,8192]{1,0:T(8,128)(2,1)} copy-done((bf16[384,8192]{1,0:T(8,128)(2,1)}, bf16[384,8192]{1,0:T(8,128)(2,1)S(1)}, u32[]{:S(2)}) %copy-start.1) | copy-done | bytes 6291480
  24.6 5.7 %collective-permute-start = (bf16[2,8192]{1,0:T(2,128)(2,1)S(1)}, bf16[2,8192]{1,0:T(2,128)(2,1)S(1)}, u32[]{:S(2)}, u32[]{:S(2)}) collective-permute-start(bf16[2,8192]{1,0:T(2,128)(2,1)S(1)} %constant_dynamic-slice_fusion.1), channel_id=1, source_target_pairs={{0,1},{2,3},{4,5},{6,7},{8,9},{10,11},{12,13},{14,15},{16,17},{18,... | collective-permute-start | bytes 98312 | tf_op jit(solution)/shard_map/ppermute | solution.py:13
  31.7 1.6 exponential_multiply_fusion
  33.3 3.5 %gather_fusion = f32[1024,512]{1,0:T(8,128)S(1)} fusion(f32[32,512]{1,0:T(8,128)S(1)} %get-tuple-element.9, s32[1024]{0:T(1024)S(1)} %broadcast_clamp_fusion), kind=kCustom, calls=%fused_computation | custom fusion | bytes 4198400 | tf_op jit(solution)/shard_map/gather | solution.py:27
  36.8 1.3 iota_compare_fusion
  39.3 0.6 slice_reduce_fusion.2
  40.0 1.0 fusion.31
  41.0 1.6 broadcast_select_fusion
  44.0 0.7 fusion.36
  45.3 136.5 %all-gather.2.cloned.1.call-done = bf16[8192,2048]{1,0:T(8,128)(2,1)} async-done(((bf16[512,2048]{1,0:T(8,128)(2,1)}), bf16[8192,2048]{1,0:T(8,128)(2,1)}) %all-gather.2.cloned.1.call-update) | async-done | bytes 33554448 | tf_op jit(solution)/shard_map/all_gather | solution.py:95
  181.8 16.7 %fusion.18 = f32[386,1536]{1,0:T(8,128)S(1)} fusion(bf16[8192,2048]{1,0:T(8,128)(2,1)} %all-gather.2.cloned.1.call-done, bf16[384,8192]{1,0:T(8,128)(2,1)} %copy-done.1, bf16[2,8192]{1,0:T(2,128)(2,1)} %copy-done.12), kind=kOutput, calls=%fused_computation.22 | convolution fusion | flops 9727842304 | bytes 33861632 | tf_op jit(solution)/shard_map/dot_general | solution.py:99
  198.6 1.6 fusion.23
  200.3 1.1 multiply_reduce_fusion.2
  201.4 1.3 multiply_reduce_fusion.3
  202.8 3.6 %collective-permute-start.1 = (f32[16,512]{1,0:T(8,128)S(1)}, f32[16,512]{1,0:T(8,128)S(1)}, u32[]{:S(2)}, u32[]{:S(2)}) collective-permute-start(f32[16,512]{1,0:T(8,128)S(1)} %fusion.32), channel_id=1, source_target_pairs={{0,1},{2,3},{4,5},{6,7},{8,9},{10,11},{12,13},{14,15},{16,17},{18,... | collective-permute-start | bytes 98312 | tf_op jit(solution)/shard_map/ppermute | solution.py:13
  206.4 5.5 %multiply_reduce_fusion = f32[12,32,512]{2,1,0:T(8,128)S(1)} fusion(f32[12,32,512]{2,1,0:T(8,128)S(1)} %bitcast.34, f32[32,32,512]{2,1,0:T(8,128)S(1)} %copy-done), kind=kLoop, calls=%fused_computation.3 | loop fusion | flops 12386304 | bytes 3670016 | tf_op jit(solution)/shard_map/reduce_sum | solution.py:52
  212.0 0.7 select_multiply_fusion
  212.9 3.4 %multiply_reduce_fusion.1 = f32[12,32,512]{2,1,0:T(8,128)S(1)} fusion(f32[12,16,512]{2,1,0:T(8,128)S(1)} %multiply_add_fusion, f32[32,16,512]{2,1,0:T(8,128)S(1)} %get-tuple-element.8), kind=kLoop, calls=%fused_computation.13 | loop fusion | flops 6094848 | bytes 2228224 | tf_op jit(solution)/shard_map/reduce_sum | solution.py:56
  216.7 11.9 %fusion.8 = bf16[1,1,384,8192]{3,2,1,0:T(8,128)(2,1)} fusion(bf16[384,512]{1,0:T(8,128)(2,1)S(1)} %fusion.27, bf16[8192,2048]{1,0:T(8,128)(2,1)} %all-gather.2.cloned.1.call-done, bf16[1,1,384,8192]{3,2,1,0:T(8,128)(2,1)} %param.12, f32[8192]{0:T(1024)S(1)} %fusion.34, pred[384]{0:T(512)(128)(4,1)S(1)} %copy-done.9), kind=kOutput, calls=%fused_computation.15 | convolution fusion | flops 3236954112 | bytes 21397888 | tf_op jit(solution)/shard_map/dot_general | solution.py:122
  (52 shorter events, 3.5 us)
Async XLA Ops:
  6.5 4.4 %copy-start.13 = (s32[1,2]{1,0:T(1,128)S(1)}, s32[1,2]{1,0:T(1,128)}, u32[]{:S(2)}) copy-start(s32[1,2]{1,0:T(1,128)} %param.13) | copy-start | bytes 28
  6.5 175.3 %all-gather.2.cloned.1.call-start = ((), (), s32[]{:S(2)}) async-start(), calls=%async_computation | async-start | bytes 35651584 | tf_op jit(solution)/shard_map/all_gather | solution.py:95
  7.8 9.3 %copy-start.4 = (f32[8192]{0:T(1024)S(1)}, f32[8192]{0:T(1024)}, u32[]{:S(2)}) copy-start(f32[8192]{0:T(1024)} %param.14) | copy-start | bytes 98308
  17.1 13.2 %copy-start.3 = (f32[16,512]{1,0:T(8,128)S(1)}, f32[16,512]{1,0:T(8,128)}, u32[]{:S(2)}) copy-start(f32[16,512]{1,0:T(8,128)} %param.17) | copy-start | bytes 98308
  17.1 14.6 %copy-start.5 = (f32[16,512]{1,0:T(8,128)S(1)}, f32[16,512]{1,0:T(8,128)}, u32[]{:S(2)}) copy-start(f32[16,512]{1,0:T(8,128)} %param.18) | copy-start | bytes 98308
  21.8 2.7 %copy-start.1 = (bf16[384,8192]{1,0:T(8,128)(2,1)}, bf16[384,8192]{1,0:T(8,128)(2,1)S(1)}, u32[]{:S(2)}) copy-start(bf16[384,8192]{1,0:T(8,128)(2,1)S(1)} %fusion.4) | copy-start | bytes 18874372
  24.6 20.1 %collective-permute-start = (bf16[2,8192]{1,0:T(2,128)(2,1)S(1)}, bf16[2,8192]{1,0:T(2,128)(2,1)S(1)}, u32[]{:S(2)}, u32[]{:S(2)}) collective-permute-start(bf16[2,8192]{1,0:T(2,128)(2,1)S(1)} %constant_dynamic-slice_fusion.1), channel_id=1, source_target_pairs={{0,1},{2,3},{4,5},{6,7},{8,9},{10,11},{12,13},{14,15},{16,17},{18,... | collective-permute-start | bytes 98312 | tf_op jit(solution)/shard_map/ppermute | solution.py:13
  33.3 6.0 %copy-start.6 = (f32[3,1536]{1,0:T(4,128)S(1)}, f32[3,1536]{1,0:T(4,128)}, u32[]{:S(2)}) copy-start(f32[3,1536]{1,0:T(4,128)} %param.16) | copy-start | bytes 55300
  44.7 0.6 copy-start.12
  198.5 1.6 copy-start.9
  198.5 1.8 copy-start.2
  198.6 2.9 %copy-start.7 = (f32[12,12]{1,0:T(8,128)S(1)}, f32[12,12]{1,0:T(8,128)}, u32[]{:S(2)}) copy-start(f32[12,12]{1,0:T(8,128)} %maximum_multiply_fusion) | copy-start | bytes 1732
  198.6 2.9 %copy-start.10 = (pred[12,12]{1,0:T(8,128)(4,1)S(1)}, pred[12,12]{1,0:T(8,128)(4,1)}, u32[]{:S(2)}) copy-start(pred[12,12]{1,0:T(8,128)(4,1)} %convert_compare_fusion) | copy-start | bytes 436
  198.6 7.8 %copy-start = (f32[32,32,512]{2,1,0:T(8,128)S(1)}, f32[32,32,512]{2,1,0:T(8,128)}, u32[]{:S(2)}) copy-start(f32[32,32,512]{2,1,0:T(8,128)} %broadcast_select_fusion) | copy-start | bytes 6291460
  200.2 12.6 %copy-start.11 = (f32[12]{0:T(128)S(1)}, f32[12]{0:T(128)}, u32[]{:S(2)}) copy-start(f32[12]{0:T(128)} %multiply_convert_fusion) | copy-start | bytes 148
  201.4 15.1 %copy-start.8 = (f32[512]{0:T(512)S(1)}, f32[512]{0:T(512)}, u32[]{:S(2)}) copy-start(f32[512]{0:T(512)} %param.19) | copy-start | bytes 6148
  202.8 9.2 %collective-permute-start.1 = (f32[16,512]{1,0:T(8,128)S(1)}, f32[16,512]{1,0:T(8,128)S(1)}, u32[]{:S(2)}, u32[]{:S(2)}) collective-permute-start(f32[16,512]{1,0:T(8,128)S(1)} %fusion.32), channel_id=1, source_target_pairs={{0,1},{2,3},{4,5},{6,7},{8,9},{10,11},{12,13},{14,15},{16,17},{18,... | collective-permute-start | bytes 98312 | tf_op jit(solution)/shard_map/ppermute | solution.py:13
Sparse Core Ops, SparseCore 0:
  11.0 170.7 all-gather.1

commit v4 on v3

--- a/solution.py
+++ b/solution.py
@@ -25,7 +25,8 @@
     taps = jnp.sum(residue[None] * jnp.exp(-decay_rate[None] * lags_float[:, None, None]), axis=1)
     diff = lags[:, None] - lags[None, :]
     toeplitz = jnp.where((diff >= 0)[:, :, None], taps[jnp.clip(diff, 0, block - 1)], 0.0)
-    lead = residue[None] * jnp.exp(-decay_rate[None] * (lags_float + 1.0)[:, None, None])
+    toeplitz = jnp.transpose(toeplitz, (1, 0, 2))
+    lead = residue[:, None] * jnp.exp(-decay_rate[:, None] * (lags_float + 1.0)[None, :, None])
     close = jnp.exp(-decay_rate[None] * (block - 1 - lags_float)[:, None, None])
     return toeplitz, lead, close
 
@@ -49,11 +50,11 @@
     cap, width = drive.shape
     count = cap // block
     pieces = drive.reshape(count, block, width)
-    inside = jnp.sum(toeplitz[None] * pieces[:, None, :, :], axis=2)
+    inside = jnp.sum(toeplitz[None] * pieces[:, :, None, :], axis=1)
     starts = (jnp.arange(count) * block).astype(jnp.float32)
     carried = incoming[None] * jnp.exp(-decay_rate[None] * starts[:, None, None])
     before = jnp.concatenate([jnp.zeros_like(states[:1]), states[:-1]], axis=0) + carried
-    earlier = jnp.sum(lead[None] * before[:, None, :, :], axis=2)
+    earlier = jnp.sum(lead[None] * before[:, :, None, :], axis=1)
     return (inside + earlier).reshape(cap, width)
 
 
@@ -97,7 +98,7 @@
     w_out_t = gathered[:, 3 * slab :]
     rows_ext = jnp.concatenate([tail_normed, normed], axis=0)
     extended = jnp.dot(rows_ext, w_in_all, preferred_element_type=jnp.float32)
-    extended = extended.astype(jnp.bfloat16).astype(jnp.float32)
+    extended = lax.reduce_precision(extended, exponent_bits=8, mantissa_bits=7)
     feat = (
         short_filter[0] * extended[2:]
         + short_filter[1] * extended[1:-1]

time: 236 us -> 230 us (0.975)
  other arithmetic: 34.3 us -> 29.1 us
  waiting for transfers between devices: 137 us -> 132 us
  local copies, waits for them, and re-layouts: 9.57 us -> 13.5 us
    reduce_sum x2, other arithmetic: 8.99 us -> 3.41 us  [the longest x1 2.4 us: block_outputs(): inside = jnp.sum(toeplitz[None] * pieces[:, :, None, :], axis=1)]
    all_gather x1, waiting for transfers between devices: 137 us -> 132 us  [per_device(): gathered = lax.all_gather(piece, 'dp', axis=0, tiled=True)]
    select_n x0 -> x1, local copies, waits for them, and re-layouts: none -> 2.58 us  [filter_tables(): jnp.where((diff >= 0)[:, :, None], taps[jnp.clip(diff, 0, block - 1)], 0.0)]
where the time goes in v4:
time: 230 us
  waiting for transfers between devices  132 us (57%)
  other arithmetic  29.1 us (13%)
  matrix products  28.7 us (12%)
  between operations  17.2 us (7%)
  local copies, waits for them, and re-layouts  13.5 us (6%)
  starting transfers between devices  9.25 us (4%)
    all_gather x1, waiting for transfers between devices, per_device(): gathered = lax.all_gather(piece, 'dp', axis=0, tiled=True)  132 us
    dot_general x1, matrix products, per_device(): extended = jnp.dot(rows_ext, w_in_all, preferred_element_type=jnp.float32)  16.7 us
    dot_general x1, matrix products, per_device(): lax.dot_general(gated, w_out_t, (((1,), (1,)), ((), ())), preferred_eleme...  11.9 us
    ppermute x2, starting transfers between devices, from_behind(): lax.ppermute(value, axis, [(source, source + steps) for source in range(f...  9.25 us
    gather x1, local copies, waits for them, and re-layouts, filter_tables(): taps[jnp.clip(diff, 0, block - 1)]  4.84 us
    convert_element_type x1, other arithmetic, normalize(): return (values * scale * gain[None, :]).astype(jnp.bfloat16)  4.73 us
  transfers between devices with their start and end apart: 3, of which 1 were waited for; matrix products, arithmetic and copies ran while one was open for 12% of the time, Pallas kernels for 0%

profile of v4, /device:TPU:0, one launch (start us, length us, event | category | flops | bytes accessed | tf_op | source)
XLA Modules:
  0.0 229.9 jit_solution(1049465095491891067)
XLA Ops:
  6.5 1.3 copy.17
  7.8 3.0 %pad_maximum_fusion = bf16[512,2048]{1,0:T(8,128)(2,1)} fusion(bf16[512,512]{1,0:T(8,128)(2,1)S(1)} %copy.17, bf16[512,1536]{1,0:T(8,128)(2,1)} %param.15), kind=kLoop, calls=%fused_computation.27 | loop fusion | flops 4194304 | bytes 4194304 | tf_op jit(solution)/shard_map/concatenate | solution.py:95
  10.9 0.7 constant_dynamic-slice_fusion.2
  12.9 4.1 %fusion.2 = f32[384]{0:T(512)S(1)} fusion(bf16[1,1,384,8192]{3,2,1,0:T(8,128)(2,1)} %param.12), kind=kLoop, calls=%fused_computation.7 | loop fusion | flops 9436800 | bytes 6292992 | tf_op jit(solution)/shard_map/reduce_sum | solution.py:18
  17.1 4.7 %fusion.4 = bf16[384,8192]{1,0:T(8,128)(2,1)S(1)} fusion(bf16[1,1,384,8192]{3,2,1,0:T(8,128)(2,1)} %param.12, f32[8192]{0:T(1024)S(1)} %copy-done.5, f32[384]{0:T(512)S(1)} %add_rsqrt_fusion), kind=kLoop, calls=%fused_computation.9 | loop fusion | flops 12582912 | bytes 12617216 | tf_op jit(solution)/shard_map/convert_element_type | solution.py:19
  21.8 2.7 %copy-done.1 = bf16[384,8192]{1,0:T(8,128)(2,1)} copy-done((bf16[384,8192]{1,0:T(8,128)(2,1)}, bf16[384,8192]{1,0:T(8,128)(2,1)S(1)}, u32[]{:S(2)}) %copy-start.1) | copy-done | bytes 6291480
  24.6 5.7 %collective-permute-start = (bf16[2,8192]{1,0:T(2,128)(2,1)S(1)}, bf16[2,8192]{1,0:T(2,128)(2,1)S(1)}, u32[]{:S(2)}, u32[]{:S(2)}) collective-permute-start(bf16[2,8192]{1,0:T(2,128)(2,1)S(1)} %constant_dynamic-slice_fusion.1), channel_id=1, source_target_pairs={{0,1},{2,3},{4,5},{6,7},{8,9},{10,11},{12,13},{14,15},{16,17},{18,... | collective-permute-start | bytes 98312 | tf_op jit(solution)/shard_map/ppermute | solution.py:13
  31.7 1.4 multiply_exponential_fusion
  33.2 4.8 %gather_fusion = f32[1024,512]{1,0:T(8,128)} fusion(f32[32,512]{1,0:T(8,128)S(1)} %get-tuple-element.9, s32[1024]{0:T(1024)S(1)} %broadcast_clamp_fusion), kind=kCustom, calls=%fused_computation | custom fusion | bytes 4198400 | tf_op jit(solution)/shard_map/gather | solution.py:27
  38.0 1.3 iota_compare_fusion
  41.2 1.0 fusion.26
  42.4 1.8 broadcast_select_fusion
  45.5 2.6 %copy.18 = f32[32,32,512]{2,1,0:T(8,128)} copy(f32[32,32,512]{2,0,1:T(8,128)S(1)} %broadcast_select_fusion) | data formatting | bytes 4194304 | tf_op jit(solution)/shard_map/jit(_where)/select_n | solution.py:27
  48.2 0.7 fusion.31
  49.5 132.3 %all-gather.2.cloned.1.call-done = bf16[8192,2048]{1,0:T(8,128)(2,1)} async-done(((bf16[512,2048]{1,0:T(8,128)(2,1)}), bf16[8192,2048]{1,0:T(8,128)(2,1)}) %all-gather.2.cloned.1.call-update) | async-done | bytes 33554448 | tf_op jit(solution)/shard_map/all_gather | solution.py:96
  181.8 16.7 %fusion.13 = f32[386,1536]{1,0:T(8,128)S(1)} fusion(bf16[8192,2048]{1,0:T(8,128)(2,1)} %all-gather.2.cloned.1.call-done, bf16[384,8192]{1,0:T(8,128)(2,1)} %copy-done.1, bf16[2,8192]{1,0:T(2,128)(2,1)} %copy-done.12), kind=kOutput, calls=%fused_computation.21 | convolution fusion | flops 9727249408 | bytes 33861632 | tf_op jit(solution)/shard_map/dot_general | solution.py:100
  198.6 1.6 fusion.18
  200.3 1.1 multiply_reduce_fusion.2
  201.4 1.3 multiply_reduce_fusion.3
  202.8 3.6 %collective-permute-start.1 = (f32[16,512]{1,0:T(8,128)S(1)}, f32[16,512]{1,0:T(8,128)S(1)}, u32[]{:S(2)}, u32[]{:S(2)}) collective-permute-start(f32[16,512]{1,0:T(8,128)S(1)} %fusion.27), channel_id=1, source_target_pairs={{0,1},{2,3},{4,5},{6,7},{8,9},{10,11},{12,13},{14,15},{16,17},{18,... | collective-permute-start | bytes 98312 | tf_op jit(solution)/shard_map/ppermute | solution.py:13
  206.4 2.4 %multiply_reduce_fusion = f32[12,32,512]{2,1,0:T(8,128)S(1)} fusion(f32[12,32,512]{2,1,0:T(8,128)S(1)} %bitcast.36, f32[32,32,512]{2,1,0:T(8,128)S(1)} %copy-done), kind=kLoop, calls=%fused_computation.3 | loop fusion | flops 12386304 | bytes 3670016 | tf_op jit(solution)/shard_map/reduce_sum | solution.py:53
  208.9 0.7 select_multiply_fusion
  209.8 1.0 multiply_reduce_fusion.1
  211.2 11.9 %fusion.8 = bf16[1,1,384,8192]{3,2,1,0:T(8,128)(2,1)} fusion(bf16[384,512]{1,0:T(8,128)(2,1)S(1)} %fusion.22, bf16[8192,2048]{1,0:T(8,128)(2,1)} %all-gather.2.cloned.1.call-done, bf16[1,1,384,8192]{3,2,1,0:T(8,128)(2,1)} %param.12, f32[8192]{0:T(1024)S(1)} %fusion.29, pred[384]{0:T(512)(128)(4,1)S(1)} %copy-done.9), kind=kOutput, calls=%fused_computation.15 | convolution fusion | flops 3236954112 | bytes 21397888 | tf_op jit(solution)/shard_map/dot_general | solution.py:123
  (55 shorter events, 4.4 us)
Async XLA Ops:
  6.5 4.4 %copy-start.13 = (s32[1,2]{1,0:T(1,128)S(1)}, s32[1,2]{1,0:T(1,128)}, u32[]{:S(2)}) copy-start(s32[1,2]{1,0:T(1,128)} %param.13) | copy-start | bytes 28
  6.5 175.3 %all-gather.2.cloned.1.call-start = ((), (), s32[]{:S(2)}) async-start(), calls=%async_computation | async-start | bytes 35651584 | tf_op jit(solution)/shard_map/all_gather | solution.py:96
  7.8 9.3 %copy-start.5 = (f32[8192]{0:T(1024)S(1)}, f32[8192]{0:T(1024)}, u32[]{:S(2)}) copy-start(f32[8192]{0:T(1024)} %param.14) | copy-start | bytes 98308
  17.1 13.2 %copy-start.3 = (f32[16,512]{1,0:T(8,128)S(1)}, f32[16,512]{1,0:T(8,128)}, u32[]{:S(2)}) copy-start(f32[16,512]{1,0:T(8,128)} %param.17) | copy-start | bytes 98308
  17.1 14.6 %copy-start.4 = (f32[16,512]{1,0:T(8,128)S(1)}, f32[16,512]{1,0:T(8,128)}, u32[]{:S(2)}) copy-start(f32[16,512]{1,0:T(8,128)} %param.18) | copy-start | bytes 98308
  21.8 2.7 %copy-start.1 = (bf16[384,8192]{1,0:T(8,128)(2,1)}, bf16[384,8192]{1,0:T(8,128)(2,1)S(1)}, u32[]{:S(2)}) copy-start(bf16[384,8192]{1,0:T(8,128)(2,1)S(1)} %fusion.4) | copy-start | bytes 18874372
  24.6 24.3 %collective-permute-start = (bf16[2,8192]{1,0:T(2,128)(2,1)S(1)}, bf16[2,8192]{1,0:T(2,128)(2,1)S(1)}, u32[]{:S(2)}, u32[]{:S(2)}) collective-permute-start(bf16[2,8192]{1,0:T(2,128)(2,1)S(1)} %constant_dynamic-slice_fusion.1), channel_id=1, source_target_pairs={{0,1},{2,3},{4,5},{6,7},{8,9},{10,11},{12,13},{14,15},{16,17},{18,... | collective-permute-start | bytes 98312 | tf_op jit(solution)/shard_map/ppermute | solution.py:13
  33.2 7.3 %copy-start.6 = (f32[3,1536]{1,0:T(4,128)S(1)}, f32[3,1536]{1,0:T(4,128)}, u32[]{:S(2)}) copy-start(f32[3,1536]{1,0:T(4,128)} %param.16) | copy-start | bytes 55300
  48.9 0.6 copy-start.12
  198.5 1.6 copy-start.9
  198.6 1.8 copy-start.2
  198.6 2.9 %copy-start.7 = (f32[12,12]{1,0:T(8,128)S(1)}, f32[12,12]{1,0:T(8,128)}, u32[]{:S(2)}) copy-start(f32[12,12]{1,0:T(8,128)} %maximum_multiply_fusion) | copy-start | bytes 1732
  198.6 2.9 %copy-start.10 = (pred[12,12]{1,0:T(8,128)(4,1)S(1)}, pred[12,12]{1,0:T(8,128)(4,1)}, u32[]{:S(2)}) copy-start(pred[12,12]{1,0:T(8,128)(4,1)} %convert_compare_fusion) | copy-start | bytes 436
  198.6 7.8 %copy-start = (f32[32,32,512]{2,1,0:T(8,128)S(1)}, f32[32,32,512]{2,1,0:T(8,128)}, u32[]{:S(2)}) copy-start(f32[32,32,512]{2,1,0:T(8,128)} %copy.18) | copy-start | bytes 6291460
  200.2 9.4 %copy-start.11 = (f32[12]{0:T(128)S(1)}, f32[12]{0:T(128)}, u32[]{:S(2)}) copy-start(f32[12]{0:T(128)} %multiply_convert_fusion) | copy-start | bytes 148
  201.4 9.5 %copy-start.8 = (f32[512]{0:T(512)S(1)}, f32[512]{0:T(512)}, u32[]{:S(2)}) copy-start(f32[512]{0:T(512)} %param.19) | copy-start | bytes 6148
  202.8 6.1 %collective-permute-start.1 = (f32[16,512]{1,0:T(8,128)S(1)}, f32[16,512]{1,0:T(8,128)S(1)}, u32[]{:S(2)}, u32[]{:S(2)}) collective-permute-start(f32[16,512]{1,0:T(8,128)S(1)} %fusion.27), channel_id=1, source_target_pairs={{0,1},{2,3},{4,5},{6,7},{8,9},{10,11},{12,13},{14,15},{16,17},{18,... | collective-permute-start | bytes 98312 | tf_op jit(solution)/shard_map/ppermute | solution.py:13
Sparse Core Ops, SparseCore 0:
  11.0 170.7 all-gather.1

commit v5 on v4

--- a/solution.py
+++ b/solution.py
@@ -31,19 +31,20 @@
     return toeplitz, lead, close
 
 
-def block_states(drive, decay_rate, close, block):
+def block_ends(drive, close, block):
     cap, width = drive.shape
-    count = cap // block
-    pieces = drive.reshape(count, block, width)
-    ends = jnp.sum(close[None] * pieces[:, :, None, :], axis=1)
+    pieces = drive.reshape(cap // block, block, width)
+    return jnp.sum(close[None] * pieces[:, :, None, :], axis=1)
+
+
+def block_powers(decay_rate, count, block):
     steps = jnp.arange(count)
     gap = (steps[:, None] - steps[None, :]).astype(jnp.float32)
-    powers = jnp.where(
+    return jnp.where(
         (gap >= 0)[:, :, None, None],
         jnp.exp(-decay_rate[None, None] * (block * jnp.maximum(gap, 0.0))[:, :, None, None]),
         0.0,
     )
-    return jnp.sum(powers * ends[None], axis=1)
 
 
 def block_outputs(drive, states, incoming, decay_rate, toeplitz, lead, block):
@@ -87,6 +88,7 @@
 
     block = BLOCK if cap % BLOCK == 0 else cap
     toeplitz, lead, close = filter_tables(decay_rate, residue, block)
+    powers = block_powers(decay_rate, cap // block, block)
 
     lens_f = group_lens.astype(jnp.float32)
     cumlen = jnp.cumsum(lens_f)
@@ -97,8 +99,8 @@
     w_in_all = gathered[:, : 3 * slab]
     w_out_t = gathered[:, 3 * slab :]
     rows_ext = jnp.concatenate([tail_normed, normed], axis=0)
-    extended = jnp.dot(rows_ext, w_in_all, preferred_element_type=jnp.float32)
-    extended = lax.reduce_precision(extended, exponent_bits=8, mantissa_bits=7)
+    proj = jnp.dot(rows_ext, w_in_all, preferred_element_type=jnp.float32).astype(jnp.bfloat16)
+    extended = lax.optimization_barrier(proj).astype(jnp.float32)
     feat = (
         short_filter[0] * extended[2:]
         + short_filter[1] * extended[1:-1]
@@ -106,8 +108,8 @@
     )
     gate = feat[:, :slab]
     drive = jnp.where(live[:, None], feat[:, slab : 2 * slab] * feat[:, 2 * slab :], 0.0)
-    states = block_states(drive, decay_rate, close, block)
-    ending = states[-1] * rescale
+    ends = block_ends(drive, close, block)
+    ending = jnp.sum(powers[-1] * ends, axis=0) * rescale
     incoming = jnp.zeros_like(ending)
     for k in range(1, groups):
         got = from_behind(ending, "ctx", k)
@@ -117,6 +119,7 @@
         ) - lax.dynamic_index_in_dim(cumlen, jnp.maximum(source, 0), 0, keepdims=False)
         weight = jnp.where(source >= 0, jnp.exp(-decay_rate * between), 0.0)
         incoming = incoming + weight * got
+    states = jnp.sum(powers * ends[None], axis=1)
     local = block_outputs(drive, states, incoming, decay_rate, toeplitz, lead, block)
     filtered = local + skip_gain[None, :] * drive
     gated = jnp.where(live[:, None], gate * filtered, 0.0).astype(jnp.bfloat16)

time: 230 us -> 232 us (level)
  waiting for transfers between devices: 132 us -> 137 us
    all_gather x1, waiting for transfers between devices: 132 us -> 137 us  [per_device(): gathered = lax.all_gather(piece, 'dp', axis=0, tiled=True)]
  transfers between devices with their start and end apart: 3 -> 3, of which waited for: 1 -> 1; matrix products, arithmetic and copies ran while one was open for 12% -> 10% of each run, Pallas kernels for 0% -> 0%
where the time goes in v5:
time: 232 us
  waiting for transfers between devices  137 us (59%)
  matrix products  29.5 us (13%)
  other arithmetic  26.9 us (12%)
  between operations  17.1 us (7%)
  local copies, waits for them, and re-layouts  11.6 us (5%)
  starting transfers between devices  9.25 us (4%)
    all_gather x1, waiting for transfers between devices, per_device(): gathered = lax.all_gather(piece, 'dp', axis=0, tiled=True)  137 us
    dot_general x1, matrix products, per_device(): jnp.dot(rows_ext, w_in_all, preferred_element_type=jnp.float32)  17.6 us
    dot_general x1, matrix products, per_device(): lax.dot_general(gated, w_out_t, (((1,), (1,)), ((), ())), preferred_eleme...  12 us
    ppermute x2, starting transfers between devices, from_behind(): lax.ppermute(value, axis, [(source, source + steps) for source in range(f...  9.25 us
    convert_element_type x1, other arithmetic, normalize(): return (values * scale * gain[None, :]).astype(jnp.bfloat16)  4.73 us
  transfers between devices with their start and end apart: 3, of which 1 were waited for; matrix products, arithmetic and copies ran while one was open for 10% of the time, Pallas kernels for 0%

profile of v5, /device:TPU:0, one launch (start us, length us, event | category | flops | bytes accessed | tf_op | source)
XLA Modules:
  0.0 231.6 jit_solution(9375103064135189318)
XLA Ops:
  6.5 1.3 copy.17
  7.8 3.0 %pad_maximum_fusion = bf16[512,2048]{1,0:T(8,128)(2,1)} fusion(bf16[512,512]{1,0:T(8,128)(2,1)S(1)} %copy.17, bf16[512,1536]{1,0:T(8,128)(2,1)} %param.15), kind=kLoop, calls=%fused_computation.28 | loop fusion | flops 4194304 | bytes 4194304 | tf_op jit(solution)/shard_map/concatenate | solution.py:97
  10.9 0.7 constant_dynamic-slice_fusion.2
  12.9 4.1 %fusion.2 = f32[384]{0:T(512)S(1)} fusion(bf16[1,1,384,8192]{3,2,1,0:T(8,128)(2,1)} %param.12), kind=kLoop, calls=%fused_computation.7 | loop fusion | flops 9436800 | bytes 6292992 | tf_op jit(solution)/shard_map/reduce_sum | solution.py:18
  17.1 4.7 %fusion.4 = bf16[384,8192]{1,0:T(8,128)(2,1)S(1)} fusion(bf16[1,1,384,8192]{3,2,1,0:T(8,128)(2,1)} %param.12, f32[8192]{0:T(1024)S(1)} %copy-done.4, f32[384]{0:T(512)S(1)} %add_rsqrt_fusion), kind=kLoop, calls=%fused_computation.9 | loop fusion | flops 12582912 | bytes 12617216 | tf_op jit(solution)/shard_map/convert_element_type | solution.py:19
  21.8 2.7 %copy-done = bf16[384,8192]{1,0:T(8,128)(2,1)} copy-done((bf16[384,8192]{1,0:T(8,128)(2,1)}, bf16[384,8192]{1,0:T(8,128)(2,1)S(1)}, u32[]{:S(2)}) %copy-start) | copy-done | bytes 6291480
  24.6 5.7 %collective-permute-start = (bf16[2,8192]{1,0:T(2,128)(2,1)S(1)}, bf16[2,8192]{1,0:T(2,128)(2,1)S(1)}, u32[]{:S(2)}, u32[]{:S(2)}) collective-permute-start(bf16[2,8192]{1,0:T(2,128)(2,1)S(1)} %constant_dynamic-slice_fusion.1), channel_id=1, source_target_pairs={{0,1},{2,3},{4,5},{6,7},{8,9},{10,11},{12,13},{14,15},{16,17},{18,... | collective-permute-start | bytes 98312 | tf_op jit(solution)/shard_map/ppermute | solution.py:13
  31.7 1.4 multiply_exponential_fusion
  33.1 3.5 %gather_fusion = f32[1024,512]{1,0:T(8,128)S(1)} fusion(f32[32,512]{1,0:T(8,128)S(1)} %get-tuple-element.11, s32[1024]{0:T(1024)S(1)} %broadcast_clamp_fusion), kind=kCustom, calls=%fused_computation | custom fusion | bytes 4198400 | tf_op jit(solution)/shard_map/gather | solution.py:27
  36.7 0.7 iota_compare_fusion
  37.5 1.0 fusion.28
  38.7 1.6 broadcast_select_fusion
  41.0 2.9 %copy.18 = f32[32,32,512]{2,1,0:T(8,128)S(1)} copy(f32[32,32,512]{2,0,1:T(8,128)} %broadcast_select_fusion) | data formatting | bytes 4194304 | tf_op jit(solution)/shard_map/jit(_where)/select_n | solution.py:27
  44.0 0.6 fusion.32
  44.6 137.1 %all-gather.2.cloned.1.call-done = bf16[8192,2048]{1,0:T(8,128)(2,1)} async-done(((bf16[512,2048]{1,0:T(8,128)(2,1)}), bf16[8192,2048]{1,0:T(8,128)(2,1)}) %all-gather.2.cloned.1.call-update) | async-done | bytes 33554448 | tf_op jit(solution)/shard_map/all_gather | solution.py:98
  181.8 17.6 %fusion.13 = bf16[386,1536]{1,0:T(8,128)(2,1)} fusion(bf16[8192,2048]{1,0:T(8,128)(2,1)} %all-gather.2.cloned.1.call-done, bf16[384,8192]{1,0:T(8,128)(2,1)} %copy-done, bf16[2,8192]{1,0:T(2,128)(2,1)S(1)} %collective-permute-done), kind=kOutput, calls=%fused_computation.22 | convolution fusion | flops 9727249408 | bytes 32675840 | tf_op jit(solution)/shard_map/dot_general | solution.py:102
  199.4 1.6 convert_element_type.79
  201.0 0.7 fusion.18
  202.2 1.1 multiply_reduce_fusion.2
  203.2 1.2 exponential_select_fusion
  204.6 3.6 %collective-permute-start.1 = (f32[16,512]{1,0:T(8,128)S(1)}, f32[16,512]{1,0:T(8,128)S(1)}, u32[]{:S(2)}, u32[]{:S(2)}) collective-permute-start(f32[16,512]{1,0:T(8,128)S(1)} %exponential_multiply_fusion.1), channel_id=1, source_target_pairs={{0,1},{2,3},{4,5},{6,7},{8,9},{10,11},{12,13},{14,15},{16,17},{18,... | collective-permute-start | bytes 98312 | tf_op jit(solution)/shard_map/ppermute | solution.py:13
  208.2 2.4 %multiply_reduce_fusion = f32[12,32,512]{2,1,0:T(8,128)S(1)} fusion(f32[12,32,512]{2,1,0:T(8,128)S(1)} %bitcast.38, f32[32,32,512]{2,1,0:T(8,128)S(1)} %copy.18), kind=kLoop, calls=%fused_computation.3 | loop fusion | flops 12386304 | bytes 3670016 | tf_op jit(solution)/shard_map/reduce_sum | solution.py:54
  211.4 1.0 multiply_reduce_fusion.1
  212.8 12.0 %fusion.8 = bf16[1,1,384,8192]{3,2,1,0:T(8,128)(2,1)} fusion(bf16[384,512]{1,0:T(8,128)(2,1)S(1)} %fusion.22, bf16[8192,2048]{1,0:T(8,128)(2,1)} %all-gather.2.cloned.1.call-done, bf16[1,1,384,8192]{3,2,1,0:T(8,128)(2,1)} %param.12, f32[8192]{0:T(1024)S(1)} %fusion.30, pred[384]{0:T(512)(128)(4,1)S(1)} %iota_compare_fusion), kind=kOutput, calls=%fused_computation.15 | convolution fusion | flops 3236954112 | bytes 21397888 | tf_op jit(solution)/shard_map/dot_general | solution.py:126
  (45 shorter events, 2.4 us)
Async XLA Ops:
  6.5 4.3 %copy-start.7 = (s32[1,2]{1,0:T(1,128)S(1)}, s32[1,2]{1,0:T(1,128)}, u32[]{:S(2)}) copy-start(s32[1,2]{1,0:T(1,128)} %param.13) | copy-start | bytes 28
  6.5 175.2 %all-gather.2.cloned.1.call-start = ((), (), s32[]{:S(2)}) async-start(), calls=%async_computation | async-start | bytes 35651584 | tf_op jit(solution)/shard_map/all_gather | solution.py:98
  10.8 6.2 %copy-start.4 = (f32[8192]{0:T(1024)S(1)}, f32[8192]{0:T(1024)}, u32[]{:S(2)}) copy-start(f32[8192]{0:T(1024)} %param.14) | copy-start | bytes 98308
  17.1 13.2 %copy-start.2 = (f32[16,512]{1,0:T(8,128)S(1)}, f32[16,512]{1,0:T(8,128)}, u32[]{:S(2)}) copy-start(f32[16,512]{1,0:T(8,128)} %param.17) | copy-start | bytes 98308
  17.1 14.6 %copy-start.3 = (f32[16,512]{1,0:T(8,128)S(1)}, f32[16,512]{1,0:T(8,128)}, u32[]{:S(2)}) copy-start(f32[16,512]{1,0:T(8,128)} %param.18) | copy-start | bytes 98308
  21.8 2.7 %copy-start = (bf16[384,8192]{1,0:T(8,128)(2,1)}, bf16[384,8192]{1,0:T(8,128)(2,1)S(1)}, u32[]{:S(2)}) copy-start(bf16[384,8192]{1,0:T(8,128)(2,1)S(1)} %fusion.4) | copy-start | bytes 18874372
  24.6 20.1 %collective-permute-start = (bf16[2,8192]{1,0:T(2,128)(2,1)S(1)}, bf16[2,8192]{1,0:T(2,128)(2,1)S(1)}, u32[]{:S(2)}, u32[]{:S(2)}) collective-permute-start(bf16[2,8192]{1,0:T(2,128)(2,1)S(1)} %constant_dynamic-slice_fusion.1), channel_id=1, source_target_pairs={{0,1},{2,3},{4,5},{6,7},{8,9},{10,11},{12,13},{14,15},{16,17},{18,... | collective-permute-start | bytes 98312 | tf_op jit(solution)/shard_map/ppermute | solution.py:13
  33.1 4.3 %copy-start.5 = (f32[3,1536]{1,0:T(4,128)S(1)}, f32[3,1536]{1,0:T(4,128)}, u32[]{:S(2)}) copy-start(f32[3,1536]{1,0:T(4,128)} %param.16) | copy-start | bytes 55300
  200.9 1.2 copy-start.1
  204.6 8.0 %copy-start.6 = (f32[512]{0:T(512)S(1)}, f32[512]{0:T(512)}, u32[]{:S(2)}) copy-start(f32[512]{0:T(512)} %param.19) | copy-start | bytes 6148
  204.6 6.0 %collective-permute-start.1 = (f32[16,512]{1,0:T(8,128)S(1)}, f32[16,512]{1,0:T(8,128)S(1)}, u32[]{:S(2)}, u32[]{:S(2)}) collective-permute-start(f32[16,512]{1,0:T(8,128)S(1)} %exponential_multiply_fusion.1), channel_id=1, source_target_pairs={{0,1},{2,3},{4,5},{6,7},{8,9},{10,11},{12,13},{14,15},{16,17},{18,... | collective-permute-start | bytes 98312 | tf_op jit(solution)/shard_map/ppermute | solution.py:13
Sparse Core Ops, SparseCore 0:
  11.0 170.7 all-gather.1

commit v6 on v4

--- a/solution.py
+++ b/solution.py
@@ -1,6 +1,7 @@
 import jax
 import jax.numpy as jnp
 from jax import lax
+from jax.experimental import pallas as pl
 from jax.sharding import PartitionSpec as P
 
 STEER_W = 1024
@@ -58,6 +59,31 @@
     return (inside + earlier).reshape(cap, width)
 
 
+def out_kernel(g_ref, w_ref, t_ref, s_ref, m_ref, o_ref):
+    acc = lax.dot_general(g_ref[...], w_ref[...], (((1,), (1,)), ((), ())), preferred_element_type=jnp.float32)
+    res = t_ref[...].astype(jnp.float32) + acc + s_ref[...]
+    o_ref[...] = jnp.where(m_ref[...] > 0, res, 0.0).astype(o_ref.dtype)
+
+def project_out(gated, gathered, rows_in, steer, live, tile=1024):
+    cap, slab = gated.shape
+    width = rows_in.shape[1]
+    column = (gathered.shape[1] - slab) // slab
+    return pl.pallas_call(
+        out_kernel,
+        grid=(width // tile,),
+        in_specs=[
+            pl.BlockSpec((cap, slab), lambda j: (0, 0)),
+            pl.BlockSpec((tile, slab), lambda j: (j, column)),
+            pl.BlockSpec((cap, tile), lambda j: (0, j)),
+            pl.BlockSpec((1, tile), lambda j: (0, j)),
+            pl.BlockSpec((cap, 1), lambda j: (0, 0)),
+        ],
+        out_specs=pl.BlockSpec((cap, tile), lambda j: (0, j)),
+        out_shape=jax.ShapeDtypeStruct((cap, width), rows_in.dtype),
+        cost_estimate=pl.CostEstimate(flops=2 * cap * slab * width, transcendentals=0,
+            bytes_accessed=2 * (cap * slab + width * slab + 2 * cap * width) + 4 * width),
+    )(gated, gathered, rows_in, steer.reshape(1, width), live.astype(jnp.int32).reshape(cap, 1))
+
 def per_device(
     tokens,
     lengths,
@@ -95,7 +121,6 @@
     piece = jnp.concatenate([w_in, w_out.T], axis=1)
     gathered = lax.all_gather(piece, "dp", axis=0, tiled=True)
     w_in_all = gathered[:, : 3 * slab]
-    w_out_t = gathered[:, 3 * slab :]
     rows_ext = jnp.concatenate([tail_normed, normed], axis=0)
     extended = jnp.dot(rows_ext, w_in_all, preferred_element_type=jnp.float32)
     extended = lax.reduce_precision(extended, exponent_bits=8, mantissa_bits=7)
@@ -120,16 +145,12 @@
     local = block_outputs(drive, states, incoming, decay_rate, toeplitz, lead, block)
     filtered = local + skip_gain[None, :] * drive
     gated = jnp.where(live[:, None], gate * filtered, 0.0).astype(jnp.bfloat16)
-    mixed = lax.dot_general(
-        gated, w_out_t, (((1,), (1,)), ((), ())), preferred_element_type=jnp.float32
-    )
     rows2 = lax.dynamic_index_in_dim(steer_table, steer_layer[0], 0, keepdims=False)
     shift_vec = rows2[0] - rows2[1]
     columns = jnp.arange(width) // STEER_W
     steer = jnp.where(columns == steer_slab[0], 2.0 * shift_vec, 0.0)
-    summed = rows_in.astype(jnp.float32) + mixed + steer[None, :]
-    summed = jnp.where(live[:, None], summed, 0.0)
-    return summed.astype(jnp.bfloat16).reshape(tokens.shape)
+    result = project_out(gated, gathered, rows_in, steer, live)
+    return result.reshape(tokens.shape)
 
 
 def solution(mesh):

time: 230 us -> 231 us (level)
  Pallas kernels: 0 us -> 12.2 us
  matrix products: 28.7 us -> 16.7 us
    pallas_call x0 -> x1, Pallas kernels: none -> 12.2 us  [project_out(): pl.pallas_call(out_kernel, grid=(width // tile,), in_specs=[pl.BlockSpec(...]
    dot_general x1 -> x0, matrix products: 11.9 us -> none  [per_device(): lax.dot_general(gated, w_out_t, (((1,), (1,)), ((), ())), preferred_eleme...]
    unnamed x28 -> x27, local copies, waits for them, and re-layouts: 3.36 us -> 4.96 us
  transfers between devices with their start and end apart: 3 -> 3, of which waited for: 1 -> 1; matrix products, arithmetic and copies ran while one was open for 12% -> 13% of each run, Pallas kernels for 0% -> 0%
where the time goes in v6:
time: 231 us; the launch traced here: 230 us
  waiting for transfers between devices  133 us (58%)
  other arithmetic  29.8 us (13%)
  between operations  16.8 us (7%)
  matrix products  16.7 us (7%)
  local copies, waits for them, and re-layouts  13.2 us (6%)
  Pallas kernels  12.2 us (5%)
  starting transfers between devices  8.94 us (4%)
    all_gather x1, waiting for transfers between devices, per_device(): gathered = lax.all_gather(piece, 'dp', axis=0, tiled=True)  133 us
    dot_general x1, matrix products, per_device(): extended = jnp.dot(rows_ext, w_in_all, preferred_element_type=jnp.float32)  16.7 us
    pallas_call x1, Pallas kernels, project_out(): pl.pallas_call(out_kernel, grid=(width // tile,), in_specs=[pl.BlockSpec(...  12.2 us
    ppermute x2, starting transfers between devices, from_behind(): lax.ppermute(value, axis, [(source, source + steps) for source in range(f...  8.94 us
    unnamed x27, local copies, waits for them, and re-layouts  4.96 us
    gather x1, local copies, waits for them, and re-layouts, filter_tables(): taps[jnp.clip(diff, 0, block - 1)]  4.84 us
    convert_element_type x1, other arithmetic, normalize(): return (values * scale * gain[None, :]).astype(jnp.bfloat16)  4.73 us
  transfers between devices with their start and end apart: 3, of which 1 were waited for; matrix products, arithmetic and copies ran while one was open for 13% of the time, Pallas kernels for 0%

profile of v6, /device:TPU:0, one launch (start us, length us, event | category | flops | bytes accessed | tf_op | source)
XLA Modules:
  0.0 230.2 jit_solution(15597064554721969218)
XLA Ops:
  6.5 1.3 copy.17
  7.8 3.0 %pad_maximum_fusion = bf16[512,2048]{1,0:T(8,128)(2,1)} fusion(bf16[512,512]{1,0:T(8,128)(2,1)S(1)} %bitcast.35, bf16[512,1536]{1,0:T(8,128)(2,1)} %param.15), kind=kLoop, calls=%fused_computation.21 | loop fusion | flops 4194304 | bytes 4194304 | tf_op jit(solution)/shard_map/concatenate | solution.py:121
  12.6 4.1 %fusion.2 = f32[384]{0:T(512)S(1)} fusion(bf16[1,1,384,8192]{3,2,1,0:T(8,128)(2,1)} %param.12), kind=kLoop, calls=%fused_computation.6 | loop fusion | flops 9436800 | bytes 6292992 | tf_op jit(solution)/shard_map/reduce_sum | solution.py:19
  16.8 4.7 %fusion.4 = bf16[384,8192]{1,0:T(8,128)(2,1)S(1)} fusion(f32[8192]{0:T(1024)S(1)} %copy-done.5, f32[384]{0:T(512)S(1)} %add_rsqrt_fusion, bf16[1,1,384,8192]{3,2,1,0:T(8,128)(2,1)} %param.12), kind=kLoop, calls=%fused_computation.8 | loop fusion | flops 12582912 | bytes 12617216 | tf_op jit(solution)/shard_map/convert_element_type | solution.py:20
  21.5 2.7 %copy-done.1 = bf16[384,8192]{1,0:T(8,128)(2,1)} copy-done((bf16[384,8192]{1,0:T(8,128)(2,1)}, bf16[384,8192]{1,0:T(8,128)(2,1)S(1)}, u32[]{:S(2)}) %copy-start.1) | copy-done | bytes 6291480
  24.3 5.3 %collective-permute-start = (bf16[2,8192]{1,0:T(2,128)(2,1)S(1)}, bf16[2,8192]{1,0:T(2,128)(2,1)S(1)}, u32[]{:S(2)}, u32[]{:S(2)}) collective-permute-start(bf16[2,8192]{1,0:T(2,128)(2,1)S(1)} %constant_dynamic-slice_fusion.1), channel_id=1, source_target_pairs={{0,1},{2,3},{4,5},{6,7},{8,9},{10,11},{12,13},{14,15},{16,17},{18,... | collective-permute-start | bytes 98312 | tf_op jit(solution)/shard_map/ppermute | solution.py:14
  31.1 1.4 multiply_exponential_fusion
  32.5 4.8 %gather_fusion = f32[1024,512]{1,0:T(8,128)} fusion(f32[32,512]{1,0:T(8,128)S(1)} %get-tuple-element.9, s32[1024]{0:T(1024)S(1)} %broadcast_clamp_fusion), kind=kCustom, calls=%fused_computation | custom fusion | bytes 4198400 | tf_op jit(solution)/shard_map/gather | solution.py:28
  37.4 1.2 iota_compare_fusion.1
  39.2 1.3 fusion.18.m_ref
  40.7 1.9 broadcast_select_fusion
  42.6 1.6 compare_select_fusion.s_ref
  45.3 2.6 %copy.18 = f32[32,32,512]{2,1,0:T(8,128)} copy(f32[32,32,512]{2,0,1:T(8,128)S(1)} %broadcast_select_fusion) | data formatting | bytes 4194304 | tf_op jit(solution)/shard_map/jit(_where)/select_n | solution.py:28
  48.6 0.6 copy-done.11
  49.2 132.5 %all-gather.2.cloned.1.call-done.w_ref = bf16[8192,2048]{1,0:T(8,128)(2,1)} async-done(((bf16[512,2048]{1,0:T(8,128)(2,1)}), bf16[8192,2048]{1,0:T(8,128)(2,1)}) %all-gather.2.cloned.1.call-update) | async-done | bytes 33554448 | tf_op jit(solution)/shard_map/all_gather | solution.py:122
  181.8 16.7 %fusion.8 = f32[386,1536]{1,0:T(8,128)S(1)} fusion(bf16[8192,2048]{1,0:T(8,128)(2,1)} %all-gather.2.cloned.1.call-done.w_ref, bf16[384,8192]{1,0:T(8,128)(2,1)} %copy-done.1, bf16[2,8192]{1,0:T(2,128)(2,1)} %copy-done.11), kind=kOutput, calls=%fused_computation.15 | convolution fusion | flops 9727249408 | bytes 33861632 | tf_op jit(solution)/shard_map/dot_general | solution.py:125
  198.6 0.7 fusion.13
  199.8 1.1 multiply_reduce_fusion.2
  200.8 1.3 multiply_reduce_fusion.3
  202.2 3.6 %collective-permute-start.1 = (f32[16,512]{1,0:T(8,128)S(1)}, f32[16,512]{1,0:T(8,128)S(1)}, u32[]{:S(2)}, u32[]{:S(2)}) collective-permute-start(f32[16,512]{1,0:T(8,128)S(1)} %fusion.20), channel_id=1, source_target_pairs={{0,1},{2,3},{4,5},{6,7},{8,9},{10,11},{12,13},{14,15},{16,17},{18,... | collective-permute-start | bytes 98312 | tf_op jit(solution)/shard_map/ppermute | solution.py:14
  205.8 2.4 %multiply_reduce_fusion = f32[12,32,512]{2,1,0:T(8,128)S(1)} fusion(f32[12,32,512]{2,1,0:T(8,128)S(1)} %bitcast.34, f32[32,32,512]{2,1,0:T(8,128)S(1)} %copy-done), kind=kLoop, calls=%fused_computation.3 | loop fusion | flops 12386304 | bytes 3670016 | tf_op jit(solution)/shard_map/reduce_sum | solution.py:54
  209.0 1.0 multiply_reduce_fusion.1
  210.2 1.0 fusion.17.g_ref
  211.2 12.2 %shard_map.118 = bf16[384,8192]{1,0:T(8,128)(2,1)} custom-call(bf16[384,512]{1,0:T(8,128)(2,1)} %fusion.17.g_ref, bf16[8192,2048]{1,0:T(8,128)(2,1)} %all-gather.2.cloned.1.call-done.w_ref, bf16[384,8192]{1,0:T(8,128)(2,1)} %bitcast.31, f32[1,8192]{1,0:T(1,128)} %compare_select_fusion.s_ref, s32[384,1]{1,0:T(8,128)} %fusion.18.m_ref), custom_call_target="tpu_custom_call" | custom-call | flops 3221225472 | bytes 21397504 | tf_op jit(solution)/shard_map/pallas_call | solution.py:71
  (53 shorter events, 4.3 us)
Async XLA Ops:
  6.5 4.3 %copy-start.12 = (s32[1,2]{1,0:T(1,128)S(1)}, s32[1,2]{1,0:T(1,128)}, u32[]{:S(2)}) copy-start(s32[1,2]{1,0:T(1,128)} %param.13) | copy-start | bytes 28
  6.5 175.2 %all-gather.2.cloned.1.call-start = ((), (), s32[]{:S(2)}) async-start(), calls=%async_computation | async-start | bytes 35651584 | tf_op jit(solution)/shard_map/all_gather | solution.py:122
  10.8 5.9 %copy-start.5 = (f32[8192]{0:T(1024)S(1)}, f32[8192]{0:T(1024)}, u32[]{:S(2)}) copy-start(f32[8192]{0:T(1024)} %param.14) | copy-start | bytes 98308
  16.7 12.9 %copy-start.3 = (f32[16,512]{1,0:T(8,128)S(1)}, f32[16,512]{1,0:T(8,128)}, u32[]{:S(2)}) copy-start(f32[16,512]{1,0:T(8,128)} %param.17) | copy-start | bytes 98308
  16.8 14.3 %copy-start.4 = (f32[16,512]{1,0:T(8,128)S(1)}, f32[16,512]{1,0:T(8,128)}, u32[]{:S(2)}) copy-start(f32[16,512]{1,0:T(8,128)} %param.18) | copy-start | bytes 98308
  21.5 2.7 %copy-start.1 = (bf16[384,8192]{1,0:T(8,128)(2,1)}, bf16[384,8192]{1,0:T(8,128)(2,1)S(1)}, u32[]{:S(2)}) copy-start(bf16[384,8192]{1,0:T(8,128)(2,1)S(1)} %fusion.4) | copy-start | bytes 18874372
  24.3 24.3 %collective-permute-start = (bf16[2,8192]{1,0:T(2,128)(2,1)S(1)}, bf16[2,8192]{1,0:T(2,128)(2,1)S(1)}, u32[]{:S(2)}, u32[]{:S(2)}) collective-permute-start(bf16[2,8192]{1,0:T(2,128)(2,1)S(1)} %constant_dynamic-slice_fusion.1), channel_id=1, source_target_pairs={{0,1},{2,3},{4,5},{6,7},{8,9},{10,11},{12,13},{14,15},{16,17},{18,... | collective-permute-start | bytes 98312 | tf_op jit(solution)/shard_map/ppermute | solution.py:14
  32.5 6.6 %copy-start.6 = (f32[3,1536]{1,0:T(4,128)S(1)}, f32[3,1536]{1,0:T(4,128)}, u32[]{:S(2)}) copy-start(f32[3,1536]{1,0:T(4,128)} %param.16) | copy-start | bytes 55300
  48.6 0.6 copy-start.11
  198.5 0.7 copy-start.8
  198.5 1.2 copy-start.2
  198.5 2.3 copy-start.9
  199.3 6.6 %copy-start = (f32[32,32,512]{2,1,0:T(8,128)S(1)}, f32[32,32,512]{2,1,0:T(8,128)}, u32[]{:S(2)}) copy-start(f32[32,32,512]{2,1,0:T(8,128)} %copy.18) | copy-start | bytes 6291460
  199.4 9.5 %copy-start.10 = (f32[12]{0:T(128)S(1)}, f32[12]{0:T(128)}, u32[]{:S(2)}) copy-start(f32[12]{0:T(128)} %multiply_convert_fusion) | copy-start | bytes 148
  202.2 8.0 %copy-start.7 = (f32[512]{0:T(512)S(1)}, f32[512]{0:T(512)}, u32[]{:S(2)}) copy-start(f32[512]{0:T(512)} %param.19) | copy-start | bytes 6148
  202.2 6.1 %collective-permute-start.1 = (f32[16,512]{1,0:T(8,128)S(1)}, f32[16,512]{1,0:T(8,128)S(1)}, u32[]{:S(2)}, u32[]{:S(2)}) collective-permute-start(f32[16,512]{1,0:T(8,128)S(1)} %fusion.20), channel_id=1, source_target_pairs={{0,1},{2,3},{4,5},{6,7},{8,9},{10,11},{12,13},{14,15},{16,17},{18,... | collective-permute-start | bytes 98312 | tf_op jit(solution)/shard_map/ppermute | solution.py:14
Sparse Core Ops, SparseCore 0:
  11.0 170.7 all-gather.1

commit v7 on v6

--- a/solution.py
+++ b/solution.py
@@ -60,11 +60,12 @@
 
 
 def out_kernel(g_ref, w_ref, t_ref, s_ref, m_ref, o_ref):
-    acc = lax.dot_general(g_ref[...], w_ref[...], (((1,), (1,)), ((), ())), preferred_element_type=jnp.float32)
-    res = t_ref[...].astype(jnp.float32) + acc + s_ref[...]
+    flipped = jnp.dot(w_ref[...], g_ref[...], preferred_element_type=jnp.float32)
+    res = t_ref[...].astype(jnp.float32) + flipped.T + s_ref[...]
     o_ref[...] = jnp.where(m_ref[...] > 0, res, 0.0).astype(o_ref.dtype)
 
-def project_out(gated, gathered, rows_in, steer, live, tile=1024):
+
+def project_out(gated, gathered, rows_in, steer, live, tile=512):
     cap, slab = gated.shape
     width = rows_in.shape[1]
     column = (gathered.shape[1] - slab) // slab
@@ -72,7 +73,7 @@
         out_kernel,
         grid=(width // tile,),
         in_specs=[
-            pl.BlockSpec((cap, slab), lambda j: (0, 0)),
+            pl.BlockSpec((slab, cap), lambda j: (0, 0)),
             pl.BlockSpec((tile, slab), lambda j: (j, column)),
             pl.BlockSpec((cap, tile), lambda j: (0, j)),
             pl.BlockSpec((1, tile), lambda j: (0, j)),
@@ -80,9 +81,12 @@
         ],
         out_specs=pl.BlockSpec((cap, tile), lambda j: (0, j)),
         out_shape=jax.ShapeDtypeStruct((cap, width), rows_in.dtype),
-        cost_estimate=pl.CostEstimate(flops=2 * cap * slab * width, transcendentals=0,
-            bytes_accessed=2 * (cap * slab + width * slab + 2 * cap * width) + 4 * width),
-    )(gated, gathered, rows_in, steer.reshape(1, width), live.astype(jnp.int32).reshape(cap, 1))
+        cost_estimate=pl.CostEstimate(
+            flops=2 * cap * slab * width,
+            transcendentals=0,
+            bytes_accessed=2 * (cap * slab + width * slab + 2 * cap * width) + 4 * width,
+        ),
+    )(gated.T, gathered, rows_in, steer.reshape(1, width), live.astype(jnp.int32).reshape(cap, 1))
 
 def per_device(
     tokens,

time: 231 us -> 250 us (1.082)
  other arithmetic: 29.8 us -> 36.9 us
  Pallas kernels: 12.2 us -> 17.4 us
  matrix products: 16.7 us -> 20 us
    pallas_call x1, Pallas kernels: 12.2 us -> 17.4 us  [project_out(): pl.pallas_call(out_kernel, grid=(width // tile,), in_specs=[pl.BlockSpec(...]
    add x1, other arithmetic: 0.69 us -> 5.02 us  [per_device(): short_filter[0] * extended[2:] + short_filter[1] * extended[1:-1]]
    dot_general x1, matrix products: 16.7 us -> 20 us  [per_device(): extended = jnp.dot(rows_ext, w_in_all, preferred_element_type=jnp.float32)]
  transfers between devices with their start and end apart: 3 -> 3, of which waited for: 1 -> 1; matrix products, arithmetic and copies ran while one was open for 13% -> 11% of each run, Pallas kernels for 0% -> 0%
where the time goes in v7:
time: 250 us; the launch traced here: 249 us
  waiting for transfers between devices  133 us (53%)
  other arithmetic  36.9 us (15%)
  matrix products  20 us (8%)
  Pallas kernels  17.4 us (7%)
  between operations  16.9 us (7%)
  local copies, waits for them, and re-layouts  15 us (6%)
  starting transfers between devices  9.06 us (4%)
    all_gather x1, waiting for transfers between devices, per_device(): gathered = lax.all_gather(piece, 'dp', axis=0, tiled=True)  133 us
    dot_general x1, matrix products, per_device(): extended = jnp.dot(rows_ext, w_in_all, preferred_element_type=jnp.float32)  20 us
    pallas_call x1, Pallas kernels, project_out(): pl.pallas_call(out_kernel, grid=(width // tile,), in_specs=[pl.BlockSpec(...  17.4 us
    ppermute x2, starting transfers between devices, from_behind(): lax.ppermute(value, axis, [(source, source + steps) for source in range(f...  9.05 us
    add x1, other arithmetic, per_device(): short_filter[0] * extended[2:] + short_filter[1] * extended[1:-1]  5.02 us
  transfers between devices with their start and end apart: 3, of which 1 were waited for; matrix products, arithmetic and copies ran while one was open for 11% of the time, Pallas kernels for 0%

profile of v7, /device:TPU:0, one launch (start us, length us, event | category | flops | bytes accessed | tf_op | source)
XLA Modules:
  0.0 248.7 jit_solution(18258174108509243132)
XLA Ops:
  6.5 1.3 copy.23
  7.8 3.0 %pad_maximum_fusion = bf16[512,2048]{1,0:T(8,128)(2,1)} fusion(bf16[512,512]{1,0:T(8,128)(2,1)S(1)} %bitcast.35, bf16[512,1536]{1,0:T(8,128)(2,1)} %param.15), kind=kLoop, calls=%fused_computation.21 | loop fusion | flops 4194304 | bytes 4194304 | tf_op jit(solution)/shard_map/concatenate | solution.py:125
  12.7 4.1 %fusion.2 = f32[384]{0:T(512)S(1)} fusion(bf16[1,1,384,8192]{3,2,1,0:T(8,128)(2,1)} %param.12), kind=kLoop, calls=%fused_computation.6 | loop fusion | flops 9436800 | bytes 6292992 | tf_op jit(solution)/shard_map/reduce_sum | solution.py:19
  16.9 4.7 %fusion.4 = bf16[384,8192]{1,0:T(8,128)(2,1)S(1)} fusion(f32[8192]{0:T(1024)S(1)} %copy-done.5, f32[384]{0:T(512)S(1)} %add_rsqrt_fusion, bf16[1,1,384,8192]{3,2,1,0:T(8,128)(2,1)} %param.12), kind=kLoop, calls=%fused_computation.8 | loop fusion | flops 12582912 | bytes 12617216 | tf_op jit(solution)/shard_map/convert_element_type | solution.py:20
  21.6 2.7 %copy-done.1 = bf16[384,8192]{1,0:T(8,128)(2,1)} copy-done((bf16[384,8192]{1,0:T(8,128)(2,1)}, bf16[384,8192]{1,0:T(8,128)(2,1)S(1)}, u32[]{:S(2)}) %copy-start.1) | copy-done | bytes 6291480
  24.4 5.5 %collective-permute-start = (bf16[2,8192]{1,0:T(2,128)(2,1)S(1)}, bf16[2,8192]{1,0:T(2,128)(2,1)S(1)}, u32[]{:S(2)}, u32[]{:S(2)}) collective-permute-start(bf16[2,8192]{1,0:T(2,128)(2,1)S(1)} %constant_dynamic-slice_fusion.1), channel_id=1, source_target_pairs={{0,1},{2,3},{4,5},{6,7},{8,9},{10,11},{12,13},{14,15},{16,17},{18,... | collective-permute-start | bytes 98312 | tf_op jit(solution)/shard_map/ppermute | solution.py:14
  31.3 1.4 multiply_exponential_fusion
  32.7 4.8 %gather_fusion = f32[1024,512]{1,0:T(8,128)} fusion(f32[32,512]{1,0:T(8,128)S(1)} %get-tuple-element.9, s32[1024]{0:T(1024)S(1)} %broadcast_clamp_fusion), kind=kCustom, calls=%fused_computation | custom fusion | bytes 4198400 | tf_op jit(solution)/shard_map/gather | solution.py:28
  38.3 1.3 fusion.19.m_ref
  39.6 1.2 exponential_multiply_fusion
  40.9 1.9 broadcast_select_fusion
  42.7 1.6 compare_select_fusion.s_ref
  44.9 2.6 %copy.25 = f32[32,32,512]{2,1,0:T(8,128)} copy(f32[32,32,512]{2,0,1:T(8,128)S(1)} %broadcast_select_fusion) | data formatting | bytes 4194304 | tf_op jit(solution)/shard_map/jit(_where)/select_n | solution.py:28
  48.4 133.4 %all-gather.2.cloned.1.call-done.w_ref = bf16[8192,2048]{1,0:T(8,128)(2,1)} async-done(((bf16[512,2048]{1,0:T(8,128)(2,1)}), bf16[8192,2048]{1,0:T(8,128)(2,1)}) %all-gather.2.cloned.1.call-update) | async-done | bytes 33554448 | tf_op jit(solution)/shard_map/all_gather | solution.py:126
  181.8 20.0 %fusion.8 = f32[386,1536]{0,1:T(8,128)} fusion(bf16[8192,2048]{1,0:T(8,128)(2,1)} %all-gather.2.cloned.1.call-done.w_ref, bf16[384,8192]{1,0:T(8,128)(2,1)} %copy-done.1, bf16[2,8192]{1,0:T(2,128)(2,1)S(1)} %collective-permute-done), kind=kOutput, calls=%fused_computation.15 | convolution fusion | flops 9727249408 | bytes 33861632 | tf_op jit(solution)/shard_map/dot_general | solution.py:129
  201.8 5.0 %fusion.13 = f32[384,1536]{0,1:T(8,128)S(1)} fusion(f32[386,1536]{0,1:T(8,128)} %fusion.8, f32[1536]{0:T(1024)S(1)} %get-tuple-element.6, f32[1536]{0:T(1024)S(1)} %get-tuple-element.7, f32[1536]{0:T(1024)S(1)} %get-tuple-element.5), kind=kLoop, calls=%fused_computation.17 | loop fusion | flops 2949120 | bytes 9455616 | tf_op jit(solution)/shard_map/add | solution.py:132
  207.8 1.4 copy.26
  209.2 2.5 %multiply_reduce_fusion.2 = f32[12,16,512]{2,1,0:T(8,128)S(1)} fusion(f32[12,32,512]{2,1,0:T(8,128)S(1)} %bitcast.32, f32[32,16,512]{2,1,0:T(8,128)} %get-tuple-element.8), kind=kLoop, calls=%fused_computation.10 | loop fusion | flops 6193152 | bytes 2228224 | tf_op jit(solution)/shard_map/reduce_sum | solution.py:39
  211.7 1.3 multiply_reduce_fusion.3
  213.1 3.6 %collective-permute-start.1 = (f32[16,512]{1,0:T(8,128)S(1)}, f32[16,512]{1,0:T(8,128)S(1)}, u32[]{:S(2)}, u32[]{:S(2)}) collective-permute-start(f32[16,512]{1,0:T(8,128)S(1)} %fusion.21), channel_id=1, source_target_pairs={{0,1},{2,3},{4,5},{6,7},{8,9},{10,11},{12,13},{14,15},{16,17},{18,... | collective-permute-start | bytes 98312 | tf_op jit(solution)/shard_map/ppermute | solution.py:14
  216.7 2.4 multiply_reduce_fusion
  220.0 1.0 multiply_reduce_fusion.1
  222.1 1.4 copy.27
  224.4 17.4 %shard_map.118 = bf16[384,8192]{1,0:T(8,128)(2,1)} custom-call(bf16[512,384]{1,0:T(8,128)(2,1)} %fusion.18.g_ref, bf16[8192,2048]{1,0:T(8,128)(2,1)} %all-gather.2.cloned.1.call-done.w_ref, bf16[384,8192]{1,0:T(8,128)(2,1)} %bitcast.30, f32[1,8192]{1,0:T(1,128)} %compare_select_fusion.s_ref, s32[384,1]{1,0:T(8,128)} %fusion.19.m_ref), custom_call_target="tpu_custom_call" | custom-call | flops 3221225472 | bytes 21397504 | tf_op jit(solution)/shard_map/pallas_call | solution.py:72
  (47 shorter events, 6.2 us)
Async XLA Ops:
  6.5 4.3 %copy-start.8 = (s32[1,2]{1,0:T(1,128)S(1)}, s32[1,2]{1,0:T(1,128)}, u32[]{:S(2)}) copy-start(s32[1,2]{1,0:T(1,128)} %param.13) | copy-start | bytes 28
  6.5 175.2 %all-gather.2.cloned.1.call-start = ((), (), s32[]{:S(2)}) async-start(), calls=%async_computation | async-start | bytes 35651584 | tf_op jit(solution)/shard_map/all_gather | solution.py:126
  10.8 6.0 %copy-start.5 = (f32[8192]{0:T(1024)S(1)}, f32[8192]{0:T(1024)}, u32[]{:S(2)}) copy-start(f32[8192]{0:T(1024)} %param.14) | copy-start | bytes 98308
  16.9 13.0 %copy-start.3 = (f32[16,512]{1,0:T(8,128)S(1)}, f32[16,512]{1,0:T(8,128)}, u32[]{:S(2)}) copy-start(f32[16,512]{1,0:T(8,128)} %param.17) | copy-start | bytes 98308
  16.9 14.4 %copy-start.4 = (f32[16,512]{1,0:T(8,128)S(1)}, f32[16,512]{1,0:T(8,128)}, u32[]{:S(2)}) copy-start(f32[16,512]{1,0:T(8,128)} %param.18) | copy-start | bytes 98308
  21.6 2.7 %copy-start.1 = (bf16[384,8192]{1,0:T(8,128)(2,1)}, bf16[384,8192]{1,0:T(8,128)(2,1)S(1)}, u32[]{:S(2)}) copy-start(bf16[384,8192]{1,0:T(8,128)(2,1)S(1)} %fusion.4) | copy-start | bytes 18874372
  24.4 24.0 %collective-permute-start = (bf16[2,8192]{1,0:T(2,128)(2,1)S(1)}, bf16[2,8192]{1,0:T(2,128)(2,1)S(1)}, u32[]{:S(2)}, u32[]{:S(2)}) collective-permute-start(bf16[2,8192]{1,0:T(2,128)(2,1)S(1)} %constant_dynamic-slice_fusion.1), channel_id=1, source_target_pairs={{0,1},{2,3},{4,5},{6,7},{8,9},{10,11},{12,13},{14,15},{16,17},{18,... | collective-permute-start | bytes 98312 | tf_op jit(solution)/shard_map/ppermute | solution.py:14
  32.7 5.5 %copy-start.6 = (f32[3,1536]{1,0:T(4,128)S(1)}, f32[3,1536]{1,0:T(4,128)}, u32[]{:S(2)}) copy-start(f32[3,1536]{1,0:T(4,128)} %param.16) | copy-start | bytes 55300
  209.2 7.5 %copy-start = (f32[32,32,512]{2,1,0:T(8,128)S(1)}, f32[32,32,512]{2,1,0:T(8,128)}, u32[]{:S(2)}) copy-start(f32[32,32,512]{2,1,0:T(8,128)} %copy.25) | copy-start | bytes 6291460
  209.2 10.8 %copy-start.2 = (f32[16,32,512]{2,1,0:T(8,128)S(1)}, f32[16,32,512]{2,1,0:T(8,128)}, u32[]{:S(2)}) copy-start(f32[16,32,512]{2,1,0:T(8,128)} %exponential_multiply_fusion) | copy-start | bytes 3145732
  213.1 6.1 %collective-permute-start.1 = (f32[16,512]{1,0:T(8,128)S(1)}, f32[16,512]{1,0:T(8,128)S(1)}, u32[]{:S(2)}, u32[]{:S(2)}) collective-permute-start(f32[16,512]{1,0:T(8,128)S(1)} %fusion.21), channel_id=1, source_target_pairs={{0,1},{2,3},{4,5},{6,7},{8,9},{10,11},{12,13},{14,15},{16,17},{18,... | collective-permute-start | bytes 98312 | tf_op jit(solution)/shard_map/ppermute | solution.py:14
  219.1 4.4 %copy-start.7 = (f32[512]{0:T(512)S(1)}, f32[512]{0:T(512)}, u32[]{:S(2)}) copy-start(f32[512]{0:T(512)} %param.19) | copy-start | bytes 6148
Sparse Core Ops, SparseCore 0:
  11.0 170.7 all-gather.1

commit v8 on v6

--- a/solution.py
+++ b/solution.py
@@ -64,9 +64,10 @@
     res = t_ref[...].astype(jnp.float32) + acc + s_ref[...]
     o_ref[...] = jnp.where(m_ref[...] > 0, res, 0.0).astype(o_ref.dtype)
 
-def project_out(gated, gathered, rows_in, steer, live, tile=1024):
+def project_out(gated, gathered, rows_in, steer, live, tile=4096):
     cap, slab = gated.shape
     width = rows_in.shape[1]
+    tile = tile if width % tile == 0 else width
     column = (gathered.shape[1] - slab) // slab
     return pl.pallas_call(
         out_kernel,

time: 231 us -> 228 us (0.987)
  Pallas kernels: 12.2 us -> 9.88 us
where the time goes in v8:
time: 228 us
  waiting for transfers between devices  133 us (58%)
  other arithmetic  29.8 us (13%)
  between operations  16.8 us (7%)
  matrix products  16.7 us (7%)
  local copies, waits for them, and re-layouts  13.2 us (6%)
  Pallas kernels  9.88 us (4%)
  starting transfers between devices  8.94 us (4%)
    all_gather x1, waiting for transfers between devices, per_device(): gathered = lax.all_gather(piece, 'dp', axis=0, tiled=True)  133 us
    dot_general x1, matrix products, per_device(): extended = jnp.dot(rows_ext, w_in_all, preferred_element_type=jnp.float32)  16.7 us
    pallas_call x1, Pallas kernels, project_out(): pl.pallas_call(out_kernel, grid=(width // tile,), in_specs=[pl.BlockSpec(...  9.88 us
    ppermute x2, starting transfers between devices, from_behind(): lax.ppermute(value, axis, [(source, source + steps) for source in range(f...  8.94 us
    unnamed x27, local copies, waits for them, and re-layouts  4.96 us
    gather x1, local copies, waits for them, and re-layouts, filter_tables(): taps[jnp.clip(diff, 0, block - 1)]  4.84 us
    convert_element_type x1, other arithmetic, normalize(): return (values * scale * gain[None, :]).astype(jnp.bfloat16)  4.73 us
  transfers between devices with their start and end apart: 3, of which 1 were waited for; matrix products, arithmetic and copies ran while one was open for 13% of the time, Pallas kernels for 0%

profile of v8, /device:TPU:0, one launch (start us, length us, event | category | flops | bytes accessed | tf_op | source)
XLA Modules:
  0.0 227.9 jit_solution(6897300811220956780)
XLA Ops:
  6.5 1.3 copy.17
  7.8 3.0 %pad_maximum_fusion = bf16[512,2048]{1,0:T(8,128)(2,1)} fusion(bf16[512,512]{1,0:T(8,128)(2,1)S(1)} %bitcast.35, bf16[512,1536]{1,0:T(8,128)(2,1)} %param.15), kind=kLoop, calls=%fused_computation.21 | loop fusion | flops 4194304 | bytes 4194304 | tf_op jit(solution)/shard_map/concatenate | solution.py:122
  12.6 4.1 %fusion.2 = f32[384]{0:T(512)S(1)} fusion(bf16[1,1,384,8192]{3,2,1,0:T(8,128)(2,1)} %param.12), kind=kLoop, calls=%fused_computation.6 | loop fusion | flops 9436800 | bytes 6292992 | tf_op jit(solution)/shard_map/reduce_sum | solution.py:19
  16.8 4.7 %fusion.4 = bf16[384,8192]{1,0:T(8,128)(2,1)S(1)} fusion(f32[8192]{0:T(1024)S(1)} %copy-done.5, f32[384]{0:T(512)S(1)} %add_rsqrt_fusion, bf16[1,1,384,8192]{3,2,1,0:T(8,128)(2,1)} %param.12), kind=kLoop, calls=%fused_computation.8 | loop fusion | flops 12582912 | bytes 12617216 | tf_op jit(solution)/shard_map/convert_element_type | solution.py:20
  21.5 2.7 %copy-done.1 = bf16[384,8192]{1,0:T(8,128)(2,1)} copy-done((bf16[384,8192]{1,0:T(8,128)(2,1)}, bf16[384,8192]{1,0:T(8,128)(2,1)S(1)}, u32[]{:S(2)}) %copy-start.1) | copy-done | bytes 6291480
  24.3 5.3 %collective-permute-start = (bf16[2,8192]{1,0:T(2,128)(2,1)S(1)}, bf16[2,8192]{1,0:T(2,128)(2,1)S(1)}, u32[]{:S(2)}, u32[]{:S(2)}) collective-permute-start(bf16[2,8192]{1,0:T(2,128)(2,1)S(1)} %constant_dynamic-slice_fusion.1), channel_id=1, source_target_pairs={{0,1},{2,3},{4,5},{6,7},{8,9},{10,11},{12,13},{14,15},{16,17},{18,... | collective-permute-start | bytes 98312 | tf_op jit(solution)/shard_map/ppermute | solution.py:14
  31.1 1.4 multiply_exponential_fusion
  32.5 4.8 %gather_fusion = f32[1024,512]{1,0:T(8,128)} fusion(f32[32,512]{1,0:T(8,128)S(1)} %get-tuple-element.9, s32[1024]{0:T(1024)S(1)} %broadcast_clamp_fusion), kind=kCustom, calls=%fused_computation | custom fusion | bytes 4198400 | tf_op jit(solution)/shard_map/gather | solution.py:28
  37.4 1.2 iota_compare_fusion.1
  39.2 1.3 fusion.18.m_ref
  40.7 1.9 broadcast_select_fusion
  42.6 1.6 compare_select_fusion.s_ref
  45.3 2.6 %copy.18 = f32[32,32,512]{2,1,0:T(8,128)} copy(f32[32,32,512]{2,0,1:T(8,128)S(1)} %broadcast_select_fusion) | data formatting | bytes 4194304 | tf_op jit(solution)/shard_map/jit(_where)/select_n | solution.py:28
  48.6 0.6 copy-done.11
  49.2 132.5 %all-gather.2.cloned.1.call-done.w_ref = bf16[8192,2048]{1,0:T(8,128)(2,1)} async-done(((bf16[512,2048]{1,0:T(8,128)(2,1)}), bf16[8192,2048]{1,0:T(8,128)(2,1)}) %all-gather.2.cloned.1.call-update) | async-done | bytes 33554448 | tf_op jit(solution)/shard_map/all_gather | solution.py:123
  181.8 16.7 %fusion.8 = f32[386,1536]{1,0:T(8,128)S(1)} fusion(bf16[8192,2048]{1,0:T(8,128)(2,1)} %all-gather.2.cloned.1.call-done.w_ref, bf16[384,8192]{1,0:T(8,128)(2,1)} %copy-done.1, bf16[2,8192]{1,0:T(2,128)(2,1)} %copy-done.11), kind=kOutput, calls=%fused_computation.15 | convolution fusion | flops 9727249408 | bytes 33861632 | tf_op jit(solution)/shard_map/dot_general | solution.py:126
  198.6 0.7 fusion.13
  199.8 1.1 multiply_reduce_fusion.2
  200.8 1.3 multiply_reduce_fusion.3
  202.2 3.6 %collective-permute-start.1 = (f32[16,512]{1,0:T(8,128)S(1)}, f32[16,512]{1,0:T(8,128)S(1)}, u32[]{:S(2)}, u32[]{:S(2)}) collective-permute-start(f32[16,512]{1,0:T(8,128)S(1)} %fusion.20), channel_id=1, source_target_pairs={{0,1},{2,3},{4,5},{6,7},{8,9},{10,11},{12,13},{14,15},{16,17},{18,... | collective-permute-start | bytes 98312 | tf_op jit(solution)/shard_map/ppermute | solution.py:14
  205.8 2.4 %multiply_reduce_fusion = f32[12,32,512]{2,1,0:T(8,128)S(1)} fusion(f32[12,32,512]{2,1,0:T(8,128)S(1)} %bitcast.34, f32[32,32,512]{2,1,0:T(8,128)S(1)} %copy-done), kind=kLoop, calls=%fused_computation.3 | loop fusion | flops 12386304 | bytes 3670016 | tf_op jit(solution)/shard_map/reduce_sum | solution.py:54
  209.0 1.0 multiply_reduce_fusion.1
  210.2 1.0 fusion.17.g_ref
  211.2 9.9 %shard_map.118 = bf16[384,8192]{1,0:T(8,128)(2,1)} custom-call(bf16[384,512]{1,0:T(8,128)(2,1)} %fusion.17.g_ref, bf16[8192,2048]{1,0:T(8,128)(2,1)} %all-gather.2.cloned.1.call-done.w_ref, bf16[384,8192]{1,0:T(8,128)(2,1)} %bitcast.31, f32[1,8192]{1,0:T(1,128)} %compare_select_fusion.s_ref, s32[384,1]{1,0:T(8,128)} %fusion.18.m_ref), custom_call_target="tpu_custom_call" | custom-call | flops 3221225472 | bytes 21397504 | tf_op jit(solution)/shard_map/pallas_call | solution.py:72
  (53 shorter events, 4.3 us)
Async XLA Ops:
  6.5 4.3 %copy-start.12 = (s32[1,2]{1,0:T(1,128)S(1)}, s32[1,2]{1,0:T(1,128)}, u32[]{:S(2)}) copy-start(s32[1,2]{1,0:T(1,128)} %param.13) | copy-start | bytes 28
  6.5 175.2 %all-gather.2.cloned.1.call-start = ((), (), s32[]{:S(2)}) async-start(), calls=%async_computation | async-start | bytes 35651584 | tf_op jit(solution)/shard_map/all_gather | solution.py:123
  10.8 5.9 %copy-start.5 = (f32[8192]{0:T(1024)S(1)}, f32[8192]{0:T(1024)}, u32[]{:S(2)}) copy-start(f32[8192]{0:T(1024)} %param.14) | copy-start | bytes 98308
  16.7 12.9 %copy-start.3 = (f32[16,512]{1,0:T(8,128)S(1)}, f32[16,512]{1,0:T(8,128)}, u32[]{:S(2)}) copy-start(f32[16,512]{1,0:T(8,128)} %param.17) | copy-start | bytes 98308
  16.8 14.3 %copy-start.4 = (f32[16,512]{1,0:T(8,128)S(1)}, f32[16,512]{1,0:T(8,128)}, u32[]{:S(2)}) copy-start(f32[16,512]{1,0:T(8,128)} %param.18) | copy-start | bytes 98308
  21.5 2.7 %copy-start.1 = (bf16[384,8192]{1,0:T(8,128)(2,1)}, bf16[384,8192]{1,0:T(8,128)(2,1)S(1)}, u32[]{:S(2)}) copy-start(bf16[384,8192]{1,0:T(8,128)(2,1)S(1)} %fusion.4) | copy-start | bytes 18874372
  24.3 24.3 %collective-permute-start = (bf16[2,8192]{1,0:T(2,128)(2,1)S(1)}, bf16[2,8192]{1,0:T(2,128)(2,1)S(1)}, u32[]{:S(2)}, u32[]{:S(2)}) collective-permute-start(bf16[2,8192]{1,0:T(2,128)(2,1)S(1)} %constant_dynamic-slice_fusion.1), channel_id=1, source_target_pairs={{0,1},{2,3},{4,5},{6,7},{8,9},{10,11},{12,13},{14,15},{16,17},{18,... | collective-permute-start | bytes 98312 | tf_op jit(solution)/shard_map/ppermute | solution.py:14
  32.5 6.6 %copy-start.6 = (f32[3,1536]{1,0:T(4,128)S(1)}, f32[3,1536]{1,0:T(4,128)}, u32[]{:S(2)}) copy-start(f32[3,1536]{1,0:T(4,128)} %param.16) | copy-start | bytes 55300
  48.6 0.6 copy-start.11
  198.5 0.7 copy-start.8
  198.5 1.2 copy-start.2
  198.5 2.3 %copy-start.9 = (pred[12,12]{1,0:T(8,128)(4,1)S(1)}, pred[12,12]{1,0:T(8,128)(4,1)}, u32[]{:S(2)}) copy-start(pred[12,12]{1,0:T(8,128)(4,1)} %convert_compare_fusion) | copy-start | bytes 436
  199.3 6.6 %copy-start = (f32[32,32,512]{2,1,0:T(8,128)S(1)}, f32[32,32,512]{2,1,0:T(8,128)}, u32[]{:S(2)}) copy-start(f32[32,32,512]{2,1,0:T(8,128)} %copy.18) | copy-start | bytes 6291460
  199.4 9.5 %copy-start.10 = (f32[12]{0:T(128)S(1)}, f32[12]{0:T(128)}, u32[]{:S(2)}) copy-start(f32[12]{0:T(128)} %multiply_convert_fusion) | copy-start | bytes 148
  202.2 8.0 %copy-start.7 = (f32[512]{0:T(512)S(1)}, f32[512]{0:T(512)}, u32[]{:S(2)}) copy-start(f32[512]{0:T(512)} %param.19) | copy-start | bytes 6148
  202.2 6.1 %collective-permute-start.1 = (f32[16,512]{1,0:T(8,128)S(1)}, f32[16,512]{1,0:T(8,128)S(1)}, u32[]{:S(2)}, u32[]{:S(2)}) collective-permute-start(f32[16,512]{1,0:T(8,128)S(1)} %fusion.20), channel_id=1, source_target_pairs={{0,1},{2,3},{4,5},{6,7},{8,9},{10,11},{12,13},{14,15},{16,17},{18,... | collective-permute-start | bytes 98312 | tf_op jit(solution)/shard_map/ppermute | solution.py:14
Sparse Core Ops, SparseCore 0:
  11.0 170.7 all-gather.1

commit v9 on v8

--- a/solution.py
+++ b/solution.py
@@ -59,6 +59,27 @@
     return (inside + earlier).reshape(cap, width)
 
 
+def pack_kernel(wi_ref, wo_ref, o_ref):
+    cols = wi_ref.shape[1]
+    o_ref[:, :cols] = wi_ref[...]
+    o_ref[:, cols:] = wo_ref[...].astype(jnp.float32).T.astype(o_ref.dtype)
+
+
+def pack_weights(w_in, w_out):
+    rows, cols = w_in.shape
+    slab = w_out.shape[0]
+    step = 256 if rows % 256 == 0 else rows
+    return pl.pallas_call(
+        pack_kernel,
+        grid=(rows // step,),
+        in_specs=[
+            pl.BlockSpec((step, cols), lambda i: (i, 0)),
+            pl.BlockSpec((slab, step), lambda i: (0, i)),
+        ],
+        out_specs=pl.BlockSpec((step, cols + slab), lambda i: (i, 0)),
+        out_shape=jax.ShapeDtypeStruct((rows, cols + slab), w_in.dtype),
+    )(w_in, w_out)
+
 def out_kernel(g_ref, w_ref, t_ref, s_ref, m_ref, o_ref):
     acc = lax.dot_general(g_ref[...], w_ref[...], (((1,), (1,)), ((), ())), preferred_element_type=jnp.float32)
     res = t_ref[...].astype(jnp.float32) + acc + s_ref[...]
@@ -119,7 +140,7 @@
     cumlen = jnp.cumsum(lens_f)
     rescale = jnp.exp(decay_rate * (cap - own_len).astype(jnp.float32))
 
-    piece = jnp.concatenate([w_in, w_out.T], axis=1)
+    piece = pack_weights(w_in, w_out)
     gathered = lax.all_gather(piece, "dp", axis=0, tiled=True)
     w_in_all = gathered[:, : 3 * slab]
     rows_ext = jnp.concatenate([tail_normed, normed], axis=0)

time: 228 us -> 227 us (level)
  other arithmetic: 29.8 us -> 24.3 us
  Pallas kernels: 9.88 us -> 12.5 us
    concatenate x1 -> x0, other arithmetic: 3.03 us -> none  [per_device(): piece = jnp.concatenate([w_in, w_out.T], axis=1)]
    pallas_call x0 -> x1, Pallas kernels: none -> 2.66 us  [pack_weights(): pl.pallas_call(pack_kernel, grid=(rows // step,), in_specs=[pl.BlockSpec(...]
    convert_element_type x1, other arithmetic: 4.73 us -> 2.11 us  [normalize(): return (values * scale * gain[None, :]).astype(jnp.bfloat16)]
    all_gather x1, waiting for transfers between devices: 133 us -> 135 us  [per_device(): gathered = lax.all_gather(piece, 'dp', axis=0, tiled=True)]
    unnamed x27 -> x28, local copies, waits for them, and re-layouts: 4.96 us -> 4.78 us
  transfers between devices with their start and end apart: 3 -> 3, of which waited for: 1 -> 1; matrix products, arithmetic and copies ran while one was open for 13% -> 12% of each run, Pallas kernels for 0% -> 0%
where the time goes in v9:
time: 227 us; the launch traced here: 226 us
  waiting for transfers between devices  135 us (59%)
  other arithmetic  24.3 us (11%)
  between operations  16.8 us (7%)
  matrix products  16.7 us (7%)
  local copies, waits for them, and re-layouts  13 us (6%)
  Pallas kernels  12.5 us (6%)
  starting transfers between devices  7.85 us (3%)
    all_gather x1, waiting for transfers between devices, per_device(): gathered = lax.all_gather(piece, 'dp', axis=0, tiled=True)  135 us
    dot_general x1, matrix products, per_device(): extended = jnp.dot(rows_ext, w_in_all, preferred_element_type=jnp.float32)  16.7 us
    pallas_call x1, Pallas kernels, project_out(): pl.pallas_call(out_kernel, grid=(width // tile,), in_specs=[pl.BlockSpec(...  9.89 us
    ppermute x2, starting transfers between devices, from_behind(): lax.ppermute(value, axis, [(source, source + steps) for source in range(f...  7.85 us
    gather x1, local copies, waits for them, and re-layouts, filter_tables(): taps[jnp.clip(diff, 0, block - 1)]  4.84 us
    unnamed x28, local copies, waits for them, and re-layouts  4.78 us
  transfers between devices with their start and end apart: 3, of which 1 were waited for; matrix products, arithmetic and copies ran while one was open for 12% of the time, Pallas kernels for 0%

profile of v9, /device:TPU:0, one launch (start us, length us, event | category | flops | bytes accessed | tf_op | source)
XLA Modules:
  0.0 226.3 jit_solution(12584116403836774335)
XLA Ops:
  6.5 2.7 %shard_map.118 = bf16[512,2048]{1,0:T(8,128)(2,1)} custom-call(bf16[512,1536]{1,0:T(8,128)(2,1)} %wi_ref.1, bf16[512,512]{1,0:T(8,128)(2,1)} %wo_ref.1), custom_call_target="tpu_custom_call" | custom-call | tf_op jit(solution)/shard_map/pallas_call | solution.py:72
  11.0 4.3 %fusion.2 = f32[384]{0:T(512)S(1)} fusion(bf16[1,1,384,8192]{3,2,1,0:T(8,128)(2,1)} %param.12), kind=kLoop, calls=%fused_computation.6 | loop fusion | flops 9436800 | bytes 6292992 | tf_op jit(solution)/shard_map/reduce_sum | solution.py:19
  15.6 2.1 fusion.4
  17.7 3.5 %copy-done.2 = bf16[384,8192]{1,0:T(8,128)(2,1)} copy-done((bf16[384,8192]{1,0:T(8,128)(2,1)}, bf16[384,8192]{1,0:T(8,128)(2,1)S(1)}, u32[]{:S(2)}) %copy-start.2) | copy-done | bytes 6291480
  21.2 4.3 %collective-permute-start = (bf16[2,8192]{1,0:T(2,128)(2,1)S(1)}, bf16[2,8192]{1,0:T(2,128)(2,1)S(1)}, u32[]{:S(2)}, u32[]{:S(2)}) collective-permute-start(bf16[2,8192]{1,0:T(2,128)(2,1)S(1)} %constant_dynamic-slice_fusion.1), channel_id=1, source_target_pairs={{0,1},{2,3},{4,5},{6,7},{8,9},{10,11},{12,13},{14,15},{16,17},{18,... | collective-permute-start | bytes 98312 | tf_op jit(solution)/shard_map/ppermute | solution.py:14
  27.0 1.4 multiply_exponential_fusion
  28.4 4.8 %gather_fusion = f32[1024,512]{1,0:T(8,128)} fusion(f32[32,512]{1,0:T(8,128)S(1)} %get-tuple-element.9, s32[1024]{0:T(1024)S(1)} %broadcast_clamp_fusion), kind=kCustom, calls=%fused_computation | custom fusion | bytes 4198400 | tf_op jit(solution)/shard_map/gather | solution.py:28
  33.2 1.2 iota_compare_fusion.1
  34.4 0.6 convert_compare_fusion
  35.1 1.3 fusion.18.m_ref
  36.6 1.8 broadcast_select_fusion
  38.4 1.6 compare_select_fusion.s_ref
  41.1 2.6 %copy.15 = f32[32,32,512]{2,1,0:T(8,128)} copy(f32[32,32,512]{2,0,1:T(8,128)S(1)} %broadcast_select_fusion) | data formatting | bytes 4194304 | tf_op jit(solution)/shard_map/jit(_where)/select_n | solution.py:28
  44.5 0.6 copy-done.12
  45.1 135.1 %all-gather.2.cloned.1.call-done.w_ref = bf16[8192,2048]{1,0:T(8,128)(2,1)} async-done(((bf16[512,2048]{1,0:T(8,128)(2,1)}), bf16[8192,2048]{1,0:T(8,128)(2,1)}) %all-gather.2.cloned.1.call-update) | async-done | bytes 33554448 | tf_op jit(solution)/shard_map/all_gather | solution.py:144
  180.1 16.7 %fusion.8 = f32[386,1536]{1,0:T(8,128)S(1)} fusion(bf16[8192,2048]{1,0:T(8,128)(2,1)} %all-gather.2.cloned.1.call-done.w_ref, bf16[384,8192]{1,0:T(8,128)(2,1)} %copy-done.2, bf16[2,8192]{1,0:T(2,128)(2,1)} %copy-done.12), kind=kOutput, calls=%fused_computation.15 | convolution fusion | flops 9727249408 | bytes 33861632 | tf_op jit(solution)/shard_map/dot_general | solution.py:147
  196.9 0.7 fusion.13
  198.1 1.1 multiply_reduce_fusion.2
  199.2 1.3 multiply_reduce_fusion.3
  200.6 3.6 %collective-permute-start.1 = (f32[16,512]{1,0:T(8,128)S(1)}, f32[16,512]{1,0:T(8,128)S(1)}, u32[]{:S(2)}, u32[]{:S(2)}) collective-permute-start(f32[16,512]{1,0:T(8,128)S(1)} %fusion.20), channel_id=1, source_target_pairs={{0,1},{2,3},{4,5},{6,7},{8,9},{10,11},{12,13},{14,15},{16,17},{18,... | collective-permute-start | bytes 98312 | tf_op jit(solution)/shard_map/ppermute | solution.py:14
  204.2 2.4 %multiply_reduce_fusion = f32[12,32,512]{2,1,0:T(8,128)S(1)} fusion(f32[12,32,512]{2,1,0:T(8,128)S(1)} %bitcast.33, f32[32,32,512]{2,1,0:T(8,128)S(1)} %copy-done.1), kind=kLoop, calls=%fused_computation.3 | loop fusion | flops 12386304 | bytes 3670016 | tf_op jit(solution)/shard_map/reduce_sum | solution.py:54
  207.4 1.0 multiply_reduce_fusion.1
  208.6 1.0 fusion.17.g_ref
  209.6 9.9 %shard_map.119 = bf16[384,8192]{1,0:T(8,128)(2,1)} custom-call(bf16[384,512]{1,0:T(8,128)(2,1)} %fusion.17.g_ref, bf16[8192,2048]{1,0:T(8,128)(2,1)} %all-gather.2.cloned.1.call-done.w_ref, bf16[384,8192]{1,0:T(8,128)(2,1)} %bitcast.30, f32[1,8192]{1,0:T(1,128)} %compare_select_fusion.s_ref, s32[384,1]{1,0:T(8,128)} %fusion.18.m_ref), custom_call_target="tpu_custom_call" | custom-call | flops 3221225472 | bytes 21397504 | tf_op jit(solution)/shard_map/pallas_call | solution.py:93
  (54 shorter events, 4.1 us)
Async XLA Ops:
  6.5 2.7 %copy-start.13 = (s32[1,2]{1,0:T(1,128)S(1)}, s32[1,2]{1,0:T(1,128)}, u32[]{:S(2)}) copy-start(s32[1,2]{1,0:T(1,128)} %param.13) | copy-start | bytes 28
  6.5 173.6 %all-gather.2.cloned.1.call-start = ((), (), s32[]{:S(2)}) async-start(), calls=%async_computation | async-start | bytes 35651584 | tf_op jit(solution)/shard_map/all_gather | solution.py:144
  9.2 6.1 %copy-start.6 = (f32[8192]{0:T(1024)S(1)}, f32[8192]{0:T(1024)}, u32[]{:S(2)}) copy-start(f32[8192]{0:T(1024)} %param.14) | copy-start | bytes 98308
  11.0 4.6 %copy-start = (bf16[1,1,384,8192]{3,2,1,0:T(8,128)(2,1)S(1)}, bf16[1,1,384,8192]{3,2,1,0:T(8,128)(2,1)}, u32[]{:S(2)}) copy-start(bf16[1,1,384,8192]{3,2,1,0:T(8,128)(2,1)} %param.12) | copy-start | bytes 18874372
  15.6 9.9 %copy-start.4 = (f32[16,512]{1,0:T(8,128)S(1)}, f32[16,512]{1,0:T(8,128)}, u32[]{:S(2)}) copy-start(f32[16,512]{1,0:T(8,128)} %param.17) | copy-start | bytes 98308
  15.6 11.4 %copy-start.5 = (f32[16,512]{1,0:T(8,128)S(1)}, f32[16,512]{1,0:T(8,128)}, u32[]{:S(2)}) copy-start(f32[16,512]{1,0:T(8,128)} %param.18) | copy-start | bytes 98308
  17.7 3.5 %copy-start.2 = (bf16[384,8192]{1,0:T(8,128)(2,1)}, bf16[384,8192]{1,0:T(8,128)(2,1)S(1)}, u32[]{:S(2)}) copy-start(bf16[384,8192]{1,0:T(8,128)(2,1)S(1)} %fusion.4) | copy-start | bytes 18874372
  21.2 23.2 %collective-permute-start = (bf16[2,8192]{1,0:T(2,128)(2,1)S(1)}, bf16[2,8192]{1,0:T(2,128)(2,1)S(1)}, u32[]{:S(2)}, u32[]{:S(2)}) collective-permute-start(bf16[2,8192]{1,0:T(2,128)(2,1)S(1)} %constant_dynamic-slice_fusion.1), channel_id=1, source_target_pairs={{0,1},{2,3},{4,5},{6,7},{8,9},{10,11},{12,13},{14,15},{16,17},{18,... | collective-permute-start | bytes 98312 | tf_op jit(solution)/shard_map/ppermute | solution.py:14
  28.4 6.6 %copy-start.7 = (f32[3,1536]{1,0:T(4,128)S(1)}, f32[3,1536]{1,0:T(4,128)}, u32[]{:S(2)}) copy-start(f32[3,1536]{1,0:T(4,128)} %param.16) | copy-start | bytes 55300
  44.5 0.6 copy-start.12
  196.9 0.7 copy-start.9
  196.9 1.2 copy-start.3
  196.9 2.3 %copy-start.10 = (pred[12,12]{1,0:T(8,128)(4,1)S(1)}, pred[12,12]{1,0:T(8,128)(4,1)}, u32[]{:S(2)}) copy-start(pred[12,12]{1,0:T(8,128)(4,1)} %convert_compare_fusion) | copy-start | bytes 436
  197.6 6.6 %copy-start.1 = (f32[32,32,512]{2,1,0:T(8,128)S(1)}, f32[32,32,512]{2,1,0:T(8,128)}, u32[]{:S(2)}) copy-start(f32[32,32,512]{2,1,0:T(8,128)} %copy.15) | copy-start | bytes 6291460
  197.8 9.5 %copy-start.11 = (f32[12]{0:T(128)S(1)}, f32[12]{0:T(128)}, u32[]{:S(2)}) copy-start(f32[12]{0:T(128)} %multiply_convert_fusion) | copy-start | bytes 148
  200.6 8.0 %copy-start.8 = (f32[512]{0:T(512)S(1)}, f32[512]{0:T(512)}, u32[]{:S(2)}) copy-start(f32[512]{0:T(512)} %param.19) | copy-start | bytes 6148
  200.6 6.1 %collective-permute-start.1 = (f32[16,512]{1,0:T(8,128)S(1)}, f32[16,512]{1,0:T(8,128)S(1)}, u32[]{:S(2)}, u32[]{:S(2)}) collective-permute-start(f32[16,512]{1,0:T(8,128)S(1)} %fusion.20), channel_id=1, source_target_pairs={{0,1},{2,3},{4,5},{6,7},{8,9},{10,11},{12,13},{14,15},{16,17},{18,... | collective-permute-start | bytes 98312 | tf_op jit(solution)/shard_map/ppermute | solution.py:14
Sparse Core Ops, SparseCore 0:
  9.3 170.7 all-gather.1

commit v10 on v9

--- a/solution.py
+++ b/solution.py
@@ -2,6 +2,7 @@
 import jax.numpy as jnp
 from jax import lax
 from jax.experimental import pallas as pl
+from jax.experimental.pallas import tpu as pltpu
 from jax.sharding import PartitionSpec as P
 
 STEER_W = 1024
@@ -79,6 +80,33 @@
         out_specs=pl.BlockSpec((step, cols + slab), lambda i: (i, 0)),
         out_shape=jax.ShapeDtypeStruct((rows, cols + slab), w_in.dtype),
     )(w_in, w_out)
+
+def proj_kernel(x_ref, w_ref, o_ref):
+    o_ref[...] = jnp.dot(x_ref[...], w_ref[...], preferred_element_type=jnp.float32).astype(
+        o_ref.dtype
+    )
+
+
+def project_in(rows_ext, gathered, columns, tile=512):
+    count, depth = rows_ext.shape
+    tile = tile if columns % tile == 0 else columns
+    return pl.pallas_call(
+        proj_kernel,
+        grid=(columns // tile,),
+        in_specs=[
+            pl.BlockSpec((count, depth), lambda j: (0, 0)),
+            pl.BlockSpec((depth, tile), lambda j: (0, j)),
+        ],
+        out_specs=pl.BlockSpec((count, tile), lambda j: (0, j)),
+        out_shape=jax.ShapeDtypeStruct((count, columns), jnp.bfloat16),
+        compiler_params=pltpu.CompilerParams(vmem_limit_bytes=60 * 1024 * 1024),
+        cost_estimate=pl.CostEstimate(
+            flops=2 * count * depth * columns,
+            transcendentals=0,
+            bytes_accessed=2 * (count * depth + depth * columns + count * columns),
+        ),
+    )(rows_ext, gathered)
+
 
 def out_kernel(g_ref, w_ref, t_ref, s_ref, m_ref, o_ref):
     acc = lax.dot_general(g_ref[...], w_ref[...], (((1,), (1,)), ((), ())), preferred_element_type=jnp.float32)
@@ -142,10 +170,8 @@
 
     piece = pack_weights(w_in, w_out)
     gathered = lax.all_gather(piece, "dp", axis=0, tiled=True)
-    w_in_all = gathered[:, : 3 * slab]
     rows_ext = jnp.concatenate([tail_normed, normed], axis=0)
-    extended = jnp.dot(rows_ext, w_in_all, preferred_element_type=jnp.float32)
-    extended = lax.reduce_precision(extended, exponent_bits=8, mantissa_bits=7)
+    extended = project_in(rows_ext, gathered, 3 * slab).astype(jnp.float32)
     feat = (
         short_filter[0] * extended[2:]
         + short_filter[1] * extended[1:-1]

time: 227 us -> 228 us (level)
  matrix products: 16.7 us -> 0 us
  Pallas kernels: 12.5 us -> 29.2 us
  other arithmetic: 24.3 us -> 31 us
  waiting for transfers between devices: 135 us -> 131 us
    dot_general x1 -> x0, matrix products: 16.7 us -> none  [per_device(): extended = jnp.dot(rows_ext, w_in_all, preferred_element_type=jnp.float32)]
    pallas_call x0 -> x1, Pallas kernels: none -> 16.6 us  [project_in(): pl.pallas_call(proj_kernel, grid=(columns // tile,), in_specs=[pl.BlockSp...]
    concatenate x0 -> x1, other arithmetic: none -> 7.13 us  [per_device(): rows_ext = jnp.concatenate([tail_normed, normed], axis=0)]
    all_gather x1, waiting for transfers between devices: 135 us -> 131 us  [per_device(): gathered = lax.all_gather(piece, 'dp', axis=0, tiled=True)]
    unnamed x28 -> x18, local copies, waits for them, and re-layouts: 4.78 us -> 4.2 us
  transfers between devices with their start and end apart: 3 -> 3, of which waited for: 1 -> 1; matrix products, arithmetic and copies ran while one was open for 12% -> 13% of each run, Pallas kernels for 0% -> 0%
where the time goes in v10:
time: 228 us
  waiting for transfers between devices  131 us (57%)
  other arithmetic  31 us (14%)
  Pallas kernels  29.2 us (13%)
  between operations  16.7 us (7%)
  local copies, waits for them, and re-layouts  11.5 us (5%)
  starting transfers between devices  7.85 us (3%)
    all_gather x1, waiting for transfers between devices, per_device(): gathered = lax.all_gather(piece, 'dp', axis=0, tiled=True)  131 us
    pallas_call x1, Pallas kernels, project_in(): pl.pallas_call(proj_kernel, grid=(columns // tile,), in_specs=[pl.BlockSp...  16.6 us
    pallas_call x1, Pallas kernels, project_out(): pl.pallas_call(out_kernel, grid=(width // tile,), in_specs=[pl.BlockSpec(...  9.89 us
    ppermute x2, starting transfers between devices, from_behind(): lax.ppermute(value, axis, [(source, source + steps) for source in range(f...  7.85 us
    concatenate x1, other arithmetic, per_device(): rows_ext = jnp.concatenate([tail_normed, normed], axis=0)  7.13 us
  transfers between devices with their start and end apart: 3, of which 1 were waited for; matrix products, arithmetic and copies ran while one was open for 13% of the time, Pallas kernels for 0%

profile of v10, /device:TPU:0, one launch (start us, length us, event | category | flops | bytes accessed | tf_op | source)
XLA Modules:
  0.0 227.7 jit_solution(2542574746124179144)
XLA Ops:
  6.5 2.7 %shard_map.118 = bf16[512,2048]{1,0:T(8,128)(2,1)} custom-call(bf16[512,1536]{1,0:T(8,128)(2,1)} %wi_ref.1, bf16[512,512]{1,0:T(8,128)(2,1)} %wo_ref.1), custom_call_target="tpu_custom_call" | custom-call | tf_op jit(solution)/shard_map/pallas_call | solution.py:73
  9.2 0.6 constant_dynamic-slice_fusion.2
  11.0 4.3 %fusion = f32[384]{0:T(512)S(1)} fusion(bf16[1,1,384,8192]{3,2,1,0:T(8,128)(2,1)} %param.12), kind=kLoop, calls=%fused_computation.4 | loop fusion | flops 9436800 | bytes 6292992 | tf_op jit(solution)/shard_map/reduce_sum | solution.py:20
  15.6 2.1 fusion.2
  17.7 3.5 %copy-done.1 = bf16[384,8192]{1,0:T(8,128)(2,1)} copy-done((bf16[384,8192]{1,0:T(8,128)(2,1)}, bf16[384,8192]{1,0:T(8,128)(2,1)S(1)}, u32[]{:S(2)}) %copy-start.1) | copy-done | bytes 6291480
  21.2 4.3 %collective-permute-start = (bf16[2,8192]{1,0:T(2,128)(2,1)S(1)}, bf16[2,8192]{1,0:T(2,128)(2,1)S(1)}, u32[]{:S(2)}, u32[]{:S(2)}) collective-permute-start(bf16[2,8192]{1,0:T(2,128)(2,1)S(1)} %constant_dynamic-slice_fusion.1), channel_id=1, source_target_pairs={{0,1},{2,3},{4,5},{6,7},{8,9},{10,11},{12,13},{14,15},{16,17},{18,... | collective-permute-start | bytes 98312 | tf_op jit(solution)/shard_map/ppermute | solution.py:15
  27.0 1.4 multiply_exponential_fusion
  28.4 3.5 %gather_fusion = f32[1024,512]{1,0:T(8,128)S(1)} fusion(f32[32,512]{1,0:T(8,128)S(1)} %get-tuple-element.9, s32[1024]{0:T(1024)S(1)} %broadcast_clamp_fusion), kind=kCustom, calls=%fused_computation | custom fusion | bytes 4198400 | tf_op jit(solution)/shard_map/gather | solution.py:29
  32.6 1.3 fusion.8.m_ref
  34.1 1.5 broadcast_select_fusion
  35.7 1.6 compare_select_fusion.s_ref
  37.8 3.0 %copy.15 = f32[32,32,512]{2,1,0:T(8,128)S(1)} copy(f32[32,32,512]{2,0,1:T(8,128)} %broadcast_select_fusion) | data formatting | bytes 4194304 | tf_op jit(solution)/shard_map/jit(_where)/select_n | solution.py:29
  41.6 7.1 %pad_maximum_fusion.x_ref = bf16[386,8192]{1,0:T(8,128)(2,1)} fusion(bf16[384,8192]{1,0:T(8,128)(2,1)} %copy-done.1, bf16[2,8192]{1,0:T(2,128)(2,1)S(1)} %collective-permute-done), kind=kLoop, calls=%fused_computation.9 | loop fusion | flops 12648448 | bytes 12648448 | tf_op jit(solution)/shard_map/concatenate | solution.py:173
  48.7 131.4 %all-gather.2.cloned.1.call-done.w_ref = bf16[8192,2048]{1,0:T(8,128)(2,1)} async-done(((bf16[512,2048]{1,0:T(8,128)(2,1)}), bf16[8192,2048]{1,0:T(8,128)(2,1)}) %all-gather.2.cloned.1.call-update) | async-done | bytes 33554448 | tf_op jit(solution)/shard_map/all_gather | solution.py:172
  180.1 16.6 %shard_map.119 = bf16[386,1536]{1,0:T(8,128)(2,1)} custom-call(bf16[386,8192]{1,0:T(8,128)(2,1)} %pad_maximum_fusion.x_ref, bf16[8192,2048]{1,0:T(8,128)(2,1)} %all-gather.2.cloned.1.call-done.w_ref), custom_call_target="tpu_custom_call" | custom-call | flops 9714008064 | bytes 32675840 | tf_op jit(solution)/shard_map/pallas_call | solution.py:93
  196.8 1.6 convert_element_type.77
  198.3 0.7 fusion.3
  199.6 1.1 multiply_reduce_fusion.2
  200.6 1.3 multiply_reduce_fusion.3
  202.0 3.6 %collective-permute-start.1 = (f32[16,512]{1,0:T(8,128)S(1)}, f32[16,512]{1,0:T(8,128)S(1)}, u32[]{:S(2)}, u32[]{:S(2)}) collective-permute-start(f32[16,512]{1,0:T(8,128)S(1)} %fusion.10), channel_id=1, source_target_pairs={{0,1},{2,3},{4,5},{6,7},{8,9},{10,11},{12,13},{14,15},{16,17},{18,... | collective-permute-start | bytes 98312 | tf_op jit(solution)/shard_map/ppermute | solution.py:15
  205.6 2.4 %multiply_reduce_fusion = f32[12,32,512]{2,1,0:T(8,128)S(1)} fusion(f32[12,32,512]{2,1,0:T(8,128)S(1)} %bitcast.33, f32[32,32,512]{2,1,0:T(8,128)S(1)} %copy.15), kind=kLoop, calls=%fused_computation.1 | loop fusion | flops 12386304 | bytes 3670016 | tf_op jit(solution)/shard_map/reduce_sum | solution.py:55
  208.8 1.0 multiply_reduce_fusion.1
  210.0 1.0 fusion.7.g_ref
  211.0 9.9 %shard_map.120 = bf16[384,8192]{1,0:T(8,128)(2,1)} custom-call(bf16[384,512]{1,0:T(8,128)(2,1)} %fusion.7.g_ref, bf16[8192,2048]{1,0:T(8,128)(2,1)} %all-gather.2.cloned.1.call-done.w_ref, bf16[384,8192]{1,0:T(8,128)(2,1)} %bitcast.30, f32[1,8192]{1,0:T(1,128)} %compare_select_fusion.s_ref, s32[384,1]{1,0:T(8,128)} %fusion.8.m_ref), custom_call_target="tpu_custom_call" | custom-call | flops 3221225472 | bytes 21397504 | tf_op jit(solution)/shard_map/pallas_call | solution.py:121
  (46 shorter events, 3.6 us)
Async XLA Ops:
  6.5 2.7 %copy-start.8 = (s32[1,2]{1,0:T(1,128)S(1)}, s32[1,2]{1,0:T(1,128)}, u32[]{:S(2)}) copy-start(s32[1,2]{1,0:T(1,128)} %param.13) | copy-start | bytes 28
  6.5 173.6 %all-gather.2.cloned.1.call-start = ((), (), s32[]{:S(2)}) async-start(), calls=%async_computation | async-start | bytes 35651584 | tf_op jit(solution)/shard_map/all_gather | solution.py:172
  9.2 6.1 %copy-start.5 = (f32[8192]{0:T(1024)S(1)}, f32[8192]{0:T(1024)}, u32[]{:S(2)}) copy-start(f32[8192]{0:T(1024)} %param.14) | copy-start | bytes 98308
  11.0 4.6 %copy-start = (bf16[1,1,384,8192]{3,2,1,0:T(8,128)(2,1)S(1)}, bf16[1,1,384,8192]{3,2,1,0:T(8,128)(2,1)}, u32[]{:S(2)}) copy-start(bf16[1,1,384,8192]{3,2,1,0:T(8,128)(2,1)} %param.12) | copy-start | bytes 18874372
  15.6 9.9 %copy-start.3 = (f32[16,512]{1,0:T(8,128)S(1)}, f32[16,512]{1,0:T(8,128)}, u32[]{:S(2)}) copy-start(f32[16,512]{1,0:T(8,128)} %param.17) | copy-start | bytes 98308
  15.6 11.4 %copy-start.4 = (f32[16,512]{1,0:T(8,128)S(1)}, f32[16,512]{1,0:T(8,128)}, u32[]{:S(2)}) copy-start(f32[16,512]{1,0:T(8,128)} %param.18) | copy-start | bytes 98308
  17.7 3.5 %copy-start.1 = (bf16[384,8192]{1,0:T(8,128)(2,1)}, bf16[384,8192]{1,0:T(8,128)(2,1)S(1)}, u32[]{:S(2)}) copy-start(bf16[384,8192]{1,0:T(8,128)(2,1)S(1)} %fusion.2) | copy-start | bytes 18874372
  21.2 20.4 %collective-permute-start = (bf16[2,8192]{1,0:T(2,128)(2,1)S(1)}, bf16[2,8192]{1,0:T(2,128)(2,1)S(1)}, u32[]{:S(2)}, u32[]{:S(2)}) collective-permute-start(bf16[2,8192]{1,0:T(2,128)(2,1)S(1)} %constant_dynamic-slice_fusion.1), channel_id=1, source_target_pairs={{0,1},{2,3},{4,5},{6,7},{8,9},{10,11},{12,13},{14,15},{16,17},{18,... | collective-permute-start | bytes 98312 | tf_op jit(solution)/shard_map/ppermute | solution.py:15
  28.4 4.2 %copy-start.6 = (f32[3,1536]{1,0:T(4,128)S(1)}, f32[3,1536]{1,0:T(4,128)}, u32[]{:S(2)}) copy-start(f32[3,1536]{1,0:T(4,128)} %param.16) | copy-start | bytes 55300
  198.3 1.2 copy-start.2
  202.0 8.0 %copy-start.7 = (f32[512]{0:T(512)S(1)}, f32[512]{0:T(512)}, u32[]{:S(2)}) copy-start(f32[512]{0:T(512)} %param.19) | copy-start | bytes 6148
  202.0 6.0 %collective-permute-start.1 = (f32[16,512]{1,0:T(8,128)S(1)}, f32[16,512]{1,0:T(8,128)S(1)}, u32[]{:S(2)}, u32[]{:S(2)}) collective-permute-start(f32[16,512]{1,0:T(8,128)S(1)} %fusion.10), channel_id=1, source_target_pairs={{0,1},{2,3},{4,5},{6,7},{8,9},{10,11},{12,13},{14,15},{16,17},{18,... | collective-permute-start | bytes 98312 | tf_op jit(solution)/shard_map/ppermute | solution.py:15
Sparse Core Ops, SparseCore 0:
  9.3 170.7 all-gather.1

commit v11 on v9

--- a/solution.py
+++ b/solution.py
@@ -80,21 +80,29 @@
         out_shape=jax.ShapeDtypeStruct((rows, cols + slab), w_in.dtype),
     )(w_in, w_out)
 
-def out_kernel(g_ref, w_ref, t_ref, s_ref, m_ref, o_ref):
-    acc = lax.dot_general(g_ref[...], w_ref[...], (((1,), (1,)), ((), ())), preferred_element_type=jnp.float32)
+def out_kernel(gate_ref, local_ref, drive_ref, skip_ref, w_ref, t_ref, s_ref, m_ref, o_ref):
+    alive = m_ref[...] > 0
+    filtered = local_ref[...] + skip_ref[...] * drive_ref[...]
+    gated = jnp.where(alive, gate_ref[...] * filtered, 0.0).astype(w_ref.dtype)
+    acc = lax.dot_general(gated, w_ref[...], (((1,), (1,)), ((), ())), preferred_element_type=jnp.float32)
     res = t_ref[...].astype(jnp.float32) + acc + s_ref[...]
-    o_ref[...] = jnp.where(m_ref[...] > 0, res, 0.0).astype(o_ref.dtype)
-
-def project_out(gated, gathered, rows_in, steer, live, tile=4096):
-    cap, slab = gated.shape
+    o_ref[...] = jnp.where(alive, res, 0.0).astype(o_ref.dtype)
+
+
+def project_out(gate, local, drive, skip, gathered, rows_in, steer, live, tile=4096):
+    cap, slab = gate.shape
     width = rows_in.shape[1]
     tile = tile if width % tile == 0 else width
     column = (gathered.shape[1] - slab) // slab
+    whole = pl.BlockSpec((cap, slab), lambda j: (0, 0))
     return pl.pallas_call(
         out_kernel,
         grid=(width // tile,),
         in_specs=[
-            pl.BlockSpec((cap, slab), lambda j: (0, 0)),
+            whole,
+            whole,
+            whole,
+            pl.BlockSpec((1, slab), lambda j: (0, 0)),
             pl.BlockSpec((tile, slab), lambda j: (j, column)),
             pl.BlockSpec((cap, tile), lambda j: (0, j)),
             pl.BlockSpec((1, tile), lambda j: (0, j)),
@@ -103,8 +111,10 @@
         out_specs=pl.BlockSpec((cap, tile), lambda j: (0, j)),
         out_shape=jax.ShapeDtypeStruct((cap, width), rows_in.dtype),
         cost_estimate=pl.CostEstimate(flops=2 * cap * slab * width, transcendentals=0,
-            bytes_accessed=2 * (cap * slab + width * slab + 2 * cap * width) + 4 * width),
-    )(gated, gathered, rows_in, steer.reshape(1, width), live.astype(jnp.int32).reshape(cap, 1))
+            bytes_accessed=12 * cap * slab + 2 * (width * slab + 2 * cap * width) + 4 * width),
+    )(gate, local, drive, skip.reshape(1, slab), gathered, rows_in, steer.reshape(1, width),
+      live.astype(jnp.int32).reshape(cap, 1))
+
 
 def per_device(
     tokens,
@@ -165,13 +175,11 @@
         weight = jnp.where(source >= 0, jnp.exp(-decay_rate * between), 0.0)
         incoming = incoming + weight * got
     local = block_outputs(drive, states, incoming, decay_rate, toeplitz, lead, block)
-    filtered = local + skip_gain[None, :] * drive
-    gated = jnp.where(live[:, None], gate * filtered, 0.0).astype(jnp.bfloat16)
     rows2 = lax.dynamic_index_in_dim(steer_table, steer_layer[0], 0, keepdims=False)
     shift_vec = rows2[0] - rows2[1]
     columns = jnp.arange(width) // STEER_W
     steer = jnp.where(columns == steer_slab[0], 2.0 * shift_vec, 0.0)
-    result = project_out(gated, gathered, rows_in, steer, live)
+    result = project_out(gate, local, drive, skip_gain, gathered, rows_in, steer, live)
     return result.reshape(tokens.shape)
 
 

time: 227 us -> 228 us (level)
  no operation moved by 1% of the time
where the time goes in v11:
time: 228 us
  waiting for transfers between devices  135 us (59%)
  other arithmetic  25.2 us (11%)
  matrix products  16.7 us (7%)
  between operations  16.7 us (7%)
  Pallas kernels  13.3 us (6%)
  local copies, waits for them, and re-layouts  12.7 us (6%)
  starting transfers between devices  7.85 us (3%)
    all_gather x1, waiting for transfers between devices, per_device(): gathered = lax.all_gather(piece, 'dp', axis=0, tiled=True)  135 us
    dot_general x1, matrix products, per_device(): extended = jnp.dot(rows_ext, w_in_all, preferred_element_type=jnp.float32)  16.7 us
    pallas_call x1, Pallas kernels, project_out(): pl.pallas_call(out_kernel, grid=(width // tile,), in_specs=[whole, whole,...  10.6 us
    ppermute x2, starting transfers between devices, from_behind(): lax.ppermute(value, axis, [(source, source + steps) for source in range(f...  7.85 us
    gather x1, local copies, waits for them, and re-layouts, filter_tables(): taps[jnp.clip(diff, 0, block - 1)]  4.84 us
  transfers between devices with their start and end apart: 3, of which 1 were waited for; matrix products, arithmetic and copies ran while one was open for 12% of the time, Pallas kernels for 0%

profile of v11, /device:TPU:0, one launch (start us, length us, event | category | flops | bytes accessed | tf_op | source)
XLA Modules:
  0.0 227.5 jit_solution(14092565493622702273)
XLA Ops:
  6.5 2.7 %shard_map.118 = bf16[512,2048]{1,0:T(8,128)(2,1)} custom-call(bf16[512,1536]{1,0:T(8,128)(2,1)} %wi_ref.1, bf16[512,512]{1,0:T(8,128)(2,1)} %wo_ref.1), custom_call_target="tpu_custom_call" | custom-call | tf_op jit(solution)/shard_map/pallas_call | solution.py:72
  11.0 4.3 %fusion.2 = f32[384]{0:T(512)S(1)} fusion(bf16[1,1,384,8192]{3,2,1,0:T(8,128)(2,1)} %param.12), kind=kLoop, calls=%fused_computation.6 | loop fusion | flops 9436800 | bytes 6292992 | tf_op jit(solution)/shard_map/reduce_sum | solution.py:19
  15.6 2.1 fusion.4
  17.7 3.5 %copy-done.3 = bf16[384,8192]{1,0:T(8,128)(2,1)} copy-done((bf16[384,8192]{1,0:T(8,128)(2,1)}, bf16[384,8192]{1,0:T(8,128)(2,1)S(1)}, u32[]{:S(2)}) %copy-start.3) | copy-done | bytes 6291480
  21.2 4.3 %collective-permute-start = (bf16[2,8192]{1,0:T(2,128)(2,1)S(1)}, bf16[2,8192]{1,0:T(2,128)(2,1)S(1)}, u32[]{:S(2)}, u32[]{:S(2)}) collective-permute-start(bf16[2,8192]{1,0:T(2,128)(2,1)S(1)} %constant_dynamic-slice_fusion.1), channel_id=1, source_target_pairs={{0,1},{2,3},{4,5},{6,7},{8,9},{10,11},{12,13},{14,15},{16,17},{18,... | collective-permute-start | bytes 98312 | tf_op jit(solution)/shard_map/ppermute | solution.py:14
  27.0 1.4 multiply_exponential_fusion
  28.4 4.8 %gather_fusion = f32[1024,512]{1,0:T(8,128)} fusion(f32[32,512]{1,0:T(8,128)S(1)} %get-tuple-element.11, s32[1024]{0:T(1024)S(1)} %broadcast_clamp_fusion), kind=kCustom, calls=%fused_computation | custom fusion | bytes 4198400 | tf_op jit(solution)/shard_map/gather | solution.py:28
  33.2 1.1 iota_compare_fusion.1
  35.0 1.3 fusion.16.m_ref
  36.5 1.8 broadcast_select_fusion
  38.4 1.6 compare_select_fusion.s_ref
  41.1 2.6 %copy.15 = f32[32,32,512]{2,1,0:T(8,128)} copy(f32[32,32,512]{2,0,1:T(8,128)S(1)} %broadcast_select_fusion) | data formatting | bytes 4194304 | tf_op jit(solution)/shard_map/jit(_where)/select_n | solution.py:28
  44.5 0.6 copy-done.12
  45.1 135.1 %all-gather.2.cloned.1.call-done.w_ref = bf16[8192,2048]{1,0:T(8,128)(2,1)} async-done(((bf16[512,2048]{1,0:T(8,128)(2,1)}), bf16[8192,2048]{1,0:T(8,128)(2,1)}) %all-gather.2.cloned.1.call-update) | async-done | bytes 33554448 | tf_op jit(solution)/shard_map/all_gather | solution.py:154
  180.1 16.7 %fusion.8 = f32[386,1536]{1,0:T(8,128)S(1)} fusion(bf16[8192,2048]{1,0:T(8,128)(2,1)} %all-gather.2.cloned.1.call-done.w_ref, bf16[384,8192]{1,0:T(8,128)(2,1)} %copy-done.3, bf16[2,8192]{1,0:T(2,128)(2,1)} %copy-done.12), kind=kOutput, calls=%fused_computation.15 | convolution fusion | flops 9727249408 | bytes 33861632 | tf_op jit(solution)/shard_map/dot_general | solution.py:157
  196.9 0.7 fusion.13
  197.6 1.1 fusion.15
  198.7 1.1 multiply_reduce_fusion.2
  199.8 1.3 multiply_reduce_fusion.3
  201.2 3.6 %collective-permute-start.1 = (f32[16,512]{1,0:T(8,128)S(1)}, f32[16,512]{1,0:T(8,128)S(1)}, u32[]{:S(2)}, u32[]{:S(2)}) collective-permute-start(f32[16,512]{1,0:T(8,128)S(1)} %fusion.18), channel_id=1, source_target_pairs={{0,1},{2,3},{4,5},{6,7},{8,9},{10,11},{12,13},{14,15},{16,17},{18,... | collective-permute-start | bytes 98312 | tf_op jit(solution)/shard_map/ppermute | solution.py:14
  204.8 2.4 %multiply_reduce_fusion = f32[12,32,512]{2,1,0:T(8,128)S(1)} fusion(f32[12,32,512]{2,1,0:T(8,128)S(1)} %bitcast.30, f32[32,32,512]{2,1,0:T(8,128)S(1)} %copy-done.2), kind=kLoop, calls=%fused_computation.3 | loop fusion | flops 12386304 | bytes 3670016 | tf_op jit(solution)/shard_map/reduce_sum | solution.py:54
  208.0 1.0 multiply_reduce_fusion.1
  209.0 1.0 add.89
  210.0 10.6 %shard_map.119 = bf16[384,8192]{1,0:T(8,128)(2,1)} custom-call(f32[384,512]{1,0:T(8,128)} %get-tuple-element.9.gate_ref, f32[384,512]{1,0:T(8,128)} %bitcast.32, f32[384,512]{1,0:T(8,128)} %copy-done.1, f32[1,512]{1,0:T(1,128)} %bitcast.33, bf16[8192,2048]{1,0:T(8,128)(2,1)} %all-gather.2.cloned.1.call-done.w_ref, bf16[384,8192]{1,0:T(8,128)(2,1)} %bitcast.28, ...), custom_call_target="tpu_custom_call" | custom-call | flops 3221225472 | bytes 23363584 | tf_op jit(solution)/shard_map/pallas_call | solution.py:98
  (53 shorter events, 4.1 us)
Async XLA Ops:
  6.5 2.7 %copy-start.13 = (s32[1,2]{1,0:T(1,128)S(1)}, s32[1,2]{1,0:T(1,128)}, u32[]{:S(2)}) copy-start(s32[1,2]{1,0:T(1,128)} %param.13) | copy-start | bytes 28
  6.5 173.6 %all-gather.2.cloned.1.call-start = ((), (), s32[]{:S(2)}) async-start(), calls=%async_computation | async-start | bytes 35651584 | tf_op jit(solution)/shard_map/all_gather | solution.py:154
  9.2 6.1 %copy-start.7 = (f32[8192]{0:T(1024)S(1)}, f32[8192]{0:T(1024)}, u32[]{:S(2)}) copy-start(f32[8192]{0:T(1024)} %param.14) | copy-start | bytes 98308
  11.0 4.6 %copy-start = (bf16[1,1,384,8192]{3,2,1,0:T(8,128)(2,1)S(1)}, bf16[1,1,384,8192]{3,2,1,0:T(8,128)(2,1)}, u32[]{:S(2)}) copy-start(bf16[1,1,384,8192]{3,2,1,0:T(8,128)(2,1)} %param.12) | copy-start | bytes 18874372
  15.6 9.9 %copy-start.5 = (f32[16,512]{1,0:T(8,128)S(1)}, f32[16,512]{1,0:T(8,128)}, u32[]{:S(2)}) copy-start(f32[16,512]{1,0:T(8,128)} %param.17) | copy-start | bytes 98308
  15.6 11.4 %copy-start.6 = (f32[16,512]{1,0:T(8,128)S(1)}, f32[16,512]{1,0:T(8,128)}, u32[]{:S(2)}) copy-start(f32[16,512]{1,0:T(8,128)} %param.18) | copy-start | bytes 98308
  17.7 3.5 %copy-start.3 = (bf16[384,8192]{1,0:T(8,128)(2,1)}, bf16[384,8192]{1,0:T(8,128)(2,1)S(1)}, u32[]{:S(2)}) copy-start(bf16[384,8192]{1,0:T(8,128)(2,1)S(1)} %fusion.4) | copy-start | bytes 18874372
  21.2 23.2 %collective-permute-start = (bf16[2,8192]{1,0:T(2,128)(2,1)S(1)}, bf16[2,8192]{1,0:T(2,128)(2,1)S(1)}, u32[]{:S(2)}, u32[]{:S(2)}) collective-permute-start(bf16[2,8192]{1,0:T(2,128)(2,1)S(1)} %constant_dynamic-slice_fusion.1), channel_id=1, source_target_pairs={{0,1},{2,3},{4,5},{6,7},{8,9},{10,11},{12,13},{14,15},{16,17},{18,... | collective-permute-start | bytes 98312 | tf_op jit(solution)/shard_map/ppermute | solution.py:14
  28.4 6.6 %copy-start.8 = (f32[3,1536]{1,0:T(4,128)S(1)}, f32[3,1536]{1,0:T(4,128)}, u32[]{:S(2)}) copy-start(f32[3,1536]{1,0:T(4,128)} %param.16) | copy-start | bytes 55300
  44.5 0.6 copy-start.12
  196.9 0.7 copy-start.10
  196.9 1.8 copy-start.4
  197.6 2.2 copy-start.9
  197.6 7.2 %copy-start.2 = (f32[32,32,512]{2,1,0:T(8,128)S(1)}, f32[32,32,512]{2,1,0:T(8,128)}, u32[]{:S(2)}) copy-start(f32[32,32,512]{2,1,0:T(8,128)} %copy.15) | copy-start | bytes 6291460
  198.7 9.3 %copy-start.1 = (f32[384,512]{1,0:T(8,128)}, f32[384,512]{1,0:T(8,128)S(1)}, u32[]{:S(2)}) copy-start(f32[384,512]{1,0:T(8,128)S(1)} %get-tuple-element.8.drive_ref) | copy-start | bytes 2359300
  198.7 9.1 %copy-start.11 = (f32[12]{0:T(128)S(1)}, f32[12]{0:T(128)}, u32[]{:S(2)}) copy-start(f32[12]{0:T(128)} %multiply_convert_fusion) | copy-start | bytes 148
  201.2 6.1 %collective-permute-start.1 = (f32[16,512]{1,0:T(8,128)S(1)}, f32[16,512]{1,0:T(8,128)S(1)}, u32[]{:S(2)}, u32[]{:S(2)}) collective-permute-start(f32[16,512]{1,0:T(8,128)S(1)} %fusion.18), channel_id=1, source_target_pairs={{0,1},{2,3},{4,5},{6,7},{8,9},{10,11},{12,13},{14,15},{16,17},{18,... | collective-permute-start | bytes 98312 | tf_op jit(solution)/shard_map/ppermute | solution.py:14
Sparse Core Ops, SparseCore 0:
  9.3 170.7 all-gather.1

commit v12 on v9

--- a/solution.py
+++ b/solution.py
@@ -32,18 +32,20 @@
     return toeplitz, lead, close
 
 
-def block_states(drive, decay_rate, close, block):
-    cap, width = drive.shape
-    count = cap // block
-    pieces = drive.reshape(count, block, width)
-    ends = jnp.sum(close[None] * pieces[:, :, None, :], axis=1)
+def block_powers(decay_rate, count, block):
     steps = jnp.arange(count)
     gap = (steps[:, None] - steps[None, :]).astype(jnp.float32)
-    powers = jnp.where(
+    return jnp.where(
         (gap >= 0)[:, :, None, None],
         jnp.exp(-decay_rate[None, None] * (block * jnp.maximum(gap, 0.0))[:, :, None, None]),
         0.0,
     )
+
+
+def block_states(drive, powers, close, block):
+    cap, width = drive.shape
+    pieces = drive.reshape(cap // block, block, width)
+    ends = jnp.sum(close[None] * pieces[:, :, None, :], axis=1)
     return jnp.sum(powers * ends[None], axis=1)
 
 
@@ -144,6 +146,8 @@
     gathered = lax.all_gather(piece, "dp", axis=0, tiled=True)
     w_in_all = gathered[:, : 3 * slab]
     rows_ext = jnp.concatenate([tail_normed, normed], axis=0)
+    powers = block_powers(decay_rate, cap // block, block)
+    rows_ext, powers = lax.optimization_barrier((rows_ext, powers))
     extended = jnp.dot(rows_ext, w_in_all, preferred_element_type=jnp.float32)
     extended = lax.reduce_precision(extended, exponent_bits=8, mantissa_bits=7)
     feat = (
@@ -153,7 +157,7 @@
     )
     gate = feat[:, :slab]
     drive = jnp.where(live[:, None], feat[:, slab : 2 * slab] * feat[:, 2 * slab :], 0.0)
-    states = block_states(drive, decay_rate, close, block)
+    states = block_states(drive, powers, close, block)
     ending = states[-1] * rescale
     incoming = jnp.zeros_like(ending)
     for k in range(1, groups):

time: 227 us -> 225 us (level)
  other arithmetic: 24.3 us -> 31.7 us
  waiting for transfers between devices: 135 us -> 129 us
    concatenate x0 -> x1, other arithmetic: none -> 7.3 us  [per_device(): rows_ext = jnp.concatenate([tail_normed, normed], axis=0)]
    all_gather x1, waiting for transfers between devices: 135 us -> 129 us  [per_device(): gathered = lax.all_gather(piece, 'dp', axis=0, tiled=True)]
    select_n x0 -> x1, other arithmetic: none -> 2.56 us  [block_powers(): jnp.where((gap >= 0)[:, :, None, None], jnp.exp(-decay_rate[None, None] *...]
    unnamed x28 -> x22, local copies, waits for them, and re-layouts: 4.78 us -> 4.5 us
  transfers between devices with their start and end apart: 3 -> 3, of which waited for: 1 -> 1; matrix products, arithmetic and copies ran while one was open for 12% -> 15% of each run, Pallas kernels for 0% -> 0%
where the time goes in v12:
time: 225 us
  waiting for transfers between devices  129 us (57%)
  other arithmetic  31.7 us (14%)
  between operations  16.8 us (7%)
  matrix products  15.7 us (7%)
  Pallas kernels  12.6 us (6%)
  local copies, waits for them, and re-layouts  11.6 us (5%)
  starting transfers between devices  7.86 us (3%)
    all_gather x1, waiting for transfers between devices, per_device(): gathered = lax.all_gather(piece, 'dp', axis=0, tiled=True)  129 us
    dot_general x1, matrix products, per_device(): extended = jnp.dot(rows_ext, w_in_all, preferred_element_type=jnp.float32)  15.7 us
    pallas_call x1, Pallas kernels, project_out(): pl.pallas_call(out_kernel, grid=(width // tile,), in_specs=[pl.BlockSpec(...  9.89 us
    ppermute x2, starting transfers between devices, from_behind(): lax.ppermute(value, axis, [(source, source + steps) for source in range(f...  7.85 us
    concatenate x1, other arithmetic, per_device(): rows_ext = jnp.concatenate([tail_normed, normed], axis=0)  7.3 us
  transfers between devices with their start and end apart: 3, of which 1 were waited for; matrix products, arithmetic and copies ran while one was open for 15% of the time, Pallas kernels for 0%

profile of v12, /device:TPU:0, one launch (start us, length us, event | category | flops | bytes accessed | tf_op | source)
XLA Modules:
  0.0 224.9 jit_solution(997918073243117174)
XLA Ops:
  6.5 2.7 %shard_map.118 = bf16[512,2048]{1,0:T(8,128)(2,1)} custom-call(bf16[512,1536]{1,0:T(8,128)(2,1)} %wi_ref.1, bf16[512,512]{1,0:T(8,128)(2,1)} %wo_ref.1), custom_call_target="tpu_custom_call" | custom-call | tf_op jit(solution)/shard_map/pallas_call | solution.py:74
  11.0 4.3 %fusion.2 = f32[384]{0:T(512)S(1)} fusion(bf16[1,1,384,8192]{3,2,1,0:T(8,128)(2,1)} %param.12), kind=kLoop, calls=%fused_computation.6 | loop fusion | flops 9436800 | bytes 6292992 | tf_op jit(solution)/shard_map/reduce_sum | solution.py:19
  15.6 2.1 fusion.4
  17.8 3.5 %copy-done.1 = bf16[384,8192]{1,0:T(8,128)(2,1)} copy-done((bf16[384,8192]{1,0:T(8,128)(2,1)}, bf16[384,8192]{1,0:T(8,128)(2,1)S(1)}, u32[]{:S(2)}) %copy-start.1) | copy-done | bytes 6291480
  21.3 4.3 %collective-permute-start = (bf16[2,8192]{1,0:T(2,128)(2,1)S(1)}, bf16[2,8192]{1,0:T(2,128)(2,1)S(1)}, u32[]{:S(2)}, u32[]{:S(2)}) collective-permute-start(bf16[2,8192]{1,0:T(2,128)(2,1)S(1)} %constant_dynamic-slice_fusion.1), channel_id=1, source_target_pairs={{0,1},{2,3},{4,5},{6,7},{8,9},{10,11},{12,13},{14,15},{16,17},{18,... | collective-permute-start | bytes 98312 | tf_op jit(solution)/shard_map/ppermute | solution.py:14
  27.0 1.5 multiply_exponential_fusion
  28.5 3.5 %gather_fusion = f32[1024,512]{1,0:T(8,128)S(1)} fusion(f32[32,512]{1,0:T(8,128)S(1)} %get-tuple-element.13, s32[1024]{0:T(1024)S(1)} %broadcast_clamp_fusion), kind=kCustom, calls=%fused_computation | custom fusion | bytes 4198400 | tf_op jit(solution)/shard_map/gather | solution.py:28
  32.7 1.3 fusion.13.m_ref
  34.2 1.5 broadcast_select_fusion
  35.8 2.6 %exponential_select_fusion = f32[12,12,16,512]{3,2,1,0:T(8,128)} fusion(f32[12,12]{1,0:T(8,128)S(1)} %maximum_multiply_fusion, f32[16,512]{1,0:T(8,128)S(1)} %neg.5, pred[12,12]{1,0:T(8,128)(4,1)S(1)} %convert_compare_fusion), kind=kLoop, calls=%fused_computation.13 | loop fusion | flops 2359296 | bytes 4752080 | tf_op jit(solution)/shard_map/jit(_where)/select_n | solution.py:38
  38.3 1.6 compare_select_fusion.s_ref
  40.5 2.8 %copy.15 = f32[32,32,512]{2,1,0:T(8,128)S(1)} copy(f32[32,32,512]{2,0,1:T(8,128)} %broadcast_select_fusion) | data formatting | bytes 4194304 | tf_op jit(solution)/shard_map/jit(_where)/select_n | solution.py:28
  43.5 0.6 fusion.16
  44.1 7.3 %pad_maximum_fusion = bf16[386,8192]{1,0:T(8,128)(2,1)} fusion(bf16[384,8192]{1,0:T(8,128)(2,1)} %copy-done.1, bf16[2,8192]{1,0:T(2,128)(2,1)S(1)} %collective-permute-done), kind=kLoop, calls=%fused_computation.11 | loop fusion | flops 12648448 | bytes 12648448 | tf_op jit(solution)/shard_map/concatenate | solution.py:148
  51.4 128.7 %all-gather.2.cloned.1.call-done.w_ref = bf16[8192,2048]{1,0:T(8,128)(2,1)} async-done(((bf16[512,2048]{1,0:T(8,128)(2,1)}), bf16[8192,2048]{1,0:T(8,128)(2,1)}) %all-gather.2.cloned.1.call-update) | async-done | bytes 33554448 | tf_op jit(solution)/shard_map/all_gather | solution.py:146
  180.2 15.7 %fusion.5 = f32[386,1536]{1,0:T(8,128)S(1)} fusion(bf16[386,8192]{1,0:T(8,128)(2,1)} %pad_maximum_fusion, bf16[8192,2048]{1,0:T(8,128)(2,1)} %all-gather.2.cloned.1.call-done.w_ref), kind=kOutput, calls=%fused_computation.14 | convolution fusion | flops 9714600960 | bytes 33959936 | tf_op jit(solution)/shard_map/dot_general | solution.py:151
  195.9 0.7 fusion.8
  197.3 1.1 multiply_reduce_fusion.2
  198.5 0.6 multiply_reduce_fusion.3
  199.2 3.6 %collective-permute-start.1 = (f32[16,512]{1,0:T(8,128)S(1)}, f32[16,512]{1,0:T(8,128)S(1)}, u32[]{:S(2)}, u32[]{:S(2)}) collective-permute-start(f32[16,512]{1,0:T(8,128)S(1)} %fusion.15), channel_id=1, source_target_pairs={{0,1},{2,3},{4,5},{6,7},{8,9},{10,11},{12,13},{14,15},{16,17},{18,... | collective-permute-start | bytes 98312 | tf_op jit(solution)/shard_map/ppermute | solution.py:14
  202.8 2.4 %multiply_reduce_fusion = f32[12,32,512]{2,1,0:T(8,128)S(1)} fusion(f32[12,32,512]{2,1,0:T(8,128)S(1)} %bitcast.36, f32[32,32,512]{2,1,0:T(8,128)S(1)} %copy.15), kind=kLoop, calls=%fused_computation.3 | loop fusion | flops 12386304 | bytes 3670016 | tf_op jit(solution)/shard_map/reduce_sum | solution.py:56
  206.0 1.0 multiply_reduce_fusion.1
  207.2 1.0 fusion.12.g_ref
  208.2 9.9 %shard_map.119 = bf16[384,8192]{1,0:T(8,128)(2,1)} custom-call(bf16[384,512]{1,0:T(8,128)(2,1)} %fusion.12.g_ref, bf16[8192,2048]{1,0:T(8,128)(2,1)} %all-gather.2.cloned.1.call-done.w_ref, bf16[384,8192]{1,0:T(8,128)(2,1)} %bitcast.31, f32[1,8192]{1,0:T(1,128)} %compare_select_fusion.s_ref, s32[384,1]{1,0:T(8,128)} %fusion.13.m_ref), custom_call_target="tpu_custom_call" | custom-call | flops 3221225472 | bytes 21397504 | tf_op jit(solution)/shard_map/pallas_call | solution.py:95
  (51 shorter events, 3.9 us)
Async XLA Ops:
  6.5 2.7 %copy-start.8 = (s32[1,2]{1,0:T(1,128)S(1)}, s32[1,2]{1,0:T(1,128)}, u32[]{:S(2)}) copy-start(s32[1,2]{1,0:T(1,128)} %param.13) | copy-start | bytes 28
  6.5 173.6 %all-gather.2.cloned.1.call-start = ((), (), s32[]{:S(2)}) async-start(), calls=%async_computation | async-start | bytes 35651584 | tf_op jit(solution)/shard_map/all_gather | solution.py:146
  9.2 6.1 %copy-start.5 = (f32[8192]{0:T(1024)S(1)}, f32[8192]{0:T(1024)}, u32[]{:S(2)}) copy-start(f32[8192]{0:T(1024)} %param.14) | copy-start | bytes 98308
  11.0 4.6 %copy-start = (bf16[1,1,384,8192]{3,2,1,0:T(8,128)(2,1)S(1)}, bf16[1,1,384,8192]{3,2,1,0:T(8,128)(2,1)}, u32[]{:S(2)}) copy-start(bf16[1,1,384,8192]{3,2,1,0:T(8,128)(2,1)} %param.12) | copy-start | bytes 18874372
  15.6 9.9 %copy-start.3 = (f32[16,512]{1,0:T(8,128)S(1)}, f32[16,512]{1,0:T(8,128)}, u32[]{:S(2)}) copy-start(f32[16,512]{1,0:T(8,128)} %param.17) | copy-start | bytes 98308
  15.6 11.4 %copy-start.4 = (f32[16,512]{1,0:T(8,128)S(1)}, f32[16,512]{1,0:T(8,128)}, u32[]{:S(2)}) copy-start(f32[16,512]{1,0:T(8,128)} %param.18) | copy-start | bytes 98308
  17.7 3.5 %copy-start.1 = (bf16[384,8192]{1,0:T(8,128)(2,1)}, bf16[384,8192]{1,0:T(8,128)(2,1)S(1)}, u32[]{:S(2)}) copy-start(bf16[384,8192]{1,0:T(8,128)(2,1)S(1)} %fusion.4) | copy-start | bytes 18874372
  21.3 22.9 %collective-permute-start = (bf16[2,8192]{1,0:T(2,128)(2,1)S(1)}, bf16[2,8192]{1,0:T(2,128)(2,1)S(1)}, u32[]{:S(2)}, u32[]{:S(2)}) collective-permute-start(bf16[2,8192]{1,0:T(2,128)(2,1)S(1)} %constant_dynamic-slice_fusion.1), channel_id=1, source_target_pairs={{0,1},{2,3},{4,5},{6,7},{8,9},{10,11},{12,13},{14,15},{16,17},{18,... | collective-permute-start | bytes 98312 | tf_op jit(solution)/shard_map/ppermute | solution.py:14
  28.5 4.2 %copy-start.6 = (f32[3,1536]{1,0:T(4,128)S(1)}, f32[3,1536]{1,0:T(4,128)}, u32[]{:S(2)}) copy-start(f32[3,1536]{1,0:T(4,128)} %param.16) | copy-start | bytes 55300
  195.9 2.5 %slice-start = ((s8[4718592]{0:T(1024)(128)(4,1)}), s8[4194304]{0:T(1024)(128)(4,1)S(1)}, s32[]{:S(2)}) async-start(s8[4718592]{0:T(1024)(128)(4,1)} %bitcast.32), calls=%async_computation.1 | async-start | bytes 8388608
  195.9 1.4 copy-start.2
  195.9 2.6 %slice-start.1 = ((s8[4718592]{0:T(1024)(128)(4,1)}), s8[524288]{0:T(1024)(128)(4,1)S(1)}, s32[]{:S(2)}) async-start(s8[4718592]{0:T(1024)(128)(4,1)} %bitcast.32), calls=%async_computation.2 | async-start | bytes 1048576
  199.2 8.0 %copy-start.7 = (f32[512]{0:T(512)S(1)}, f32[512]{0:T(512)}, u32[]{:S(2)}) copy-start(f32[512]{0:T(512)} %param.19) | copy-start | bytes 6148
  199.2 6.1 %collective-permute-start.1 = (f32[16,512]{1,0:T(8,128)S(1)}, f32[16,512]{1,0:T(8,128)S(1)}, u32[]{:S(2)}, u32[]{:S(2)}) collective-permute-start(f32[16,512]{1,0:T(8,128)S(1)} %fusion.15), channel_id=1, source_target_pairs={{0,1},{2,3},{4,5},{6,7},{8,9},{10,11},{12,13},{14,15},{16,17},{18,... | collective-permute-start | bytes 98312 | tf_op jit(solution)/shard_map/ppermute | solution.py:14
Sparse Core Ops, SparseCore 0:
  9.4 170.7 all-gather.1

commit v13 on v12

--- a/solution.py
+++ b/solution.py
@@ -49,13 +49,12 @@
     return jnp.sum(powers * ends[None], axis=1)
 
 
-def block_outputs(drive, states, incoming, decay_rate, toeplitz, lead, block):
+def block_outputs(drive, states, incoming, reach, toeplitz, lead, block):
     cap, width = drive.shape
     count = cap // block
     pieces = drive.reshape(count, block, width)
     inside = jnp.sum(toeplitz[None] * pieces[:, :, None, :], axis=1)
-    starts = (jnp.arange(count) * block).astype(jnp.float32)
-    carried = incoming[None] * jnp.exp(-decay_rate[None] * starts[:, None, None])
+    carried = incoming[None] * reach
     before = jnp.concatenate([jnp.zeros_like(states[:1]), states[:-1]], axis=0) + carried
     earlier = jnp.sum(lead[None] * before[:, :, None, :], axis=1)
     return (inside + earlier).reshape(cap, width)
@@ -147,7 +146,9 @@
     w_in_all = gathered[:, : 3 * slab]
     rows_ext = jnp.concatenate([tail_normed, normed], axis=0)
     powers = block_powers(decay_rate, cap // block, block)
-    rows_ext, powers = lax.optimization_barrier((rows_ext, powers))
+    starts = (jnp.arange(cap // block) * block).astype(jnp.float32)
+    reach = jnp.exp(-decay_rate[None] * starts[:, None, None])
+    rows_ext, powers, reach = lax.optimization_barrier((rows_ext, powers, reach))
     extended = jnp.dot(rows_ext, w_in_all, preferred_element_type=jnp.float32)
     extended = lax.reduce_precision(extended, exponent_bits=8, mantissa_bits=7)
     feat = (
@@ -168,7 +169,7 @@
         ) - lax.dynamic_index_in_dim(cumlen, jnp.maximum(source, 0), 0, keepdims=False)
         weight = jnp.where(source >= 0, jnp.exp(-decay_rate * between), 0.0)
         incoming = incoming + weight * got
-    local = block_outputs(drive, states, incoming, decay_rate, toeplitz, lead, block)
+    local = block_outputs(drive, states, incoming, reach, toeplitz, lead, block)
     filtered = local + skip_gain[None, :] * drive
     gated = jnp.where(live[:, None], gate * filtered, 0.0).astype(jnp.bfloat16)
     rows2 = lax.dynamic_index_in_dim(steer_table, steer_layer[0], 0, keepdims=False)

time: 225 us -> 225 us (level)
  no operation moved by 1% of the time
where the time goes in v13:
time: 225 us
  waiting for transfers between devices  128 us (57%)
  other arithmetic  32.4 us (14%)
  between operations  16.8 us (7%)
  matrix products  15.7 us (7%)
  Pallas kernels  12.6 us (6%)
  local copies, waits for them, and re-layouts  11.6 us (5%)
  starting transfers between devices  7.86 us (3%)
    all_gather x1, waiting for transfers between devices, per_device(): gathered = lax.all_gather(piece, 'dp', axis=0, tiled=True)  128 us
    dot_general x1, matrix products, per_device(): extended = jnp.dot(rows_ext, w_in_all, preferred_element_type=jnp.float32)  15.7 us
    pallas_call x1, Pallas kernels, project_out(): pl.pallas_call(out_kernel, grid=(width // tile,), in_specs=[pl.BlockSpec(...  9.89 us
    ppermute x2, starting transfers between devices, from_behind(): lax.ppermute(value, axis, [(source, source + steps) for source in range(f...  7.85 us
    concatenate x1, other arithmetic, per_device(): rows_ext = jnp.concatenate([tail_normed, normed], axis=0)  7.24 us
  transfers between devices with their start and end apart: 3, of which 1 were waited for; matrix products, arithmetic and copies ran while one was open for 15% of the time, Pallas kernels for 0%

profile of v13, /device:TPU:0, one launch (start us, length us, event | category | flops | bytes accessed | tf_op | source)
XLA Modules:
  0.0 224.8 jit_solution(12850317362591383032)
XLA Ops:
  6.5 2.7 %shard_map.118 = bf16[512,2048]{1,0:T(8,128)(2,1)} custom-call(bf16[512,1536]{1,0:T(8,128)(2,1)} %wi_ref.1, bf16[512,512]{1,0:T(8,128)(2,1)} %wo_ref.1), custom_call_target="tpu_custom_call" | custom-call | tf_op jit(solution)/shard_map/pallas_call | solution.py:73
  11.0 4.3 %fusion.2 = f32[384]{0:T(512)S(1)} fusion(bf16[1,1,384,8192]{3,2,1,0:T(8,128)(2,1)} %param.12), kind=kLoop, calls=%fused_computation.6 | loop fusion | flops 9436800 | bytes 6292992 | tf_op jit(solution)/shard_map/reduce_sum | solution.py:19
  15.6 2.1 fusion.4
  17.8 3.5 %copy-done.1 = bf16[384,8192]{1,0:T(8,128)(2,1)} copy-done((bf16[384,8192]{1,0:T(8,128)(2,1)}, bf16[384,8192]{1,0:T(8,128)(2,1)S(1)}, u32[]{:S(2)}) %copy-start.1) | copy-done | bytes 6291480
  21.3 4.3 %collective-permute-start = (bf16[2,8192]{1,0:T(2,128)(2,1)S(1)}, bf16[2,8192]{1,0:T(2,128)(2,1)S(1)}, u32[]{:S(2)}, u32[]{:S(2)}) collective-permute-start(bf16[2,8192]{1,0:T(2,128)(2,1)S(1)} %constant_dynamic-slice_fusion.1), channel_id=1, source_target_pairs={{0,1},{2,3},{4,5},{6,7},{8,9},{10,11},{12,13},{14,15},{16,17},{18,... | collective-permute-start | bytes 98312 | tf_op jit(solution)/shard_map/ppermute | solution.py:14
  27.0 1.5 multiply_exponential_fusion
  28.5 3.5 %gather_fusion = f32[1024,512]{1,0:T(8,128)S(1)} fusion(f32[32,512]{1,0:T(8,128)S(1)} %get-tuple-element.15, s32[1024]{0:T(1024)S(1)} %broadcast_clamp_fusion), kind=kCustom, calls=%fused_computation | custom fusion | bytes 4198400 | tf_op jit(solution)/shard_map/gather | solution.py:28
  32.1 1.3 fusion.13.m_ref
  33.4 0.9 multiply_exponential_fusion.1
  34.5 1.5 broadcast_select_fusion
  36.1 2.6 %exponential_select_fusion = f32[12,12,16,512]{3,2,1,0:T(8,128)} fusion(f32[12,12]{1,0:T(8,128)S(1)} %maximum_multiply_fusion, f32[16,512]{1,0:T(8,128)S(1)} %neg.5, pred[12,12]{1,0:T(8,128)(4,1)S(1)} %convert_compare_fusion), kind=kLoop, calls=%fused_computation.13 | loop fusion | flops 2359296 | bytes 4752080 | tf_op jit(solution)/shard_map/jit(_where)/select_n | solution.py:38
  38.6 1.6 compare_select_fusion.s_ref
  41.4 2.8 %copy.15 = f32[32,32,512]{2,1,0:T(8,128)S(1)} copy(f32[32,32,512]{2,0,1:T(8,128)} %broadcast_select_fusion) | data formatting | bytes 4194304 | tf_op jit(solution)/shard_map/jit(_where)/select_n | solution.py:28
  45.0 7.2 %pad_maximum_fusion = bf16[386,8192]{1,0:T(8,128)(2,1)} fusion(bf16[384,8192]{1,0:T(8,128)(2,1)} %copy-done.1, bf16[2,8192]{1,0:T(2,128)(2,1)S(1)} %collective-permute-done), kind=kLoop, calls=%fused_computation.11 | loop fusion | flops 12648448 | bytes 12648448 | tf_op jit(solution)/shard_map/concatenate | solution.py:147
  52.2 128.0 %all-gather.2.cloned.1.call-done.w_ref = bf16[8192,2048]{1,0:T(8,128)(2,1)} async-done(((bf16[512,2048]{1,0:T(8,128)(2,1)}), bf16[8192,2048]{1,0:T(8,128)(2,1)}) %all-gather.2.cloned.1.call-update) | async-done | bytes 33554448 | tf_op jit(solution)/shard_map/all_gather | solution.py:145
  180.2 15.7 %fusion.5 = f32[386,1536]{1,0:T(8,128)S(1)} fusion(bf16[386,8192]{1,0:T(8,128)(2,1)} %pad_maximum_fusion, bf16[8192,2048]{1,0:T(8,128)(2,1)} %all-gather.2.cloned.1.call-done.w_ref), kind=kOutput, calls=%fused_computation.14 | convolution fusion | flops 9714600960 | bytes 33959936 | tf_op jit(solution)/shard_map/dot_general | solution.py:152
  195.9 0.7 fusion.8
  197.3 1.1 multiply_reduce_fusion.2
  198.5 0.6 multiply_reduce_fusion.3
  199.2 3.6 %collective-permute-start.1 = (f32[16,512]{1,0:T(8,128)S(1)}, f32[16,512]{1,0:T(8,128)S(1)}, u32[]{:S(2)}, u32[]{:S(2)}) collective-permute-start(f32[16,512]{1,0:T(8,128)S(1)} %fusion.15), channel_id=1, source_target_pairs={{0,1},{2,3},{4,5},{6,7},{8,9},{10,11},{12,13},{14,15},{16,17},{18,... | collective-permute-start | bytes 98312 | tf_op jit(solution)/shard_map/ppermute | solution.py:14
  202.8 2.4 %multiply_reduce_fusion = f32[12,32,512]{2,1,0:T(8,128)S(1)} fusion(f32[12,32,512]{2,1,0:T(8,128)S(1)} %bitcast.36, f32[32,32,512]{2,1,0:T(8,128)S(1)} %copy.15), kind=kLoop, calls=%fused_computation.3 | loop fusion | flops 12386304 | bytes 3670016 | tf_op jit(solution)/shard_map/reduce_sum | solution.py:56
  205.9 1.0 multiply_reduce_fusion.1
  207.1 1.0 fusion.12.g_ref
  208.1 9.9 %shard_map.119 = bf16[384,8192]{1,0:T(8,128)(2,1)} custom-call(bf16[384,512]{1,0:T(8,128)(2,1)} %fusion.12.g_ref, bf16[8192,2048]{1,0:T(8,128)(2,1)} %all-gather.2.cloned.1.call-done.w_ref, bf16[384,8192]{1,0:T(8,128)(2,1)} %bitcast.31, f32[1,8192]{1,0:T(1,128)} %compare_select_fusion.s_ref, s32[384,1]{1,0:T(8,128)} %fusion.13.m_ref), custom_call_target="tpu_custom_call" | custom-call | flops 3221225472 | bytes 21397504 | tf_op jit(solution)/shard_map/pallas_call | solution.py:94
  (54 shorter events, 4.4 us)
Async XLA Ops:
  6.5 2.7 %copy-start.9 = (s32[1,2]{1,0:T(1,128)S(1)}, s32[1,2]{1,0:T(1,128)}, u32[]{:S(2)}) copy-start(s32[1,2]{1,0:T(1,128)} %param.13) | copy-start | bytes 28
  6.5 173.6 %all-gather.2.cloned.1.call-start = ((), (), s32[]{:S(2)}) async-start(), calls=%async_computation | async-start | bytes 35651584 | tf_op jit(solution)/shard_map/all_gather | solution.py:145
  9.2 6.1 %copy-start.6 = (f32[8192]{0:T(1024)S(1)}, f32[8192]{0:T(1024)}, u32[]{:S(2)}) copy-start(f32[8192]{0:T(1024)} %param.14) | copy-start | bytes 98308
  11.0 4.6 %copy-start = (bf16[1,1,384,8192]{3,2,1,0:T(8,128)(2,1)S(1)}, bf16[1,1,384,8192]{3,2,1,0:T(8,128)(2,1)}, u32[]{:S(2)}) copy-start(bf16[1,1,384,8192]{3,2,1,0:T(8,128)(2,1)} %param.12) | copy-start | bytes 18874372
  15.6 9.9 %copy-start.4 = (f32[16,512]{1,0:T(8,128)S(1)}, f32[16,512]{1,0:T(8,128)}, u32[]{:S(2)}) copy-start(f32[16,512]{1,0:T(8,128)} %param.17) | copy-start | bytes 98308
  15.6 11.4 %copy-start.5 = (f32[16,512]{1,0:T(8,128)S(1)}, f32[16,512]{1,0:T(8,128)}, u32[]{:S(2)}) copy-start(f32[16,512]{1,0:T(8,128)} %param.18) | copy-start | bytes 98308
  17.7 3.5 %copy-start.1 = (bf16[384,8192]{1,0:T(8,128)(2,1)}, bf16[384,8192]{1,0:T(8,128)(2,1)S(1)}, u32[]{:S(2)}) copy-start(bf16[384,8192]{1,0:T(8,128)(2,1)S(1)} %fusion.4) | copy-start | bytes 18874372
  21.3 23.7 %collective-permute-start = (bf16[2,8192]{1,0:T(2,128)(2,1)S(1)}, bf16[2,8192]{1,0:T(2,128)(2,1)S(1)}, u32[]{:S(2)}, u32[]{:S(2)}) collective-permute-start(bf16[2,8192]{1,0:T(2,128)(2,1)S(1)} %constant_dynamic-slice_fusion.1), channel_id=1, source_target_pairs={{0,1},{2,3},{4,5},{6,7},{8,9},{10,11},{12,13},{14,15},{16,17},{18,... | collective-permute-start | bytes 98312 | tf_op jit(solution)/shard_map/ppermute | solution.py:14
  28.5 3.6 %copy-start.7 = (f32[3,1536]{1,0:T(4,128)S(1)}, f32[3,1536]{1,0:T(4,128)}, u32[]{:S(2)}) copy-start(f32[3,1536]{1,0:T(4,128)} %param.16) | copy-start | bytes 55300
  195.9 2.5 %slice-start = ((s8[4718592]{0:T(1024)(128)(4,1)}), s8[4194304]{0:T(1024)(128)(4,1)S(1)}, s32[]{:S(2)}) async-start(s8[4718592]{0:T(1024)(128)(4,1)} %bitcast.32), calls=%async_computation.1 | async-start | bytes 8388608
  195.9 1.4 copy-start.2
  195.9 2.6 %slice-start.1 = ((s8[4718592]{0:T(1024)(128)(4,1)}), s8[524288]{0:T(1024)(128)(4,1)S(1)}, s32[]{:S(2)}) async-start(s8[4718592]{0:T(1024)(128)(4,1)} %bitcast.32), calls=%async_computation.2 | async-start | bytes 1048576
  198.5 7.3 %copy-start.3 = (f32[12,16,512]{2,1,0:T(8,128)S(1)}, f32[12,16,512]{2,1,0:T(8,128)}, u32[]{:S(2)}) copy-start(f32[12,16,512]{2,1,0:T(8,128)} %multiply_exponential_fusion.1) | copy-start | bytes 1179652
  199.2 7.9 %copy-start.8 = (f32[512]{0:T(512)S(1)}, f32[512]{0:T(512)}, u32[]{:S(2)}) copy-start(f32[512]{0:T(512)} %param.19) | copy-start | bytes 6148
  199.2 6.1 %collective-permute-start.1 = (f32[16,512]{1,0:T(8,128)S(1)}, f32[16,512]{1,0:T(8,128)S(1)}, u32[]{:S(2)}, u32[]{:S(2)}) collective-permute-start(f32[16,512]{1,0:T(8,128)S(1)} %fusion.15), channel_id=1, source_target_pairs={{0,1},{2,3},{4,5},{6,7},{8,9},{10,11},{12,13},{14,15},{16,17},{18,... | collective-permute-start | bytes 98312 | tf_op jit(solution)/shard_map/ppermute | solution.py:14
Sparse Core Ops, SparseCore 0:
  9.4 170.7 all-gather.1

commit v14 on v13

--- a/solution.py
+++ b/solution.py
@@ -148,7 +148,9 @@
     powers = block_powers(decay_rate, cap // block, block)
     starts = (jnp.arange(cap // block) * block).astype(jnp.float32)
     reach = jnp.exp(-decay_rate[None] * starts[:, None, None])
-    rows_ext, powers, reach = lax.optimization_barrier((rows_ext, powers, reach))
+    rows_ext, powers, reach, toeplitz, lead, close = lax.optimization_barrier(
+        (rows_ext, powers, reach, toeplitz, lead, close)
+    )
     extended = jnp.dot(rows_ext, w_in_all, preferred_element_type=jnp.float32)
     extended = lax.reduce_precision(extended, exponent_bits=8, mantissa_bits=7)
     feat = (

time: 225 us -> 225 us (level)
  waiting for transfers between devices: 128 us -> 122 us
  other arithmetic: 32.4 us -> 36 us
    all_gather x1, waiting for transfers between devices: 128 us -> 122 us  [per_device(): gathered = lax.all_gather(piece, 'dp', axis=0, tiled=True)]
    select_n x1 -> x0, local copies, waits for them, and re-layouts: 2.81 us -> none  [filter_tables(): jnp.where((diff >= 0)[:, :, None], taps[jnp.clip(diff, 0, block - 1)], 0.0)]
    optimization_barrier x0 -> x1, local copies, waits for them, and re-layouts: none -> 2.54 us  [per_device(): lax.optimization_barrier((rows_ext, powers, reach, toeplitz, lead, close))]
  transfers between devices with their start and end apart: 3 -> 3, of which waited for: 1 -> 1; matrix products, arithmetic and copies ran while one was open for 15% -> 18% of each run, Pallas kernels for 0% -> 0%
where the time goes in v14:
time: 225 us
  waiting for transfers between devices  122 us (54%)
  other arithmetic  36 us (16%)
  between operations  16.9 us (8%)
  matrix products  15.7 us (7%)
  local copies, waits for them, and re-layouts  13.8 us (6%)
  Pallas kernels  12.6 us (6%)
  starting transfers between devices  8.4 us (4%)
    all_gather x1, waiting for transfers between devices, per_device(): gathered = lax.all_gather(piece, 'dp', axis=0, tiled=True)  122 us
    dot_general x1, matrix products, per_device(): extended = jnp.dot(rows_ext, w_in_all, preferred_element_type=jnp.float32)  15.7 us
    pallas_call x1, Pallas kernels, project_out(): pl.pallas_call(out_kernel, grid=(width // tile,), in_specs=[pl.BlockSpec(...  9.89 us
    ppermute x2, starting transfers between devices, from_behind(): lax.ppermute(value, axis, [(source, source + steps) for source in range(f...  8.4 us
    concatenate x1, other arithmetic, per_device(): rows_ext = jnp.concatenate([tail_normed, normed], axis=0)  7.39 us
    gather x1, local copies, waits for them, and re-layouts, filter_tables(): taps[jnp.clip(diff, 0, block - 1)]  4.89 us
  transfers between devices with their start and end apart: 3, of which 1 were waited for; matrix products, arithmetic and copies ran while one was open for 18% of the time, Pallas kernels for 0%

profile of v14, /device:TPU:0, one launch (start us, length us, event | category | flops | bytes accessed | tf_op | source)
XLA Modules:
  0.0 225.0 jit_solution(17087521154827550031)
XLA Ops:
  6.5 2.7 %shard_map.118 = bf16[512,2048]{1,0:T(8,128)(2,1)} custom-call(bf16[512,1536]{1,0:T(8,128)(2,1)} %wi_ref.1, bf16[512,512]{1,0:T(8,128)(2,1)} %wo_ref.1), custom_call_target="tpu_custom_call" | custom-call | tf_op jit(solution)/shard_map/pallas_call | solution.py:73
  11.2 4.3 %fusion.2 = f32[384]{0:T(512)S(1)} fusion(bf16[1,1,384,8192]{3,2,1,0:T(8,128)(2,1)} %param.12), kind=kLoop, calls=%fused_computation.6 | loop fusion | flops 9436800 | bytes 6292992 | tf_op jit(solution)/shard_map/reduce_sum | solution.py:19
  15.8 2.1 fusion.4
  17.9 3.3 %copy-done.1 = bf16[384,8192]{1,0:T(8,128)(2,1)} copy-done((bf16[384,8192]{1,0:T(8,128)(2,1)}, bf16[384,8192]{1,0:T(8,128)(2,1)S(1)}, u32[]{:S(2)}) %copy-start.1) | copy-done | bytes 6291480
  21.9 4.8 %collective-permute-start = (bf16[2,8192]{1,0:T(2,128)(2,1)}, bf16[2,8192]{1,0:T(2,128)(2,1)}, u32[]{:S(2)}, u32[]{:S(2)}) collective-permute-start(bf16[2,8192]{1,0:T(2,128)(2,1)} %constant_dynamic-slice_fusion.1), channel_id=1, source_target_pairs={{0,1},{2,3},{4,5},{6,7},{8,9},{10,11},{12,13},{14,15},{16,17},{18,... | collective-permute-start | bytes 98312 | tf_op jit(solution)/shard_map/ppermute | solution.py:14
  28.1 1.5 multiply_exponential_fusion
  29.6 4.9 %gather_fusion = f32[1024,512]{1,0:T(8,128)} fusion(f32[32,512]{1,0:T(8,128)S(1)} %get-tuple-element.21, s32[1024]{0:T(1024)S(1)} %broadcast_clamp_fusion), kind=kCustom, calls=%fused_computation | custom fusion | bytes 4198400 | tf_op jit(solution)/shard_map/gather | solution.py:28
  35.2 1.3 fusion.13.m_ref
  37.5 1.8 broadcast_select_fusion
  39.3 3.3 %exponential_select_fusion = f32[12,12,16,512]{3,2,1,0:T(8,128)} fusion(f32[12,12]{1,0:T(8,128)S(1)} %maximum_multiply_fusion, f32[16,512]{1,0:T(8,128)} %copy-done.4, pred[12,12]{1,0:T(8,128)(4,1)S(1)} %convert_compare_fusion), kind=kLoop, calls=%fused_computation.13 | loop fusion | flops 2359296 | bytes 4752080 | tf_op jit(solution)/shard_map/jit(_where)/select_n | solution.py:38
  42.6 1.6 compare_select_fusion.s_ref
  44.2 1.2 iota_compare_fusion.1
  46.1 1.3 reduce-window.4
  47.4 1.3 fusion.16
  48.7 7.4 %pad_maximum_fusion = bf16[386,8192]{1,0:T(8,128)(2,1)} fusion(bf16[384,8192]{1,0:T(8,128)(2,1)} %copy-done.1, bf16[2,8192]{1,0:T(2,128)(2,1)} %collective-permute-done), kind=kLoop, calls=%fused_computation.11 | loop fusion | flops 12648448 | bytes 12648448 | tf_op jit(solution)/shard_map/concatenate | solution.py:147
  56.1 2.5 %copy.15 = f32[32,32,512]{2,1,0:T(8,128)} copy(f32[32,32,512]{2,0,1:T(8,128)S(1)} %broadcast_select_fusion) | data formatting | bytes 4194304 | tf_op jit(solution)/shard_map/optimization_barrier | solution.py:151
  58.6 121.6 %all-gather.2.cloned.1.call-done.w_ref = bf16[8192,2048]{1,0:T(8,128)(2,1)} async-done(((bf16[512,2048]{1,0:T(8,128)(2,1)}), bf16[8192,2048]{1,0:T(8,128)(2,1)}) %all-gather.2.cloned.1.call-update) | async-done | bytes 33554448 | tf_op jit(solution)/shard_map/all_gather | solution.py:145
  180.2 15.7 %fusion.5 = f32[386,1536]{1,0:T(8,128)S(1)} fusion(bf16[386,8192]{1,0:T(8,128)(2,1)} %pad_maximum_fusion, bf16[8192,2048]{1,0:T(8,128)(2,1)} %all-gather.2.cloned.1.call-done.w_ref), kind=kOutput, calls=%fused_computation.14 | convolution fusion | flops 9714600960 | bytes 33959936 | tf_op jit(solution)/shard_map/dot_general | solution.py:154
  197.3 1.1 multiply_reduce_fusion.2
  199.2 3.6 %collective-permute-start.1 = (f32[16,512]{1,0:T(8,128)S(1)}, f32[16,512]{1,0:T(8,128)S(1)}, u32[]{:S(2)}, u32[]{:S(2)}) collective-permute-start(f32[16,512]{1,0:T(8,128)S(1)} %fusion.15), channel_id=1, source_target_pairs={{0,1},{2,3},{4,5},{6,7},{8,9},{10,11},{12,13},{14,15},{16,17},{18,... | collective-permute-start | bytes 98312 | tf_op jit(solution)/shard_map/ppermute | solution.py:14
  202.8 2.4 %multiply_reduce_fusion = f32[12,32,512]{2,1,0:T(8,128)S(1)} fusion(f32[12,32,512]{2,1,0:T(8,128)S(1)} %bitcast.36, f32[32,32,512]{2,1,0:T(8,128)S(1)} %copy-done.2), kind=kLoop, calls=%fused_computation.3 | loop fusion | flops 12386304 | bytes 3670016 | tf_op jit(solution)/shard_map/reduce_sum | solution.py:56
  206.1 1.0 multiply_reduce_fusion.1
  207.2 1.0 fusion.12.g_ref
  208.2 9.9 %shard_map.119 = bf16[384,8192]{1,0:T(8,128)(2,1)} custom-call(bf16[384,512]{1,0:T(8,128)(2,1)} %fusion.12.g_ref, bf16[8192,2048]{1,0:T(8,128)(2,1)} %all-gather.2.cloned.1.call-done.w_ref, bf16[384,8192]{1,0:T(8,128)(2,1)} %bitcast.31, f32[1,8192]{1,0:T(1,128)} %compare_select_fusion.s_ref, s32[384,1]{1,0:T(8,128)} %fusion.13.m_ref), custom_call_target="tpu_custom_call" | custom-call | flops 3221225472 | bytes 21397504 | tf_op jit(solution)/shard_map/pallas_call | solution.py:94
  (62 shorter events, 6.5 us)
Async XLA Ops:
  6.5 2.7 %copy-start.13 = (s32[1,2]{1,0:T(1,128)S(1)}, s32[1,2]{1,0:T(1,128)}, u32[]{:S(2)}) copy-start(s32[1,2]{1,0:T(1,128)} %param.13) | copy-start | bytes 28
  6.5 173.6 %all-gather.2.cloned.1.call-start = ((), (), s32[]{:S(2)}) async-start(), calls=%async_computation | async-start | bytes 35651584 | tf_op jit(solution)/shard_map/all_gather | solution.py:145
  9.2 6.2 %copy-start.8 = (f32[8192]{0:T(1024)S(1)}, f32[8192]{0:T(1024)}, u32[]{:S(2)}) copy-start(f32[8192]{0:T(1024)} %param.14) | copy-start | bytes 98308
  11.2 4.6 %copy-start = (bf16[1,1,384,8192]{3,2,1,0:T(8,128)(2,1)S(1)}, bf16[1,1,384,8192]{3,2,1,0:T(8,128)(2,1)}, u32[]{:S(2)}) copy-start(bf16[1,1,384,8192]{3,2,1,0:T(8,128)(2,1)} %param.12) | copy-start | bytes 18874372
  15.8 10.9 %copy-start.5 = (f32[16,512]{1,0:T(8,128)S(1)}, f32[16,512]{1,0:T(8,128)}, u32[]{:S(2)}) copy-start(f32[16,512]{1,0:T(8,128)} %param.17) | copy-start | bytes 98308
  15.8 12.3 %copy-start.7 = (f32[16,512]{1,0:T(8,128)S(1)}, f32[16,512]{1,0:T(8,128)}, u32[]{:S(2)}) copy-start(f32[16,512]{1,0:T(8,128)} %param.18) | copy-start | bytes 98308
  17.9 3.3 %copy-start.1 = (bf16[384,8192]{1,0:T(8,128)(2,1)}, bf16[384,8192]{1,0:T(8,128)(2,1)S(1)}, u32[]{:S(2)}) copy-start(bf16[384,8192]{1,0:T(8,128)(2,1)S(1)} %fusion.4) | copy-start | bytes 18874372
  21.9 26.8 %collective-permute-start = (bf16[2,8192]{1,0:T(2,128)(2,1)}, bf16[2,8192]{1,0:T(2,128)(2,1)}, u32[]{:S(2)}, u32[]{:S(2)}) collective-permute-start(bf16[2,8192]{1,0:T(2,128)(2,1)} %constant_dynamic-slice_fusion.1), channel_id=1, source_target_pairs={{0,1},{2,3},{4,5},{6,7},{8,9},{10,11},{12,13},{14,15},{16,17},{18,... | collective-permute-start | bytes 98312 | tf_op jit(solution)/shard_map/ppermute | solution.py:14
  26.7 10.6 %copy-start.4 = (f32[16,512]{1,0:T(8,128)}, f32[16,512]{1,0:T(8,128)S(1)}, u32[]{:S(2)}) copy-start(f32[16,512]{1,0:T(8,128)S(1)} %neg.5) | copy-start | bytes 98308
  29.6 4.9 %copy-start.10 = (f32[3,1536]{1,0:T(4,128)S(1)}, f32[3,1536]{1,0:T(4,128)}, u32[]{:S(2)}) copy-start(f32[3,1536]{1,0:T(4,128)} %param.16) | copy-start | bytes 55300
  58.6 137.3 %copy-start.9 = (f32[1536]{0:T(1024)S(1)}, f32[1536]{0:T(1024)}, u32[]{:S(2)}) copy-start(f32[1536]{0:T(1024)} %get-tuple-element.19) | copy-start | bytes 18436
  195.9 2.5 %slice-start = ((s8[4718592]{0:T(1024)(128)(4,1)}), s8[4194304]{0:T(1024)(128)(4,1)S(1)}, s32[]{:S(2)}) async-start(s8[4718592]{0:T(1024)(128)(4,1)} %bitcast.32), calls=%async_computation.1 | async-start | bytes 8388608
  195.9 0.8 copy-start.12
  195.9 1.4 copy-start.3
  195.9 2.6 %slice-start.1 = ((s8[4718592]{0:T(1024)(128)(4,1)}), s8[524288]{0:T(1024)(128)(4,1)S(1)}, s32[]{:S(2)}) async-start(s8[4718592]{0:T(1024)(128)(4,1)} %bitcast.32), calls=%async_computation.2 | async-start | bytes 1048576
  196.7 2.4 %copy-start.6 = (f32[16,512]{1,0:T(8,128)S(1)}, f32[16,512]{1,0:T(8,128)}, u32[]{:S(2)}) copy-start(f32[16,512]{1,0:T(8,128)} %param.17) | copy-start | bytes 98308
  196.7 6.1 %copy-start.2 = (f32[32,32,512]{2,1,0:T(8,128)S(1)}, f32[32,32,512]{2,1,0:T(8,128)}, u32[]{:S(2)}) copy-start(f32[32,32,512]{2,1,0:T(8,128)} %copy.15) | copy-start | bytes 6291460
  199.2 8.0 %copy-start.11 = (f32[512]{0:T(512)S(1)}, f32[512]{0:T(512)}, u32[]{:S(2)}) copy-start(f32[512]{0:T(512)} %param.19) | copy-start | bytes 6148
  199.2 6.1 %collective-permute-start.1 = (f32[16,512]{1,0:T(8,128)S(1)}, f32[16,512]{1,0:T(8,128)S(1)}, u32[]{:S(2)}, u32[]{:S(2)}) collective-permute-start(f32[16,512]{1,0:T(8,128)S(1)} %fusion.15), channel_id=1, source_target_pairs={{0,1},{2,3},{4,5},{6,7},{8,9},{10,11},{12,13},{14,15},{16,17},{18,... | collective-permute-start | bytes 98312 | tf_op jit(solution)/shard_map/ppermute | solution.py:14
Sparse Core Ops, SparseCore 0:
  9.4 170.7 all-gather.1

commit v15 on v13

--- a/solution.py
+++ b/solution.py
@@ -69,7 +69,7 @@
 def pack_weights(w_in, w_out):
     rows, cols = w_in.shape
     slab = w_out.shape[0]
-    step = 256 if rows % 256 == 0 else rows
+    step = rows
     return pl.pallas_call(
         pack_kernel,
         grid=(rows // step,),

time: 225 us -> 226 us (level)
  no operation moved by 1% of the time
where the time goes in v15:
time: 226 us; the launch traced here: 225 us
  waiting for transfers between devices  128 us (57%)
  other arithmetic  32.3 us (14%)
  between operations  16.8 us (7%)
  matrix products  15.7 us (7%)
  Pallas kernels  13 us (6%)
  local copies, waits for them, and re-layouts  11.6 us (5%)
  starting transfers between devices  7.86 us (3%)
    all_gather x1, waiting for transfers between devices, per_device(): gathered = lax.all_gather(piece, 'dp', axis=0, tiled=True)  128 us
    dot_general x1, matrix products, per_device(): extended = jnp.dot(rows_ext, w_in_all, preferred_element_type=jnp.float32)  15.7 us
    pallas_call x1, Pallas kernels, project_out(): pl.pallas_call(out_kernel, grid=(width // tile,), in_specs=[pl.BlockSpec(...  9.89 us
    ppermute x2, starting transfers between devices, from_behind(): lax.ppermute(value, axis, [(source, source + steps) for source in range(f...  7.85 us
    concatenate x1, other arithmetic, per_device(): rows_ext = jnp.concatenate([tail_normed, normed], axis=0)  7.24 us
  transfers between devices with their start and end apart: 3, of which 1 were waited for; matrix products, arithmetic and copies ran while one was open for 15% of the time, Pallas kernels for 0%

profile of v15, /device:TPU:0, one launch (start us, length us, event | category | flops | bytes accessed | tf_op | source)
XLA Modules:
  0.0 225.3 jit_solution(15337316590879476594)
XLA Ops:
  6.5 3.1 %shard_map.118 = bf16[512,2048]{1,0:T(8,128)(2,1)} custom-call(bf16[512,1536]{1,0:T(8,128)(2,1)} %wi_ref.1, bf16[512,512]{1,0:T(8,128)(2,1)} %wo_ref.1), custom_call_target="tpu_custom_call" | custom-call | tf_op jit(solution)/shard_map/pallas_call | solution.py:73
  11.5 4.3 %fusion.2 = f32[384]{0:T(512)S(1)} fusion(bf16[1,1,384,8192]{3,2,1,0:T(8,128)(2,1)} %param.12), kind=kLoop, calls=%fused_computation.6 | loop fusion | flops 9436800 | bytes 6292992 | tf_op jit(solution)/shard_map/reduce_sum | solution.py:19
  16.1 2.1 fusion.4
  18.2 3.5 %copy-done.1 = bf16[384,8192]{1,0:T(8,128)(2,1)} copy-done((bf16[384,8192]{1,0:T(8,128)(2,1)}, bf16[384,8192]{1,0:T(8,128)(2,1)S(1)}, u32[]{:S(2)}) %copy-start.1) | copy-done | bytes 6291480
  21.7 4.3 %collective-permute-start = (bf16[2,8192]{1,0:T(2,128)(2,1)S(1)}, bf16[2,8192]{1,0:T(2,128)(2,1)S(1)}, u32[]{:S(2)}, u32[]{:S(2)}) collective-permute-start(bf16[2,8192]{1,0:T(2,128)(2,1)S(1)} %constant_dynamic-slice_fusion.1), channel_id=1, source_target_pairs={{0,1},{2,3},{4,5},{6,7},{8,9},{10,11},{12,13},{14,15},{16,17},{18,... | collective-permute-start | bytes 98312 | tf_op jit(solution)/shard_map/ppermute | solution.py:14
  27.4 1.5 multiply_exponential_fusion
  28.9 3.5 %gather_fusion = f32[1024,512]{1,0:T(8,128)S(1)} fusion(f32[32,512]{1,0:T(8,128)S(1)} %get-tuple-element.15, s32[1024]{0:T(1024)S(1)} %broadcast_clamp_fusion), kind=kCustom, calls=%fused_computation | custom fusion | bytes 4198400 | tf_op jit(solution)/shard_map/gather | solution.py:28
  32.6 1.3 fusion.13.m_ref
  33.9 0.9 multiply_exponential_fusion.1
  35.0 1.5 broadcast_select_fusion
  36.5 2.6 %exponential_select_fusion = f32[12,12,16,512]{3,2,1,0:T(8,128)} fusion(f32[12,12]{1,0:T(8,128)S(1)} %maximum_multiply_fusion, f32[16,512]{1,0:T(8,128)S(1)} %neg.5, pred[12,12]{1,0:T(8,128)(4,1)S(1)} %convert_compare_fusion), kind=kLoop, calls=%fused_computation.13 | loop fusion | flops 2359296 | bytes 4752080 | tf_op jit(solution)/shard_map/jit(_where)/select_n | solution.py:38
  39.1 1.6 compare_select_fusion.s_ref
  41.8 2.8 %copy.15 = f32[32,32,512]{2,1,0:T(8,128)S(1)} copy(f32[32,32,512]{2,0,1:T(8,128)} %broadcast_select_fusion) | data formatting | bytes 4194304 | tf_op jit(solution)/shard_map/jit(_where)/select_n | solution.py:28
  45.4 7.2 %pad_maximum_fusion = bf16[386,8192]{1,0:T(8,128)(2,1)} fusion(bf16[384,8192]{1,0:T(8,128)(2,1)} %copy-done.1, bf16[2,8192]{1,0:T(2,128)(2,1)S(1)} %collective-permute-done), kind=kLoop, calls=%fused_computation.11 | loop fusion | flops 12648448 | bytes 12648448 | tf_op jit(solution)/shard_map/concatenate | solution.py:147
  52.6 128.0 %all-gather.2.cloned.1.call-done.w_ref = bf16[8192,2048]{1,0:T(8,128)(2,1)} async-done(((bf16[512,2048]{1,0:T(8,128)(2,1)}), bf16[8192,2048]{1,0:T(8,128)(2,1)}) %all-gather.2.cloned.1.call-update) | async-done | bytes 33554448 | tf_op jit(solution)/shard_map/all_gather | solution.py:145
  180.6 15.7 %fusion.5 = f32[386,1536]{1,0:T(8,128)S(1)} fusion(bf16[386,8192]{1,0:T(8,128)(2,1)} %pad_maximum_fusion, bf16[8192,2048]{1,0:T(8,128)(2,1)} %all-gather.2.cloned.1.call-done.w_ref), kind=kOutput, calls=%fused_computation.14 | convolution fusion | flops 9714600960 | bytes 33959936 | tf_op jit(solution)/shard_map/dot_general | solution.py:152
  196.4 0.7 fusion.8
  197.7 1.1 multiply_reduce_fusion.2
  199.0 0.6 multiply_reduce_fusion.3
  199.6 3.6 %collective-permute-start.1 = (f32[16,512]{1,0:T(8,128)S(1)}, f32[16,512]{1,0:T(8,128)S(1)}, u32[]{:S(2)}, u32[]{:S(2)}) collective-permute-start(f32[16,512]{1,0:T(8,128)S(1)} %fusion.15), channel_id=1, source_target_pairs={{0,1},{2,3},{4,5},{6,7},{8,9},{10,11},{12,13},{14,15},{16,17},{18,... | collective-permute-start | bytes 98312 | tf_op jit(solution)/shard_map/ppermute | solution.py:14
  203.2 2.4 %multiply_reduce_fusion = f32[12,32,512]{2,1,0:T(8,128)S(1)} fusion(f32[12,32,512]{2,1,0:T(8,128)S(1)} %bitcast.36, f32[32,32,512]{2,1,0:T(8,128)S(1)} %copy.15), kind=kLoop, calls=%fused_computation.3 | loop fusion | flops 12386304 | bytes 3670016 | tf_op jit(solution)/shard_map/reduce_sum | solution.py:56
  206.4 1.0 multiply_reduce_fusion.1
  207.5 1.0 fusion.12.g_ref
  208.6 9.9 %shard_map.119 = bf16[384,8192]{1,0:T(8,128)(2,1)} custom-call(bf16[384,512]{1,0:T(8,128)(2,1)} %fusion.12.g_ref, bf16[8192,2048]{1,0:T(8,128)(2,1)} %all-gather.2.cloned.1.call-done.w_ref, bf16[384,8192]{1,0:T(8,128)(2,1)} %bitcast.31, f32[1,8192]{1,0:T(1,128)} %compare_select_fusion.s_ref, s32[384,1]{1,0:T(8,128)} %fusion.13.m_ref), custom_call_target="tpu_custom_call" | custom-call | flops 3221225472 | bytes 21397504 | tf_op jit(solution)/shard_map/pallas_call | solution.py:94
  (54 shorter events, 4.4 us)
Async XLA Ops:
  6.5 3.2 %copy-start.9 = (s32[1,2]{1,0:T(1,128)S(1)}, s32[1,2]{1,0:T(1,128)}, u32[]{:S(2)}) copy-start(s32[1,2]{1,0:T(1,128)} %param.13) | copy-start | bytes 28
  6.5 174.1 %all-gather.2.cloned.1.call-start = ((), (), s32[]{:S(2)}) async-start(), calls=%async_computation | async-start | bytes 35651584 | tf_op jit(solution)/shard_map/all_gather | solution.py:145
  9.7 6.1 %copy-start.6 = (f32[8192]{0:T(1024)S(1)}, f32[8192]{0:T(1024)}, u32[]{:S(2)}) copy-start(f32[8192]{0:T(1024)} %param.14) | copy-start | bytes 98308
  11.5 4.6 %copy-start = (bf16[1,1,384,8192]{3,2,1,0:T(8,128)(2,1)S(1)}, bf16[1,1,384,8192]{3,2,1,0:T(8,128)(2,1)}, u32[]{:S(2)}) copy-start(bf16[1,1,384,8192]{3,2,1,0:T(8,128)(2,1)} %param.12) | copy-start | bytes 18874372
  16.1 9.9 %copy-start.4 = (f32[16,512]{1,0:T(8,128)S(1)}, f32[16,512]{1,0:T(8,128)}, u32[]{:S(2)}) copy-start(f32[16,512]{1,0:T(8,128)} %param.17) | copy-start | bytes 98308
  16.1 11.4 %copy-start.5 = (f32[16,512]{1,0:T(8,128)S(1)}, f32[16,512]{1,0:T(8,128)}, u32[]{:S(2)}) copy-start(f32[16,512]{1,0:T(8,128)} %param.18) | copy-start | bytes 98308
  18.2 3.5 %copy-start.1 = (bf16[384,8192]{1,0:T(8,128)(2,1)}, bf16[384,8192]{1,0:T(8,128)(2,1)S(1)}, u32[]{:S(2)}) copy-start(bf16[384,8192]{1,0:T(8,128)(2,1)S(1)} %fusion.4) | copy-start | bytes 18874372
  21.7 23.7 %collective-permute-start = (bf16[2,8192]{1,0:T(2,128)(2,1)S(1)}, bf16[2,8192]{1,0:T(2,128)(2,1)S(1)}, u32[]{:S(2)}, u32[]{:S(2)}) collective-permute-start(bf16[2,8192]{1,0:T(2,128)(2,1)S(1)} %constant_dynamic-slice_fusion.1), channel_id=1, source_target_pairs={{0,1},{2,3},{4,5},{6,7},{8,9},{10,11},{12,13},{14,15},{16,17},{18,... | collective-permute-start | bytes 98312 | tf_op jit(solution)/shard_map/ppermute | solution.py:14
  28.9 3.6 %copy-start.7 = (f32[3,1536]{1,0:T(4,128)S(1)}, f32[3,1536]{1,0:T(4,128)}, u32[]{:S(2)}) copy-start(f32[3,1536]{1,0:T(4,128)} %param.16) | copy-start | bytes 55300
  196.3 2.5 %slice-start = ((s8[4718592]{0:T(1024)(128)(4,1)}), s8[4194304]{0:T(1024)(128)(4,1)S(1)}, s32[]{:S(2)}) async-start(s8[4718592]{0:T(1024)(128)(4,1)} %bitcast.32), calls=%async_computation.1 | async-start | bytes 8388608
  196.3 1.4 copy-start.2
  196.4 2.6 %slice-start.1 = ((s8[4718592]{0:T(1024)(128)(4,1)}), s8[524288]{0:T(1024)(128)(4,1)S(1)}, s32[]{:S(2)}) async-start(s8[4718592]{0:T(1024)(128)(4,1)} %bitcast.32), calls=%async_computation.2 | async-start | bytes 1048576
  199.0 7.3 %copy-start.3 = (f32[12,16,512]{2,1,0:T(8,128)S(1)}, f32[12,16,512]{2,1,0:T(8,128)}, u32[]{:S(2)}) copy-start(f32[12,16,512]{2,1,0:T(8,128)} %multiply_exponential_fusion.1) | copy-start | bytes 1179652
  199.6 7.9 %copy-start.8 = (f32[512]{0:T(512)S(1)}, f32[512]{0:T(512)}, u32[]{:S(2)}) copy-start(f32[512]{0:T(512)} %param.19) | copy-start | bytes 6148
  199.6 6.1 %collective-permute-start.1 = (f32[16,512]{1,0:T(8,128)S(1)}, f32[16,512]{1,0:T(8,128)S(1)}, u32[]{:S(2)}, u32[]{:S(2)}) collective-permute-start(f32[16,512]{1,0:T(8,128)S(1)} %fusion.15), channel_id=1, source_target_pairs={{0,1},{2,3},{4,5},{6,7},{8,9},{10,11},{12,13},{14,15},{16,17},{18,... | collective-permute-start | bytes 98312 | tf_op jit(solution)/shard_map/ppermute | solution.py:14
Sparse Core Ops, SparseCore 0:
  9.8 170.7 all-gather.1
